TPU v7x, 512 devices: a whole 4x4x16 slice. The times are simulated.
512 devices in a mesh: cfg: 2 (over x_lo), seq: 32 (over z, core), wgt: 8 (over y, x_hi).
Axes of the slice: x: 4 (x_hi: 2, x_lo: 2; x = x_hi * 2 + x_lo), y: 4, z: 16, core: 2. Of those that a mesh axis runs over, the one named last changes fastest.
Arguments:
- latent: float32 [1024, 4, 64], P(('seq', 'wgt'), 'cfg'), may hold values from -6 to 6
- img_hidden: bfloat16 [2, 1024, 4, 2432], P('cfg', 'seq'), may hold values from -5 to 5
- txt_hidden: bfloat16 [2, 512, 2432], P('cfg', 'seq'), may hold values from -6 to 6
- segments: int32 [2, 512], P('cfg', 'seq'), may hold values from 0 to 3, never falling along the last dimension, each value on 1 to 154 neighbouring positions
- timesteps: int32 [4], replicated, may hold values from 0 to 27
- modulation: float32 [2, 4, 10, 2432], P('cfg'), may hold values from -3 to 3
- qk_gain: float32 [2, 64], replicated, may hold values from 1.5 to 8
- qkv_weight: bfloat16 [3, 2432, 1536], P(None, 'seq', 'wgt'), may hold values from -0.08111071 to 0.08111071, as said below
- text_weight: bfloat16 [2, 2432, 1536], P(None, 'seq', 'wgt'), may hold values from -0.125 to 0.125
- out_weight: bfloat16 [1536, 2432], P('wgt', 'seq'), may hold values from -0.15625 to 0.15625
- expand_weight: bfloat16 [2432, 5632], P('seq', 'wgt'), may hold values from -0.125 to 0.125
- contract_weight: bfloat16 [5632, 2432], P('wgt', 'seq'), may hold values from -0.078125 to 0.078125
- final_weight: bfloat16 [2432, 64], replicated, may hold values from -0.0625 to 0.0625
Outputs:
- velocity: float32 [1024, 4, 64], P(('seq', 'wgt'), 'cfg')
- next_latent: float32 [1024, 4, 64], P(('seq', 'wgt'), 'cfg')
Inputs may be any that keep to these rules, and one draw needn't show every extreme that they name: `segments`: along each row the segment never falls, and each request has 1 to 154 positions. `qkv_weight`: entries are of order 2432 ** -0.5.
All inputs are finite; a program needn't handle non-finite values.
Results may differ from a plain program's by a relative error of at most 0.012.
The roundings to bfloat16 on the way count: a program that leaves them out, or rounds other values in their place, can miss the bound.
Values may be sent and summed in bfloat16 or wider, within the bound.
No kernel may reach another device: no remote copies, remote signals or barrier semaphores. Data moves between devices by JAX's collectives and lax.ppermute only.
A program may use at most 128 MiB of HBM per device.

v0:
```python
import jax
import jax.numpy as jnp
from jax import lax
from jax.sharding import PartitionSpec as P

STEPS = 28


guidance_scale = 3.5
flow_shift = 3.0
eps_norm = 1e-06
masked_score = -1e30


def from_partner(value, axis, bit):
    mask = 2**bit
    pairs = [(source, source ^ mask) for source in range(lax.axis_size(axis))]
    return lax.ppermute(value, axis, pairs)


def layer_norm(values):
    center = jnp.mean(values, axis=-1, keepdims=True)
    centred = values - center
    spread = jnp.mean(centred * centred, axis=-1, keepdims=True)
    return centred * lax.rsqrt(spread + eps_norm)


def head_norm(values, gain_row):
    power = jnp.mean(values * values, axis=-1, keepdims=True)
    return values * lax.rsqrt(power + eps_norm) * gain_row


def sigma_of(index_row):
    time_left = 1.0 - index_row.astype(jnp.float32) / STEPS
    return flow_shift * time_left / (1.0 + (flow_shift - 1.0) * time_left)


def body(
    latent,
    img_hidden,
    txt_hidden,
    segments,
    timesteps,
    modulation,
    qk_gain,
    qkv_weight,
    text_weight,
    out_weight,
    expand_weight,
    contract_weight,
    final_weight,
):
    tokens_here = img_hidden.shape[1]
    requests = img_hidden.shape[2]
    feat_width = img_hidden.shape[3]
    head_size = qk_gain.shape[1]
    local_cols = qkv_weight.shape[2]
    heads_here = local_cols // head_size
    text_here = txt_hidden.shape[1]
    modulate = modulation[0]
    hidden = img_hidden[0].astype(jnp.float32)
    image_normed = (layer_norm(hidden) * (1.0 + modulate[:, 1]) + modulate[:, 0]).astype(
        jnp.bfloat16
    )
    row_count = tokens_here * requests
    token_rows = image_normed.reshape(row_count, feat_width)
    segment_row = segments[0]
    one_hot = (segment_row[:, None] == jnp.arange(requests, dtype=jnp.int32)[None, :]).astype(
        jnp.float32
    )
    text_mod = jnp.einsum("tr,rkd->tkd", one_hot, modulate[:, 3:5], precision=lax.Precision.HIGHEST)
    text_normed = (
        layer_norm(txt_hidden[0].astype(jnp.float32)) * (1.0 + text_mod[:, 1]) + text_mod[:, 0]
    ).astype(jnp.bfloat16)
    all_weights = jnp.concatenate([qkv_weight, text_weight], axis=0)
    out_full, contract_full = (
        lax.all_gather(out_weight, "seq", axis=1, tiled=True),
        lax.all_gather(contract_weight, "seq", axis=1, tiled=True),
    )
    piece = lax.all_gather(all_weights, "seq", axis=1, tiled=True)
    image_term = jnp.einsum(
        "rd,kdc->rkc", token_rows, piece[:3], preferred_element_type=jnp.float32
    )
    text_term = jnp.einsum(
        "rd,kdc->rkc", text_normed, piece[3:], preferred_element_type=jnp.float32
    )
    queries = head_norm(
        image_term[:, 0].reshape(tokens_here, requests, heads_here, head_size), qk_gain[0]
    ).astype(jnp.bfloat16)
    keys_img = head_norm(
        image_term[:, 1].reshape(tokens_here, requests, heads_here, head_size), qk_gain[1]
    ).astype(jnp.bfloat16)
    values_img = image_term[:, 2].reshape(tokens_here, requests, local_cols).astype(jnp.bfloat16)
    keys_txt = head_norm(
        text_term[:, 0].reshape(text_here, heads_here, head_size), qk_gain[1]
    ).astype(jnp.bfloat16)
    values_txt = text_term[:, 1].astype(jnp.bfloat16)
    image_pair = jnp.stack(
        [keys_img.reshape(tokens_here, requests, local_cols), values_img], axis=2
    )
    text_pair = jnp.stack([keys_txt.reshape(text_here, local_cols), values_txt], axis=1)
    text_owner = segment_row.astype(jnp.float32).astype(jnp.bfloat16)
    scale_factor = head_size ** (-0.5)
    request_ids = jnp.arange(requests, dtype=jnp.float32)
    running_max = jnp.full((requests, heads_here, tokens_here), masked_score, jnp.float32)
    image_piece = lax.all_gather(image_pair, "seq", axis=0, tiled=True)
    text_piece = lax.all_gather(text_pair, "seq", axis=0, tiled=True)
    owner_piece = lax.all_gather(text_owner, "seq", axis=0, tiled=True)
    piece_keys = image_piece[:, :, 0].reshape(-1, requests, heads_here, head_size)
    piece_values = image_piece[:, :, 1].reshape(-1, requests, heads_here, head_size)
    text_keys = text_piece[:, 0].reshape(-1, heads_here, head_size)
    text_values = text_piece[:, 1].reshape(-1, heads_here, head_size)
    image_scores = (
        jnp.einsum("qrhd,krhd->rhqk", queries, piece_keys, preferred_element_type=jnp.float32)
        * scale_factor
    )
    text_scores = (
        jnp.einsum("qrhd,khd->rhqk", queries, text_keys, preferred_element_type=jnp.float32)
        * scale_factor
    )
    allowed = owner_piece.astype(jnp.float32)[None, :] == request_ids[:, None]
    text_scores = jnp.where(allowed[:, None, None, :], text_scores, masked_score)
    block_max = jnp.maximum(jnp.max(image_scores, axis=-1), jnp.max(text_scores, axis=-1))
    new_max = jnp.maximum(running_max, block_max)
    image_weights = jnp.exp(image_scores - new_max[..., None])
    text_weights = jnp.exp(text_scores - new_max[..., None])
    new_sum = jnp.sum(image_weights, axis=-1) + jnp.sum(text_weights, axis=-1)
    new_acc = jnp.einsum(
        "rhqk,krhd->rhqd",
        image_weights.astype(jnp.bfloat16),
        piece_values,
        preferred_element_type=jnp.float32,
    )
    new_acc = new_acc + jnp.einsum(
        "rhqk,khd->rhqd",
        text_weights.astype(jnp.bfloat16),
        text_values,
        preferred_element_type=jnp.float32,
    )
    attended = new_acc / new_sum[..., None]
    attended = (
        jnp.transpose(attended, (2, 0, 1, 3)).reshape(row_count, local_cols).astype(jnp.bfloat16)
    )
    share_rows = row_count // lax.axis_size("wgt")
    piece_rows = attended
    mixed = lax.psum_scatter(
        jnp.dot(piece_rows, out_full, preferred_element_type=jnp.float32).astype(jnp.bfloat16),
        "wgt",
        scatter_dimension=0,
        tiled=True,
    ).astype(jnp.float32)
    tokens_out = share_rows // requests
    row_place = lax.axis_index("wgt") * share_rows
    base_rows = lax.dynamic_slice_in_dim(
        hidden.reshape(row_count, feat_width), row_place, share_rows, 0
    )
    residual = base_rows.reshape(tokens_out, requests, feat_width) + modulate[:, 2] * mixed.reshape(
        tokens_out, requests, feat_width
    )
    branch_in = (layer_norm(residual) * (1.0 + modulate[:, 6]) + modulate[:, 5]).astype(
        jnp.bfloat16
    )
    branch_rows = lax.all_gather(
        branch_in.reshape(share_rows, feat_width), "wgt", axis=0, tiled=True
    )
    expanded = jnp.dot(
        branch_rows,
        lax.all_gather(expand_weight, "seq", axis=0, tiled=True),
        preferred_element_type=jnp.float32,
    )
    expanded = jax.nn.gelu(expanded, approximate=True).astype(jnp.bfloat16)
    piece_rows = expanded
    branch = lax.psum_scatter(
        jnp.dot(piece_rows, contract_full, preferred_element_type=jnp.float32).astype(jnp.bfloat16),
        "wgt",
        scatter_dimension=0,
        tiled=True,
    ).astype(jnp.float32)
    second = residual + modulate[:, 7] * branch.reshape(tokens_out, requests, feat_width)
    final_in = (layer_norm(second) * (1.0 + modulate[:, 9]) + modulate[:, 8]).astype(jnp.bfloat16)
    own_velocity = jnp.dot(
        final_in.reshape(share_rows, feat_width), final_weight, preferred_element_type=jnp.float32
    ).reshape(tokens_out, requests, -1)
    guide_side = lax.axis_index("cfg")
    guided_count = latent.shape[1]
    kept_rows = lax.dynamic_slice_in_dim(own_velocity, guide_side * guided_count, guided_count, 1)
    sent_rows = lax.dynamic_slice_in_dim(
        own_velocity, (1 - guide_side) * guided_count, guided_count, 1
    )
    partner_velocity = from_partner(sent_rows, "cfg", 0)
    is_first = guide_side == 0
    conditional = jnp.where(is_first, kept_rows, partner_velocity)
    unconditional = jnp.where(is_first, partner_velocity, kept_rows)
    velocity = unconditional + guidance_scale * (conditional - unconditional)
    step_size = sigma_of(timesteps + 1) - sigma_of(timesteps)
    step_here = lax.dynamic_slice_in_dim(step_size, guide_side * guided_count, guided_count, 0)
    next_latent = latent + step_here[None, :, None] * velocity
    return (velocity, next_latent)


def solution(mesh):
    return jax.shard_map(
        body,
        mesh=mesh,
        in_specs=(
            P(("seq", "wgt"), "cfg", None),
            P("cfg", "seq", None, None),
            P("cfg", "seq", None),
            P("cfg", "seq"),
            P(),
            P("cfg", None, None, None),
            P(),
            P(None, "seq", "wgt"),
            P(None, "seq", "wgt"),
            P("wgt", "seq"),
            P("seq", "wgt"),
            P("wgt", "seq"),
            P(),
        ),
        out_specs=(P(("seq", "wgt"), "cfg", None), P(("seq", "wgt"), "cfg", None)),
        check_vma=False,
    )
```

profile of v0, /device:TPU:32, one launch (start us, length us, event | category | flops | bytes accessed | tf_op | source)
XLA Modules:
  0.0 552.4 jit_solution(9732671429837447822)
XLA Ops:
  7.2 1.0 copy.132
  8.2 1.8 pad_maximum_fusion
  10.1 1.6 fusion.55
  11.9 1.5 add.219
  13.5 1.5 mul.301
  15.0 1.1 reshape.249
  17.9 76.2 %all-gather.8.cloned.1.call-done = bf16[5,2432,192]{2,0,1:T(8,128)(2,1)} async-done(((bf16[5,76,192]{2,0,1:T(8,128)(2,1)}), bf16[5,2432,192]{2,0,1:T(8,128)(2,1)}) %all-gather.8.cloned.1.call-update) | async-done | bytes 4669456 | tf_op jit(solution)/shard_map/all_gather | solution.py:80
  94.1 8.2 %slice.102 = bf16[3,2432,192]{2,0,1:T(4,128)(2,1)} slice(bf16[5,2432,192]{2,0,1:T(8,128)(2,1)} %all-gather.8.cloned.1.call-done), slice={[0:3], [0:2432], [0:192]} | slice | bytes 5603328 | tf_op jit(solution)/shard_map/slice | solution.py:82
  102.3 7.0 %copy.161 = bf16[3,2432,192]{1,2,0:T(8,128)(2,1)S(1)} copy(bf16[3,2432,192]{2,0,1:T(4,128)(2,1)} %slice.102) | data formatting | bytes 5603328
  109.3 3.0 fusion.15
  116.0 1.3 dynamic-slice
  118.2 46.0 %all-reduce = bf16[512]{0:T(512)(128)(2,1)S(1)} all-reduce(bf16[512]{0:T(512)(128)(2,1)S(1)} %dynamic-update-slice), channel_id=1, replica_groups=mesh['cfg'=2,'seq'=32,'wgt'=8] {'seq'}, use_global_device_ids=true, to_apply=%add | all-reduce | flops 512 | bytes 2048
  164.2 33.9 %all-gather = bf16[32,76,192]{2,1,0:T(8,128)(2,1)S(1)} all-gather(bf16[1,76,192]{2,1,0:T(8,128)(2,1)S(1)} %bitcast.150), channel_id=1, replica_groups=mesh['cfg'=2,'seq'=32,'wgt'=8] {'seq'}, dimensions={0}, use_global_device_ids=true | all-gather | bytes 963072 | tf_op jit(solution)/shard_map/all_gather | solution.py:77
  198.2 1.3 reshape.268
  199.8 1.3 fusion.49
  201.7 6.4 %slice.110 = bf16[2,2432,192]{2,0,1:T(2,128)(2,1)S(1)} slice(bf16[5,2432,192]{2,0,1:T(8,128)(2,1)} %all-gather.8.cloned.1.call-done), slice={[3:5], [0:2432], [0:192]} | slice | bytes 3735552 | tf_op jit(solution)/shard_map/slice | solution.py:85
  209.1 29.8 %all_gather.27 = bf16[512,2,192]{2,0,1:T(8,128)(2,1)S(1)} all-gather(bf16[16,2,192]{2,0,1:T(8,128)(2,1)S(1)} %pad_maximum_fusion.2), channel_id=1, replica_groups=mesh['cfg'=2,'seq'=32,'wgt'=8] {'seq'}, dimensions={0}, use_global_device_ids=true | all-gather | bytes 405504 | tf_op jit(solution)/shard_map/all_gather | solution.py:107
  240.3 4.1 fusion.69
  244.3 4.3 copy.153
  248.6 2.5 copy.147
  251.2 2.0 fusion.73
  256.5 1.4 convolution_convert_fusion.1
  258.5 6.3 %reshape.258 = bf16[2432,704]{1,0:T(8,128)(2,1)} reshape(bf16[32,76,704]{2,1,0:T(8,128)(2,1)} %all-gather.14.cloned.1.call-done) | data formatting | bytes 6848512
  264.8 65.5 %all-gather.12.cloned.1.call-done = bf16[32,76,704]{2,1,0:T(8,128)(2,1)} async-done(((bf16[1,76,704]{2,1,0:T(8,128)(2,1)}), bf16[32,76,704]{2,1,0:T(8,128)(2,1)}) %all-gather.12.cloned.1.call-update) | async-done | bytes 3424272 | tf_op jit(solution)/shard_map/all_gather | solution.py:168
  330.3 6.3 %reshape.256 = bf16[2432,704]{1,0:T(8,128)(2,1)} reshape(bf16[32,76,704]{2,1,0:T(8,128)(2,1)} %all-gather.12.cloned.1.call-done) | data formatting | bytes 6848512
  336.6 75.6 %reduce-scatter.3.cloned.1.call-done = bf16[16,2432]{1,0:T(8,128)(2,1)} async-done(((bf16[128,2432]{1,0:T(8,128)(2,1)}), bf16[16,2432]{1,0:T(8,128)(2,1)}) %reduce-scatter.3.cloned.1.call-update) | async-done | bytes 77840 | tf_op jit(solution)/shard_map/reduce_scatter | solution.py:146
  412.2 1.1 fusion.68
  413.6 36.4 %all_gather.29 = bf16[128,2432]{1,0:T(8,128)(2,1)S(1)} all-gather(bf16[16,2432]{1,0:T(8,128)(2,1)S(1)} %add_convert_fusion.3), channel_id=1, replica_groups=mesh['cfg'=2,'seq'=32,'wgt'=8] {'wgt'}, dimensions={0}, use_global_device_ids=true | all-gather | bytes 700416 | tf_op jit(solution)/shard_map/all_gather | solution.py:163
  450.0 7.7 %convolution_convert_fusion = bf16[128,2432]{1,0:T(8,128)(2,1)} fusion(bf16[2432,704]{1,0:T(8,128)(2,1)} %reshape.258, bf16[128,2432]{1,0:T(8,128)(2,1)S(1)} %all_gather.29, bf16[2432,704]{1,0:T(8,128)(2,1)} %reshape.256), kind=kOutput, calls=%fused_computation | convolution fusion | flops 877731840 | bytes 8093696 | tf_op jit(solution)/shard_map/dot_general | solution.py:174
  458.0 79.8 %reduce-scatter.5.cloned.1.call-done = bf16[16,2432]{1,0:T(8,128)(2,1)} async-done(((bf16[128,2432]{1,0:T(8,128)(2,1)}), bf16[16,2432]{1,0:T(8,128)(2,1)}) %reduce-scatter.5.cloned.1.call-update) | async-done | bytes 77840 | tf_op jit(solution)/shard_map/reduce_scatter | solution.py:173
  539.4 2.7 collective-permute-start
  542.3 2.7 collective-permute-done
  (139 shorter events, 16.0 us)
Async XLA Ops:
  7.2 532.0 %copy-start = (bf16[2432,64]{0,1:T(8,128)(2,1)S(1)}, bf16[2432,64]{0,1:T(8,128)(2,1)}, u32[]{:S(2)}) copy-start(bf16[2432,64]{0,1:T(8,128)(2,1)} %param.25) | copy-start | bytes 933892
  7.2 86.9 %all-gather.8.cloned.1.call-start = ((), (), s32[]{:S(2)}) async-start(), calls=%async_computation.2 | async-start | bytes 10272768 | tf_op jit(solution)/shard_map/all_gather | solution.py:80
  10.1 230.2 %all-gather.10.cloned.1.call-start = ((), (), s32[]{:S(2)}) async-start(), calls=%async_computation.3 | async-start | bytes 4325376 | tf_op jit(solution)/shard_map/all_gather | solution.py:106
  13.4 1.6 copy-start.2
  15.0 2.3 copy-start.13
  112.6 5.3 copy-start.14
  112.6 51.6 %copy-start.10 = (bf16[192,76]{0,1:T(8,128)(2,1)S(1)}, bf16[192,76]{0,1:T(8,128)(2,1)}, u32[]{:S(2)}) copy-start(bf16[192,76]{0,1:T(8,128)(2,1)} %param.22) | copy-start | bytes 87556
  114.6 143.9 %all-gather.14.cloned.1.call-start = ((), (), s32[]{:S(2)}) async-start(), calls=%async_computation.7 | async-start | bytes 4055040 | tf_op jit(solution)/shard_map/all_gather | solution.py:78
  115.4 214.9 %all-gather.12.cloned.1.call-start = ((), (), s32[]{:S(2)}) async-start(), calls=%async_computation.6 | async-start | bytes 4055040 | tf_op jit(solution)/shard_map/all_gather | solution.py:168
  116.0 296.2 %reduce-scatter.3.cloned.1.call-start = ((), (), s32[]{:S(2)}) async-start(), calls=%async_computation.4 | async-start | bytes 700416 | tf_op jit(solution)/shard_map/reduce_scatter | solution.py:146
  198.2 1.3 copy-start.4
  208.7 31.2 %copy-start.11 = (f32[64]{0:T(128)S(1)}, f32[64]{0:T(128)}, u32[]{:S(2)}) copy-start(f32[64]{0:T(128)} %get-tuple-element.25) | copy-start | bytes 772
  253.1 1.4 copy-start.1
  254.6 0.9 copy-start.5
  255.2 1.3 copy-start.3
  255.8 2.2 copy-start.9
  256.5 1.6 copy-start.8
  256.5 1.7 copy-start.7
  257.9 279.9 %reduce-scatter.5.cloned.1.call-start = ((), (), s32[]{:S(2)}) async-start(), calls=%async_computation.5 | async-start | bytes 700416 | tf_op jit(solution)/shard_map/reduce_scatter | solution.py:173
  450.0 7.7 %copy-start.6 = (f32[4,2432]{1,0:T(4,128)S(1)}, f32[4,2432]{1,0:T(4,128)}, u32[]{:S(2)}) copy-start(f32[4,2432]{1,0:T(4,128)} %get-tuple-element.15) | copy-start | bytes 116740
  457.7 84.4 %copy-start.15 = (s32[4]{0:T(128)S(1)}, s32[4]{0:T(128)}, u32[]{:S(2)}) copy-start(s32[4]{0:T(128)} %param.17) | copy-start | bytes 52
  457.8 87.2 %copy-start.12 = (f32[4,2,64]{2,1,0:T(2,128)S(1)}, f32[4,2,64]{2,1,0:T(2,128)}, u32[]{:S(2)}) copy-start(f32[4,2,64]{2,1,0:T(2,128)} %param.13) | copy-start | bytes 6148
  539.4 5.5 collective-permute-start
Sparse Core Ops, SparseCore 0:
  10.2 83.8 all-gather.7
  114.8 70.4 all-gather.9
  187.4 71.1 all-gather.13
  260.5 69.7 all-gather.11
  334.5 77.6 reduce-scatter.2
  457.8 79.9 reduce-scatter.4
where the time goes:
time: 554 us; the launch traced here: 552 us
  waiting for transfers between devices  301 us (54%)
  blocking collectives  146 us (26%)
  local copies, waits for them, and re-layouts  60 us (11%)
  matrix products  17.3 us (3%)
  between operations  15.3 us (3%)
  other arithmetic  9.52 us (2%)
    reduce_scatter x1, waiting for transfers between devices, body(): lax.psum_scatter(jnp.dot(piece_rows, contract_full, preferred_element_typ...  79.8 us
    all_gather x1, waiting for transfers between devices, body(): piece = lax.all_gather(all_weights, 'seq', axis=1, tiled=True)  76.2 us
    reduce_scatter x1, waiting for transfers between devices, body(): lax.psum_scatter(jnp.dot(piece_rows, out_full, preferred_element_type=jnp...  75.6 us
    all_gather x1, waiting for transfers between devices, body(): lax.all_gather(expand_weight, 'seq', axis=0, tiled=True)  65.5 us
    unnamed x1, blocking collectives  46 us
    all_gather x1, blocking collectives, body(): lax.all_gather(branch_in.reshape(share_rows, feat_width), 'wgt', axis=0,...  36.4 us
    all_gather x1, blocking collectives, body(): lax.all_gather(out_weight, 'seq', axis=1, tiled=True)  33.9 us
    all_gather x1, blocking collectives, body(): text_piece = lax.all_gather(text_pair, 'seq', axis=0, tiled=True)  29.8 us
  transfers between devices with their start and end apart: 7, of which 6 were waited for; matrix products, arithmetic and copies ran while one was open for 9% of the time, Pallas kernels for 0%

commit v1 on v0

--- a/solution.py
+++ b/solution.py
@@ -33,6 +33,12 @@
 def sigma_of(index_row):
     time_left = 1.0 - index_row.astype(jnp.float32) / STEPS
     return flow_shift * time_left / (1.0 + (flow_shift - 1.0) * time_left)
+
+
+def group_sum(partial, groups):
+    swapped = lax.all_to_all(partial, "wgt", 0, 0, tiled=True)
+    rows = swapped.shape[0] // groups
+    return jnp.sum(swapped.reshape(groups, rows, -1).astype(jnp.float32), axis=0)
 
 
 def body(
@@ -57,6 +63,8 @@
     local_cols = qkv_weight.shape[2]
     heads_here = local_cols // head_size
     text_here = txt_hidden.shape[1]
+    seq_size = lax.axis_size("seq")
+    wgt_size = lax.axis_size("wgt")
     modulate = modulation[0]
     hidden = img_hidden[0].astype(jnp.float32)
     image_normed = (layer_norm(hidden) * (1.0 + modulate[:, 1]) + modulate[:, 0]).astype(
@@ -73,17 +81,16 @@
         layer_norm(txt_hidden[0].astype(jnp.float32)) * (1.0 + text_mod[:, 1]) + text_mod[:, 0]
     ).astype(jnp.bfloat16)
     all_weights = jnp.concatenate([qkv_weight, text_weight], axis=0)
-    out_full, contract_full = (
-        lax.all_gather(out_weight, "seq", axis=1, tiled=True),
-        lax.all_gather(contract_weight, "seq", axis=1, tiled=True),
-    )
     piece = lax.all_gather(all_weights, "seq", axis=1, tiled=True)
-    image_term = jnp.einsum(
-        "rd,kdc->rkc", token_rows, piece[:3], preferred_element_type=jnp.float32
-    )
-    text_term = jnp.einsum(
-        "rd,kdc->rkc", text_normed, piece[3:], preferred_element_type=jnp.float32
-    )
+    mlp_local = jnp.stack([expand_weight, contract_weight.T], axis=0)
+    mlp_full = lax.all_gather(mlp_local, "seq", axis=1, tiled=True)
+    out_full = lax.all_gather(out_weight, "seq", axis=1, tiled=True)
+    both_rows = jnp.concatenate([token_rows, text_normed], axis=0)
+    both_term = jnp.einsum(
+        "rd,kdc->rkc", both_rows, piece, preferred_element_type=jnp.float32
+    )
+    image_term = both_term[:row_count]
+    text_term = both_term[row_count:]
     queries = head_norm(
         image_term[:, 0].reshape(tokens_here, requests, heads_here, head_size), qk_gain[0]
     ).astype(jnp.bfloat16)
@@ -92,20 +99,30 @@
     ).astype(jnp.bfloat16)
     values_img = image_term[:, 2].reshape(tokens_here, requests, local_cols).astype(jnp.bfloat16)
     keys_txt = head_norm(
-        text_term[:, 0].reshape(text_here, heads_here, head_size), qk_gain[1]
-    ).astype(jnp.bfloat16)
-    values_txt = text_term[:, 1].astype(jnp.bfloat16)
+        text_term[:, 3].reshape(text_here, heads_here, head_size), qk_gain[1]
+    ).astype(jnp.bfloat16)
+    values_txt = text_term[:, 4].astype(jnp.bfloat16)
     image_pair = jnp.stack(
         [keys_img.reshape(tokens_here, requests, local_cols), values_img], axis=2
-    )
-    text_pair = jnp.stack([keys_txt.reshape(text_here, local_cols), values_txt], axis=1)
-    text_owner = segment_row.astype(jnp.float32).astype(jnp.bfloat16)
+    ).reshape(tokens_here * requests * 2, local_cols)
+    text_pair = jnp.stack([keys_txt.reshape(text_here, local_cols), values_txt], axis=1).reshape(
+        text_here * 2, local_cols
+    )
+    owner_row = jnp.pad(
+        segment_row.astype(jnp.float32).astype(jnp.bfloat16), (0, local_cols - text_here)
+    )[None, :]
+    image_len = tokens_here * requests * 2
+    shared = jnp.concatenate([image_pair, text_pair, owner_row], axis=0)
+    shared_piece = lax.all_gather(shared, "seq", axis=0, tiled=False)
+    image_piece = shared_piece[:, :image_len].reshape(
+        seq_size * tokens_here, requests, 2, local_cols
+    )
+    text_piece = shared_piece[:, image_len : image_len + 2 * text_here].reshape(
+        seq_size * text_here, 2, local_cols
+    )
+    owner_piece = shared_piece[:, image_len + 2 * text_here, :text_here].reshape(-1)
     scale_factor = head_size ** (-0.5)
     request_ids = jnp.arange(requests, dtype=jnp.float32)
-    running_max = jnp.full((requests, heads_here, tokens_here), masked_score, jnp.float32)
-    image_piece = lax.all_gather(image_pair, "seq", axis=0, tiled=True)
-    text_piece = lax.all_gather(text_pair, "seq", axis=0, tiled=True)
-    owner_piece = lax.all_gather(text_owner, "seq", axis=0, tiled=True)
     piece_keys = image_piece[:, :, 0].reshape(-1, requests, heads_here, head_size)
     piece_values = image_piece[:, :, 1].reshape(-1, requests, heads_here, head_size)
     text_keys = text_piece[:, 0].reshape(-1, heads_here, head_size)
@@ -120,35 +137,31 @@
     )
     allowed = owner_piece.astype(jnp.float32)[None, :] == request_ids[:, None]
     text_scores = jnp.where(allowed[:, None, None, :], text_scores, masked_score)
-    block_max = jnp.maximum(jnp.max(image_scores, axis=-1), jnp.max(text_scores, axis=-1))
-    new_max = jnp.maximum(running_max, block_max)
-    image_weights = jnp.exp(image_scores - new_max[..., None])
-    text_weights = jnp.exp(text_scores - new_max[..., None])
-    new_sum = jnp.sum(image_weights, axis=-1) + jnp.sum(text_weights, axis=-1)
-    new_acc = jnp.einsum(
+    row_max = jnp.maximum(jnp.max(image_scores, axis=-1), jnp.max(text_scores, axis=-1))
+    image_weights = jnp.exp(image_scores - row_max[..., None])
+    text_weights = jnp.exp(text_scores - row_max[..., None])
+    row_sum = jnp.sum(image_weights, axis=-1) + jnp.sum(text_weights, axis=-1)
+    acc = jnp.einsum(
         "rhqk,krhd->rhqd",
         image_weights.astype(jnp.bfloat16),
         piece_values,
         preferred_element_type=jnp.float32,
     )
-    new_acc = new_acc + jnp.einsum(
+    acc = acc + jnp.einsum(
         "rhqk,khd->rhqd",
         text_weights.astype(jnp.bfloat16),
         text_values,
         preferred_element_type=jnp.float32,
     )
-    attended = new_acc / new_sum[..., None]
+    attended = acc / row_sum[..., None]
     attended = (
         jnp.transpose(attended, (2, 0, 1, 3)).reshape(row_count, local_cols).astype(jnp.bfloat16)
     )
-    share_rows = row_count // lax.axis_size("wgt")
-    piece_rows = attended
-    mixed = lax.psum_scatter(
-        jnp.dot(piece_rows, out_full, preferred_element_type=jnp.float32).astype(jnp.bfloat16),
-        "wgt",
-        scatter_dimension=0,
-        tiled=True,
-    ).astype(jnp.float32)
+    share_rows = row_count // wgt_size
+    mixed = group_sum(
+        jnp.dot(attended, out_full, preferred_element_type=jnp.float32).astype(jnp.bfloat16),
+        wgt_size,
+    )
     tokens_out = share_rows // requests
     row_place = lax.axis_index("wgt") * share_rows
     base_rows = lax.dynamic_slice_in_dim(
@@ -163,19 +176,14 @@
     branch_rows = lax.all_gather(
         branch_in.reshape(share_rows, feat_width), "wgt", axis=0, tiled=True
     )
-    expanded = jnp.dot(
-        branch_rows,
-        lax.all_gather(expand_weight, "seq", axis=0, tiled=True),
-        preferred_element_type=jnp.float32,
-    )
+    expanded = jnp.dot(branch_rows, mlp_full[0], preferred_element_type=jnp.float32)
     expanded = jax.nn.gelu(expanded, approximate=True).astype(jnp.bfloat16)
-    piece_rows = expanded
-    branch = lax.psum_scatter(
-        jnp.dot(piece_rows, contract_full, preferred_element_type=jnp.float32).astype(jnp.bfloat16),
-        "wgt",
-        scatter_dimension=0,
-        tiled=True,
-    ).astype(jnp.float32)
+    branch = group_sum(
+        jnp.einsum(
+            "rf,df->rd", expanded, mlp_full[1], preferred_element_type=jnp.float32
+        ).astype(jnp.bfloat16),
+        wgt_size,
+    )
     second = residual + modulate[:, 7] * branch.reshape(tokens_out, requests, feat_width)
     final_in = (layer_norm(second) * (1.0 + modulate[:, 9]) + modulate[:, 8]).astype(jnp.bfloat16)
     own_velocity = jnp.dot(

time: 554 us -> 377 us (0.68)
  waiting for transfers between devices: 301 us -> 125 us
  blocking collectives: 146 us -> 69.7 us
  local copies, waits for them, and re-layouts: 60 us -> 115 us
  starting transfers between devices: 2.96 us -> 16.6 us
    reduce_scatter x2 -> x0, waiting for transfers between devices: 155 us -> none  [the longest x1 79.8 us: body(): lax.psum_scatter(jnp.dot(piece_rows, contract_full, preferred_element_typ...]
    unnamed x1 -> x0, blocking collectives: 46 us -> none
    all_gather x2 -> x1, blocking collectives: 63.7 us -> 33.8 us  [body(): out_full = lax.all_gather(out_weight, 'seq', axis=1, tiled=True)]
    all_gather x3 -> x2, waiting for transfers between devices: 65.8 us -> 41.4 us  [the longest x1 31.7 us: body(): shared_piece = lax.all_gather(shared, 'seq', axis=0, tiled=False)]
    all_to_all x0 -> x2, starting transfers between devices: none -> 14 us  [group_sum(): swapped = lax.all_to_all(partial, 'wgt', 0, 0, tiled=True)]
    slice x2, local copies, waits for them, and re-layouts: 6.57 us -> 20.6 us  [body(): image_piece[:, :, 0].reshape(-1, requests, heads_here, head_size)]
    unnamed x40 -> x53, local copies, waits for them, and re-layouts: 25 us -> 37.1 us
    slice x5 -> x8, local copies, waits for them, and re-layouts: 14.9 us -> 25.4 us  [the longest x1 16 us: body(): mlp_full[0]]
  transfers between devices with their start and end apart: 7 -> 6, of which waited for: 6 -> 5; matrix products, arithmetic and copies ran while one was open for 9% -> 33% of each run, Pallas kernels for 0% -> 0%
where the time goes in v1:
time: 377 us; the launch traced here: 375 us
  waiting for transfers between devices  125 us (33%)
  local copies, waits for them, and re-layouts  115 us (31%)
  blocking collectives  69.7 us (18%)
  matrix products  19.5 us (5%)
  starting transfers between devices  16.6 us (4%)
  other arithmetic  14.5 us (4%)
  between operations  14.4 us (4%)
    all_gather x1, waiting for transfers between devices, body(): piece = lax.all_gather(all_weights, 'seq', axis=1, tiled=True)  70.1 us
    unnamed x53, local copies, waits for them, and re-layouts  37.1 us
    all_gather x1, blocking collectives, body(): lax.all_gather(branch_in.reshape(share_rows, feat_width), 'wgt', axis=0,...  35.8 us
    all_gather x1, blocking collectives, body(): out_full = lax.all_gather(out_weight, 'seq', axis=1, tiled=True)  33.8 us
    all_gather x1, waiting for transfers between devices, body(): shared_piece = lax.all_gather(shared, 'seq', axis=0, tiled=False)  31.7 us
    slice x2, local copies, waits for them, and re-layouts, body(): image_piece[:, :, 0].reshape(-1, requests, heads_here, head_size)  20.6 us
    slice x1, local copies, waits for them, and re-layouts, body(): mlp_full[0]  16 us
    all_to_all x2, starting transfers between devices, group_sum(): swapped = lax.all_to_all(partial, 'wgt', 0, 0, tiled=True)  14 us
  transfers between devices with their start and end apart: 6, of which 5 were waited for; matrix products, arithmetic and copies ran while one was open for 33% of the time, Pallas kernels for 0%

profile of v1, /device:TPU:32, one launch (start us, length us, event | category | flops | bytes accessed | tf_op | source)
XLA Modules:
  0.0 374.7 jit_solution(12533228190600719340)
XLA Ops:
  8.2 1.8 pad_maximum_fusion
  11.3 1.6 fusion.57
  13.7 1.5 mul.301
  22.3 1.6 add_convert_fusion
  23.9 70.1 %all-gather.7.cloned.1.call-done = bf16[5,2432,192]{2,0,1:T(8,128)(2,1)} async-done(((bf16[5,76,192]{2,0,1:T(8,128)(2,1)}), bf16[5,2432,192]{2,0,1:T(8,128)(2,1)}) %all-gather.7.cloned.1.call-update) | async-done | bytes 4669456 | tf_op jit(solution)/shard_map/all_gather | solution.py:84
  94.1 6.1 %fusion.74 = (bf16[144,5,192]{2,0,1:T(8,128)(2,1)S(1)}, f32[144,5,192]{2,0,1:T(8,128)S(1)}) fusion(bf16[5,2432,192]{2,0,1:T(8,128)(2,1)} %all-gather.7.cloned.1.call-done, bf16[16,2432]{1,0:T(8,128)(2,1)S(1)} %copy-done.11, bf16[128,2432]{1,0:T(8,128)(2,1)S(1)} %add_convert_fusion), kind=kOutput, calls=%fused_computation.133 | convolution fusion | flops 673938432 | bytes 6199296 | tf_op jit(solution)/shard_map/rd,kdc->rkc/dot_general | solution.py:89
  105.0 33.8 %all-gather.2 = bf16[32,76,192]{2,1,0:T(8,128)(2,1)S(1)} all-gather(bf16[1,76,192]{2,1,0:T(8,128)(2,1)S(1)} %bitcast.148), channel_id=1, replica_groups=mesh['cfg'=2,'seq'=32,'wgt'=8] {'seq'}, dimensions={0}, use_global_device_ids=true | all-gather | bytes 963072 | tf_op jit(solution)/shard_map/all_gather | solution.py:87
  142.5 31.7 %all-gather.11.cloned.1.call-done = bf16[32,289,192]{1,2,0:T(8,128)(2,1)} async-done(((bf16[1,289,192]{1,2,0:T(8,128)(2,1)}), bf16[32,289,192]{1,2,0:T(8,128)(2,1)}) %all-gather.11.cloned.1.call-update) | async-done | bytes 3551248 | tf_op jit(solution)/shard_map/all_gather | solution.py:116
  174.2 1.9 slice-done
  176.1 4.6 %copy.143 = bf16[32,256,192]{2,1,0:T(8,128)(2,1)} copy(bf16[32,256,192]{1,2,0:T(8,128)(2,1)S(1)} %slice-done) | data formatting | bytes 6291456 | tf_op jit(solution)/shard_map/slice | solution.py:117
  180.7 7.5 %reshape.277 = bf16[1024,4,2,192]{3,2,1,0:T(2,128)(2,1)} reshape(bf16[32,256,192]{2,1,0:T(8,128)(2,1)} %copy.143) | data formatting | bytes 6291456 | tf_op jit(solution)/shard_map/reshape | solution.py:117
  188.1 10.1 %fusion.71 = (bf16[1024,4,1,192]{3,2,1,0:T(2,128)(2,1)}, bf16[1024,4,1,192]{3,2,1,0:T(2,128)(2,1)}) fusion(bf16[1024,4,2,192]{3,2,1,0:T(2,128)(2,1)} %reshape.277), kind=kLoop, calls=%fused_computation.130 | loop fusion | bytes 6291456 | tf_op jit(solution)/shard_map/slice | solution.py:126
  198.2 8.9 %copy.150 = bf16[1024,4,1,192]{0,3,1,2:T(8,128)(2,1)S(1)} copy(bf16[1024,4,1,192]{3,2,1,0:T(2,128)(2,1)} %get-tuple-element.11) | data formatting | bytes 3145728 | tf_op jit(solution)/shard_map/slice | solution.py:127
  207.2 10.5 %copy.144 = bf16[1024,4,1,192]{0,3,1,2:T(8,128)(2,1)} copy(bf16[1024,4,1,192]{3,2,1,0:T(2,128)(2,1)} %get-tuple-element.10) | data formatting | bytes 3145728 | tf_op jit(solution)/shard_map/slice | solution.py:126
  217.7 1.4 slice-done.1
  219.1 1.5 copy.145
  220.5 1.3 reshape.278
  221.9 1.5 fusion.73
  226.2 2.1 fusion.76
  228.3 1.9 copy.151
  233.5 1.4 convolution_convert_fusion.1
  234.9 6.7 %all-to-all-start = ((bf16[8,16,2432]{2,1,0:T(8,128)(2,1)}), bf16[8,16,2432]{2,1,0:T(8,128)(2,1)S(1)}, u32[]{:S(2)}, u32[]{:S(2)}) async-start(bf16[8,16,2432]{2,1,0:T(8,128)(2,1)} %bitcast.28), calls=%async_computation | async-start | bytes 1245184 | tf_op jit(solution)/shard_map/all_to_all | solution.py:39
  241.6 9.7 %all-gather.9.cloned.1.call-done = bf16[2,2432,704]{2,0,1:T(2,128)(2,1)} async-done(((bf16[2,76,704]{2,0,1:T(2,128)(2,1)}), bf16[2,2432,704]{2,0,1:T(2,128)(2,1)}) %all-gather.9.cloned.1.call-update) | async-done | bytes 6848528 | tf_op jit(solution)/shard_map/all_gather | solution.py:86
  251.3 16.0 %fusion.70 = (bf16[1,2432,704]{2,0,1:T(2,128)(2,1)}, bf16[1,2432,704]{2,0,1:T(2,128)(2,1)}) fusion(bf16[2,2432,704]{2,0,1:T(2,128)(2,1)} %all-gather.9.cloned.1.call-done), kind=kLoop, calls=%fused_computation.129 | loop fusion | bytes 13697024 | tf_op jit(solution)/shard_map/slice | solution.py:179
  267.3 15.9 %copy.162 = bf16[1,2432,704]{1,2,0:T(8,128)(2,1)} copy(bf16[1,2432,704]{2,0,1:T(2,128)(2,1)} %get-tuple-element.9) | data formatting | bytes 6848512
  283.3 16.0 %copy.161 = bf16[1,2432,704]{1,2,0:T(8,128)(2,1)} copy(bf16[1,2432,704]{2,0,1:T(2,128)(2,1)} %get-tuple-element.8) | data formatting | bytes 6848512
  300.8 35.8 %all_gather.22 = bf16[128,2432]{1,0:T(8,128)(2,1)S(1)} all-gather(bf16[16,2432]{1,0:T(8,128)(2,1)S(1)} %add_convert_fusion.2), channel_id=1, replica_groups=mesh['cfg'=2,'seq'=32,'wgt'=8] {'wgt'}, dimensions={0}, use_global_device_ids=true | all-gather | bytes 700416 | tf_op jit(solution)/shard_map/all_gather | solution.py:176
  336.7 6.5 %convolution_convert_fusion = bf16[128,2432]{1,0:T(8,128)(2,1)} fusion(bf16[1,2432,704]{1,2,0:T(8,128)(2,1)} %copy.162, bf16[128,2432]{1,0:T(8,128)(2,1)S(1)} %all_gather.22, bf16[1,2432,704]{1,2,0:T(8,128)(2,1)} %copy.161), kind=kOutput, calls=%fused_computation.2 | convolution fusion | flops 877731840 | bytes 8093696 | tf_op jit(solution)/shard_map/rf,df->rd/dot_general | solution.py:182
  343.1 7.3 %all-to-all-start.1 = ((bf16[8,16,2432]{2,1,0:T(8,128)(2,1)}), bf16[8,16,2432]{2,1,0:T(8,128)(2,1)S(1)}, u32[]{:S(2)}, u32[]{:S(2)}) async-start(bf16[8,16,2432]{2,1,0:T(8,128)(2,1)} %bitcast.37), calls=%async_computation.1 | async-start | bytes 1245184 | tf_op jit(solution)/shard_map/all_to_all | solution.py:39
  350.8 10.4 %all-to-all-done.1 = bf16[8,16,2432]{2,1,0:T(8,128)(2,1)S(1)} async-done(((bf16[8,16,2432]{2,1,0:T(8,128)(2,1)}), bf16[8,16,2432]{2,1,0:T(8,128)(2,1)S(1)}, u32[]{:S(2)}, u32[]{:S(2)}) %all-to-all-start.1) | async-done | bytes 622624 | tf_op jit(solution)/shard_map/all_to_all | solution.py:39
  362.0 2.5 collective-permute-start
  364.6 2.9 collective-permute-done
  (161 shorter events, 27.9 us)
Async XLA Ops:
  7.2 354.6 %copy-start = (bf16[2432,64]{0,1:T(8,128)(2,1)S(1)}, bf16[2432,64]{0,1:T(8,128)(2,1)}, u32[]{:S(2)}) copy-start(bf16[2432,64]{0,1:T(8,128)(2,1)} %param.25) | copy-start | bytes 933892
  7.2 86.9 %all-gather.7.cloned.1.call-start = ((), (), s32[]{:S(2)}) async-start(), calls=%async_computation.2 | async-start | bytes 10272768 | tf_op jit(solution)/shard_map/all_gather | solution.py:84
  10.0 164.2 %all-gather.11.cloned.1.call-start = ((), (), s32[]{:S(2)}) async-start(), calls=%async_computation.4 | async-start | bytes 4866048 | tf_op jit(solution)/shard_map/all_gather | solution.py:116
  13.5 1.6 copy-start.2
  15.2 4.8 %copy-start.7 = (bf16[1,16,2432]{2,1,0:T(8,128)(2,1)S(1)}, bf16[1,16,2432]{2,1,0:T(8,128)(2,1)}, u32[]{:S(2)}) copy-start(bf16[1,16,2432]{2,1,0:T(8,128)(2,1)} %param.15) | copy-start | bytes 233476
  15.3 8.7 %copy-start.1 = (f32[128,2432]{1,0:T(8,128)}, f32[128,2432]{1,0:T(8,128)S(1)}, u32[]{:S(2)}) copy-start(f32[128,2432]{1,0:T(8,128)S(1)} %reshape.279) | copy-start | bytes 3735556
  22.3 71.8 %copy-start.11 = (bf16[16,2432]{1,0:T(8,128)(2,1)S(1)}, bf16[16,2432]{1,0:T(8,128)(2,1)}, u32[]{:S(2)}) copy-start(bf16[16,2432]{1,0:T(8,128)(2,1)} %fusion.49) | copy-start | bytes 233476
  100.7 1.6 copy-start.22
  101.1 2.1 copy-start.18
  101.1 2.1 copy-start.19
  102.0 2.2 copy-start.17
  102.0 3.0 copy-start.20
  103.2 148.1 %all-gather.9.cloned.1.call-start = ((), (), s32[]{:S(2)}) async-start(), calls=%async_computation.3 | async-start | bytes 7704576 | tf_op jit(solution)/shard_map/all_gather | solution.py:86
  138.8 1.3 copy-start.16
  138.8 2.0 copy-start.15
  141.7 0.7 copy-start.4
  174.2 1.9 slice-start
  217.7 1.4 slice-start.1
  221.9 3.1 copy-start.5
  230.1 1.1 copy-start.6
  231.6 0.9 copy-start.12
  232.2 1.4 copy-start.3
  234.9 64.3 %all-to-all-start = ((bf16[8,16,2432]{2,1,0:T(8,128)(2,1)}), bf16[8,16,2432]{2,1,0:T(8,128)(2,1)S(1)}, u32[]{:S(2)}, u32[]{:S(2)}) async-start(bf16[8,16,2432]{2,1,0:T(8,128)(2,1)} %bitcast.28), calls=%async_computation | async-start | bytes 1245184 | tf_op jit(solution)/shard_map/all_to_all | solution.py:39
  283.3 16.1 %copy-start.8 = (f32[16,2432]{1,0:T(8,128)S(1)}, f32[16,2432]{1,0:T(8,128)}, u32[]{:S(2)}) copy-start(f32[16,2432]{1,0:T(8,128)} %mul.296) | copy-start | bytes 466948
  299.3 1.4 copy-start.9
  299.3 1.4 copy-start.10
  336.7 13.8 %copy-start.14 = (f32[4,2432]{1,0:T(4,128)S(1)}, f32[4,2432]{1,0:T(4,128)}, u32[]{:S(2)}) copy-start(f32[4,2432]{1,0:T(4,128)} %get-tuple-element.20) | copy-start | bytes 116740
  343.1 7.4 %copy-start.13 = (f32[4,2432]{1,0:T(4,128)S(1)}, f32[4,2432]{1,0:T(4,128)}, u32[]{:S(2)}) copy-start(f32[4,2432]{1,0:T(4,128)} %get-tuple-element.21) | copy-start | bytes 116740
  343.1 18.1 %all-to-all-start.1 = ((bf16[8,16,2432]{2,1,0:T(8,128)(2,1)}), bf16[8,16,2432]{2,1,0:T(8,128)(2,1)S(1)}, u32[]{:S(2)}, u32[]{:S(2)}) async-start(bf16[8,16,2432]{2,1,0:T(8,128)(2,1)} %bitcast.37), calls=%async_computation.1 | async-start | bytes 1245184 | tf_op jit(solution)/shard_map/all_to_all | solution.py:39
  350.6 13.9 %copy-start.23 = (s32[4]{0:T(128)S(1)}, s32[4]{0:T(128)}, u32[]{:S(2)}) copy-start(s32[4]{0:T(128)} %param.17) | copy-start | bytes 52
  350.7 16.9 %copy-start.21 = (f32[4,2,64]{2,1,0:T(2,128)S(1)}, f32[4,2,64]{2,1,0:T(2,128)}, u32[]{:S(2)}) copy-start(f32[4,2,64]{2,1,0:T(2,128)} %param.13) | copy-start | bytes 6148
  362.0 5.5 %collective-permute-start = (f32[4,2,64]{2,1,0:T(2,128)S(1)}, f32[4,2,64]{2,1,0:T(2,128)S(1)}, u32[]{:S(2)}, u32[]{:S(2)}) collective-permute-start(f32[4,2,64]{2,1,0:T(2,128)S(1)} %constant_dynamic-slice_fusion), channel_id=1, source_target_pairs={{0,256},{256,0},{1,257},{257,1},{2,258},{258,2},{3,259},{259,3},{4... | collective-permute-start | bytes 6152 | tf_op jit(solution)/shard_map/ppermute | solution.py:18
Sparse Core Ops, SparseCore 0:
  10.2 83.8 all-gather.6
  103.3 70.8 all-gather.10
  176.4 74.9 all-gather.8

commit v2 on v1

--- a/solution.py
+++ b/solution.py
@@ -1,6 +1,8 @@
 import jax
 import jax.numpy as jnp
 from jax import lax
+from jax.experimental import pallas as pl
+from jax.experimental.pallas import tpu as pltpu
 from jax.sharding import PartitionSpec as P
 
 STEPS = 28
@@ -39,6 +41,57 @@
     swapped = lax.all_to_all(partial, "wgt", 0, 0, tiled=True)
     rows = swapped.shape[0] // groups
     return jnp.sum(swapped.reshape(groups, rows, -1).astype(jnp.float32), axis=0)
+
+
+def make_attention(heads, head_size, text_at, text_here):
+    scale = head_size ** (-0.5)
+
+    def kernel(q_ref, kv_ref, mask_ref, o_ref):
+        requests, tokens, cols = q_ref.shape
+        blocks = kv_ref.shape[0]
+        lane = lax.broadcasted_iota(jnp.int32, (1, cols), 1)
+        k_txt = kv_ref[:, text_at : text_at + text_here, :].reshape(blocks * text_here, cols)
+        v_txt = kv_ref[:, text_at + text_here : text_at + 2 * text_here, :].reshape(
+            blocks * text_here, cols
+        )
+        dims = (((1,), (1,)), ((), ()))
+        for r in range(requests):
+            q = q_ref[r].astype(jnp.float32)
+            k_img = kv_ref[:, 2 * tokens * r : 2 * tokens * r + tokens, :].reshape(
+                blocks * tokens, cols
+            )
+            v_img = kv_ref[:, 2 * tokens * r + tokens : 2 * tokens * (r + 1), :].reshape(
+                blocks * tokens, cols
+            )
+            allowed = mask_ref[r : r + 1, :] > 0.5
+            out = jnp.zeros((tokens, cols), jnp.float32)
+            for h in range(heads):
+                in_head = (lane >= h * head_size) & (lane < (h + 1) * head_size)
+                qh = jnp.where(in_head, q, 0.0).astype(jnp.bfloat16)
+                s_img = lax.dot_general(qh, k_img, dims, preferred_element_type=jnp.float32) * scale
+                s_txt = lax.dot_general(qh, k_txt, dims, preferred_element_type=jnp.float32) * scale
+                s_txt = jnp.where(allowed, s_txt, masked_score)
+                top = jnp.maximum(
+                    jnp.max(s_img, axis=1, keepdims=True), jnp.max(s_txt, axis=1, keepdims=True)
+                )
+                p_img = jnp.exp(s_img - top)
+                p_txt = jnp.exp(s_txt - top)
+                total = jnp.sum(p_img, axis=1, keepdims=True) + jnp.sum(p_txt, axis=1, keepdims=True)
+                acc = jnp.dot(
+                    p_img.astype(jnp.bfloat16), v_img, preferred_element_type=jnp.float32
+                ) + jnp.dot(p_txt.astype(jnp.bfloat16), v_txt, preferred_element_type=jnp.float32)
+                out = jnp.where(in_head, acc / total, out)
+            o_ref[r] = out.astype(o_ref.dtype)
+
+    def run(q, kv, mask):
+        return pl.pallas_call(
+            kernel,
+            out_shape=jax.ShapeDtypeStruct(q.shape, jnp.bfloat16),
+            in_specs=[pl.BlockSpec(memory_space=pltpu.VMEM)] * 3,
+            out_specs=pl.BlockSpec(memory_space=pltpu.VMEM),
+        )(q, kv, mask)
+
+    return run
 
 
 def body(
@@ -82,8 +135,13 @@
     ).astype(jnp.bfloat16)
     all_weights = jnp.concatenate([qkv_weight, text_weight], axis=0)
     piece = lax.all_gather(all_weights, "seq", axis=1, tiled=True)
-    mlp_local = jnp.stack([expand_weight, contract_weight.T], axis=0)
-    mlp_full = lax.all_gather(mlp_local, "seq", axis=1, tiled=True)
+    block_rows = expand_weight.shape[0]
+    padded_rows = block_rows + (-block_rows) % 8
+    mlp_local = jnp.pad(
+        jnp.stack([expand_weight, contract_weight.T], axis=0),
+        ((0, 0), (0, padded_rows - block_rows), (0, 0)),
+    )
+    mlp_full = lax.all_gather(mlp_local, "seq", axis=0, tiled=False)
     out_full = lax.all_gather(out_weight, "seq", axis=1, tiled=True)
     both_rows = jnp.concatenate([token_rows, text_normed], axis=0)
     both_term = jnp.einsum(
@@ -102,61 +160,38 @@
         text_term[:, 3].reshape(text_here, heads_here, head_size), qk_gain[1]
     ).astype(jnp.bfloat16)
     values_txt = text_term[:, 4].astype(jnp.bfloat16)
-    image_pair = jnp.stack(
-        [keys_img.reshape(tokens_here, requests, local_cols), values_img], axis=2
-    ).reshape(tokens_here * requests * 2, local_cols)
-    text_pair = jnp.stack([keys_txt.reshape(text_here, local_cols), values_txt], axis=1).reshape(
-        text_here * 2, local_cols
-    )
+    image_pair = jnp.transpose(
+        jnp.stack([keys_img.reshape(tokens_here, requests, local_cols), values_img], axis=0),
+        (2, 0, 1, 3),
+    ).reshape(requests * 2 * tokens_here, local_cols)
+    text_pair = jnp.stack([keys_txt.reshape(text_here, local_cols), values_txt], axis=0).reshape(
+        2 * text_here, local_cols
+    )
+    lanes = local_cols + (-local_cols) % 128
+    image_pair = jnp.pad(image_pair, ((0, 0), (0, lanes - local_cols)))
+    text_pair = jnp.pad(text_pair, ((0, 0), (0, lanes - local_cols)))
     owner_row = jnp.pad(
-        segment_row.astype(jnp.float32).astype(jnp.bfloat16), (0, local_cols - text_here)
+        segment_row.astype(jnp.float32).astype(jnp.bfloat16), (0, lanes - text_here)
     )[None, :]
-    image_len = tokens_here * requests * 2
-    shared = jnp.concatenate([image_pair, text_pair, owner_row], axis=0)
+    image_len = requests * 2 * tokens_here
+    owner_at = image_len + 2 * text_here
+    pad_rows = (-(owner_at + 1)) % 16
+    shared = jnp.concatenate(
+        [image_pair, text_pair, owner_row, jnp.zeros((pad_rows, lanes), jnp.bfloat16)], axis=0
+    )
     shared_piece = lax.all_gather(shared, "seq", axis=0, tiled=False)
-    image_piece = shared_piece[:, :image_len].reshape(
-        seq_size * tokens_here, requests, 2, local_cols
-    )
-    text_piece = shared_piece[:, image_len : image_len + 2 * text_here].reshape(
-        seq_size * text_here, 2, local_cols
-    )
-    owner_piece = shared_piece[:, image_len + 2 * text_here, :text_here].reshape(-1)
-    scale_factor = head_size ** (-0.5)
+    owner_piece = shared_piece[:, owner_at, :text_here].reshape(-1)
     request_ids = jnp.arange(requests, dtype=jnp.float32)
-    piece_keys = image_piece[:, :, 0].reshape(-1, requests, heads_here, head_size)
-    piece_values = image_piece[:, :, 1].reshape(-1, requests, heads_here, head_size)
-    text_keys = text_piece[:, 0].reshape(-1, heads_here, head_size)
-    text_values = text_piece[:, 1].reshape(-1, heads_here, head_size)
-    image_scores = (
-        jnp.einsum("qrhd,krhd->rhqk", queries, piece_keys, preferred_element_type=jnp.float32)
-        * scale_factor
-    )
-    text_scores = (
-        jnp.einsum("qrhd,khd->rhqk", queries, text_keys, preferred_element_type=jnp.float32)
-        * scale_factor
-    )
-    allowed = owner_piece.astype(jnp.float32)[None, :] == request_ids[:, None]
-    text_scores = jnp.where(allowed[:, None, None, :], text_scores, masked_score)
-    row_max = jnp.maximum(jnp.max(image_scores, axis=-1), jnp.max(text_scores, axis=-1))
-    image_weights = jnp.exp(image_scores - row_max[..., None])
-    text_weights = jnp.exp(text_scores - row_max[..., None])
-    row_sum = jnp.sum(image_weights, axis=-1) + jnp.sum(text_weights, axis=-1)
-    acc = jnp.einsum(
-        "rhqk,krhd->rhqd",
-        image_weights.astype(jnp.bfloat16),
-        piece_values,
-        preferred_element_type=jnp.float32,
-    )
-    acc = acc + jnp.einsum(
-        "rhqk,khd->rhqd",
-        text_weights.astype(jnp.bfloat16),
-        text_values,
-        preferred_element_type=jnp.float32,
-    )
-    attended = acc / row_sum[..., None]
-    attended = (
-        jnp.transpose(attended, (2, 0, 1, 3)).reshape(row_count, local_cols).astype(jnp.bfloat16)
-    )
+    text_mask = (owner_piece.astype(jnp.float32)[None, :] == request_ids[:, None]).astype(
+        jnp.float32
+    )
+    query_block = jnp.pad(
+        jnp.transpose(queries.reshape(tokens_here, requests, local_cols), (1, 0, 2)),
+        ((0, 0), (0, 0), (0, lanes - local_cols)),
+    )
+    attend = make_attention(heads_here, head_size, image_len, text_here)
+    attended = attend(query_block, shared_piece, text_mask)
+    attended = jnp.transpose(attended[:, :, :local_cols], (1, 0, 2)).reshape(row_count, local_cols)
     share_rows = row_count // wgt_size
     mixed = group_sum(
         jnp.dot(attended, out_full, preferred_element_type=jnp.float32).astype(jnp.bfloat16),
@@ -173,17 +208,27 @@
     branch_in = (layer_norm(residual) * (1.0 + modulate[:, 6]) + modulate[:, 5]).astype(
         jnp.bfloat16
     )
-    branch_rows = lax.all_gather(
-        branch_in.reshape(share_rows, feat_width), "wgt", axis=0, tiled=True
-    )
-    expanded = jnp.dot(branch_rows, mlp_full[0], preferred_element_type=jnp.float32)
+    branch_rows = lax.all_to_all(
+        jnp.broadcast_to(
+            branch_in.reshape(1, share_rows, feat_width), (wgt_size, share_rows, feat_width)
+        ),
+        "wgt",
+        0,
+        0,
+        tiled=True,
+    ).reshape(row_count, feat_width)
+    padded_rows_in = jnp.pad(
+        branch_rows.reshape(row_count, seq_size, block_rows),
+        ((0, 0), (0, 0), (0, padded_rows - block_rows)),
+    )
+    expanded = jnp.einsum(
+        "rsd,sdf->rf", padded_rows_in, mlp_full[:, 0], preferred_element_type=jnp.float32
+    )
     expanded = jax.nn.gelu(expanded, approximate=True).astype(jnp.bfloat16)
-    branch = group_sum(
-        jnp.einsum(
-            "rf,df->rd", expanded, mlp_full[1], preferred_element_type=jnp.float32
-        ).astype(jnp.bfloat16),
-        wgt_size,
-    )
+    contracted = jnp.einsum(
+        "rf,sdf->rsd", expanded, mlp_full[:, 1], preferred_element_type=jnp.float32
+    )[:, :, :block_rows].reshape(row_count, feat_width)
+    branch = group_sum(contracted.astype(jnp.bfloat16), wgt_size)
     second = residual + modulate[:, 7] * branch.reshape(tokens_out, requests, feat_width)
     final_in = (layer_norm(second) * (1.0 + modulate[:, 9]) + modulate[:, 8]).astype(jnp.bfloat16)
     own_velocity = jnp.dot(

time: 377 us -> 298 us (0.79)
  local copies, waits for them, and re-layouts: 115 us -> 21.2 us
  waiting for transfers between devices: 125 us -> 155 us
  blocking collectives: 69.7 us -> 48.9 us
  Pallas kernels: 0 us -> 9.76 us
    slice x14 -> x1, local copies, waits for them, and re-layouts: 58.6 us -> 1.9 us  [body(): jnp.einsum('rf,sdf->rsd', expanded, mlp_full[:, 1], preferred_element_typ...]
    all_gather x1 -> x0, blocking collectives: 35.8 us -> none  [body(): lax.all_gather(branch_in.reshape(share_rows, feat_width), 'wgt', axis=0,...]
    unnamed x53 -> x38, local copies, waits for them, and re-layouts: 37.1 us -> 2.49 us
    all_to_all x0 -> x1, blocking collectives: none -> 15.4 us  [body(): lax.all_to_all(jnp.broadcast_to(branch_in.reshape(1, share_rows, feat_wid...]
    all_to_all x2, waiting for transfers between devices: 10.4 us -> 25.4 us  [group_sum(): swapped = lax.all_to_all(partial, 'wgt', 0, 0, tiled=True)]
    all_gather x1, waiting for transfers between devices: 9.66 us -> 22.7 us  [body(): mlp_full = lax.all_gather(mlp_local, 'seq', axis=0, tiled=False)]
    pallas_call x0 -> x1, Pallas kernels: none -> 9.76 us  [run(): pl.pallas_call(kernel, out_shape=jax.ShapeDtypeStruct(q.shape, jnp.bfloat...]
    reshape x4 -> x1, local copies, waits for them, and re-layouts: 8.93 us -> 0.04 us  [body(): jnp.transpose(attended[:, :, :local_cols], (1, 0, 2))]
  transfers between devices with their start and end apart: 6 -> 6, of which waited for: 5 -> 6; matrix products, arithmetic and copies ran while one was open for 33% -> 9% of each run, Pallas kernels for 0% -> 3%
where the time goes in v2:
time: 298 us; the launch traced here: 297 us
  waiting for transfers between devices  155 us (52%)
  blocking collectives  48.9 us (16%)
  local copies, waits for them, and re-layouts  21.2 us (7%)
  matrix products  17.2 us (6%)
  starting transfers between devices  16.3 us (5%)
  other arithmetic  14.5 us (5%)
  between operations  14.4 us (5%)
  Pallas kernels  9.76 us (3%)
    all_gather x1, waiting for transfers between devices, body(): piece = lax.all_gather(all_weights, 'seq', axis=1, tiled=True)  71.3 us
    all_gather x1, blocking collectives, body(): out_full = lax.all_gather(out_weight, 'seq', axis=1, tiled=True)  33.5 us
    all_gather x1, waiting for transfers between devices, body(): shared_piece = lax.all_gather(shared, 'seq', axis=0, tiled=False)  33.1 us
    all_to_all x2, waiting for transfers between devices, group_sum(): swapped = lax.all_to_all(partial, 'wgt', 0, 0, tiled=True)  25.4 us
    all_gather x1, waiting for transfers between devices, body(): mlp_full = lax.all_gather(mlp_local, 'seq', axis=0, tiled=False)  22.7 us
    all_to_all x1, blocking collectives, body(): lax.all_to_all(jnp.broadcast_to(branch_in.reshape(1, share_rows, feat_wid...  15.4 us
    all_to_all x2, starting transfers between devices, group_sum(): swapped = lax.all_to_all(partial, 'wgt', 0, 0, tiled=True)  13.5 us
    pallas_call x1, Pallas kernels, run(): pl.pallas_call(kernel, out_shape=jax.ShapeDtypeStruct(q.shape, jnp.bfloat...  9.76 us
  transfers between devices with their start and end apart: 6, of which 6 were waited for; matrix products, arithmetic and copies ran while one was open for 9% of the time, Pallas kernels for 3%

profile of v2, /device:TPU:32, one launch (start us, length us, event | category | flops | bytes accessed | tf_op | source)
XLA Modules:
  0.0 297.4 jit_solution(10229685511453182383)
XLA Ops:
  7.2 1.1 copy.54
  8.3 1.8 pad_maximum_fusion
  11.6 1.5 mul.312
  14.1 0.8 div.51
  14.9 1.3 fusion.5
  19.2 1.3 fusion.54
  20.5 0.7 fusion.45
  21.2 1.6 add_convert_fusion
  22.8 71.3 %all-gather.7.cloned.1.call-done = bf16[5,2432,192]{2,0,1:T(8,128)(2,1)} async-done(((bf16[5,76,192]{2,0,1:T(8,128)(2,1)}), bf16[5,2432,192]{2,0,1:T(8,128)(2,1)}) %all-gather.7.cloned.1.call-update) | async-done | bytes 4669456 | tf_op jit(solution)/shard_map/all_gather | solution.py:137
  94.1 6.1 %fusion.77 = (bf16[144,5,192]{2,0,1:T(8,128)(2,1)S(1)}, f32[144,5,192]{2,0,1:T(8,128)S(1)}) fusion(bf16[5,2432,192]{2,0,1:T(8,128)(2,1)} %all-gather.7.cloned.1.call-done, bf16[16,2432]{1,0:T(8,128)(2,1)S(1)} %copy-done.5, bf16[128,2432]{1,0:T(8,128)(2,1)S(1)} %add_convert_fusion), kind=kOutput, calls=%fused_computation.132 | convolution fusion | flops 673938432 | bytes 6199296 | tf_op jit(solution)/shard_map/rd,kdc->rkc/dot_general | solution.py:147
  102.1 0.8 fusion.48
  102.9 1.6 fusion.34
  104.7 33.5 %all-gather.2 = bf16[32,76,192]{2,1,0:T(8,128)(2,1)S(1)} all-gather(bf16[1,76,192]{2,1,0:T(8,128)(2,1)S(1)} %bitcast.153), channel_id=1, replica_groups=mesh['cfg'=2,'seq'=32,'wgt'=8] {'seq'}, dimensions={0}, use_global_device_ids=true | all-gather | bytes 963072 | tf_op jit(solution)/shard_map/all_gather | solution.py:145
  138.2 1.3 reshape.335
  141.3 33.1 %all-gather.9.cloned.1.call-done = bf16[9728,256]{1,0:T(8,128)(2,1)} async-done(((bf16[304,256]{1,0:T(8,128)(2,1)}), bf16[9728,256]{1,0:T(8,128)(2,1)}) %all-gather.9.cloned.1.call-update) | async-done | bytes 4980752 | tf_op jit(solution)/shard_map/all_gather | solution.py:182
  174.4 0.9 fusion.60
  176.0 9.8 %shard_map.140 = bf16[4,32,256]{2,1,0:T(8,128)(2,1)} custom-call(bf16[4,32,256]{2,1,0:T(8,128)(2,1)} %pad.24.q_ref, bf16[32,304,256]{2,1,0:T(8,128)(2,1)} %bitcast.145, f32[4,512]{1,0:T(4,128)} %fusion.63.mask_ref), custom_call_target="tpu_custom_call" | custom-call | tf_op jit(solution)/shard_map/pallas_call | solution.py:87
  185.7 0.8 slice_bitcast_fusion.15
  186.7 1.4 convolution_convert_fusion
  188.1 6.9 %all-to-all-start = ((bf16[8,16,2432]{2,1,0:T(8,128)(2,1)}), bf16[8,16,2432]{2,1,0:T(8,128)(2,1)S(1)}, u32[]{:S(2)}, u32[]{:S(2)}) async-start(bf16[8,16,2432]{2,1,0:T(8,128)(2,1)} %bitcast.23), calls=%async_computation | async-start | bytes 1245184 | tf_op jit(solution)/shard_map/all_to_all | solution.py:41
  195.3 12.7 %all-to-all-done = bf16[8,16,2432]{2,1,0:T(8,128)(2,1)S(1)} async-done(((bf16[8,16,2432]{2,1,0:T(8,128)(2,1)}), bf16[8,16,2432]{2,1,0:T(8,128)(2,1)S(1)}, u32[]{:S(2)}, u32[]{:S(2)}) %all-to-all-start) | async-done | bytes 622624 | tf_op jit(solution)/shard_map/all_to_all | solution.py:41
  208.7 15.4 %all_to_all.20 = bf16[8,16,2432]{2,1,0:T(8,128)(2,1)S(1)} all-to-all(bf16[8,16,2432]{2,1,0:T(8,128)(2,1)S(1)} %broadcast_in_dim.8), channel_id=1, replica_groups=mesh['cfg'=2,'seq'=32,'wgt'=8] {'wgt'}, dimensions={0} | all-to-all | bytes 1245184 | tf_op jit(solution)/shard_map/all_to_all | solution.py:211
  224.1 3.5 %reshape_reshape.3 = bf16[128,32,76]{2,1,0:T(8,128)(2,1)S(1)} reshape(bf16[8,16,2432]{2,1,0:T(8,128)(2,1)S(1)} %all_to_all.20) | data formatting | bytes 1245184 | tf_op jit(solution)/shard_map/reshape;reshape | solution.py:221
  227.6 1.1 copy.66
  228.7 22.7 %all-gather.11.cloned.1.call-done = bf16[64,80,704]{2,1,0:T(8,128)(2,1)} async-done(((bf16[2,80,704]{2,1,0:T(8,128)(2,1)}), bf16[64,80,704]{2,1,0:T(8,128)(2,1)}) %all-gather.11.cloned.1.call-update) | async-done | bytes 7208976 | tf_op jit(solution)/shard_map/all_gather | solution.py:144
  251.3 8.2 %fusion.2 = bf16[128,32,80]{0,2,1:T(8,128)(2,1)} fusion(bf16[32,2,80,704]{3,2,1,0:T(8,128)(2,1)} %bitcast.155, bf16[128,32,76]{0,2,1:T(8,128)(2,1)S(1)} %copy.66), kind=kOutput, calls=%fused_computation.3 | convolution fusion | flops 923557888 | bytes 8486912 | tf_op jit(solution)/shard_map/rf,sdf->rsd/dot_general | solution.py:228
  259.5 1.9 copy.69
  261.5 2.8 convert_element_type.158
  264.2 6.6 %all-to-all-start.2 = ((bf16[8,16,2432]{2,1,0:T(8,128)(2,1)}), bf16[8,16,2432]{2,1,0:T(8,128)(2,1)S(1)}, u32[]{:S(2)}, u32[]{:S(2)}) async-start(bf16[8,16,2432]{2,1,0:T(8,128)(2,1)} %convert_element_type.158), calls=%async_computation.2 | async-start | bytes 1245184 | tf_op jit(solution)/shard_map/all_to_all | solution.py:41
  271.2 12.7 %all-to-all-done.2 = bf16[8,16,2432]{2,1,0:T(8,128)(2,1)S(1)} async-done(((bf16[8,16,2432]{2,1,0:T(8,128)(2,1)}), bf16[8,16,2432]{2,1,0:T(8,128)(2,1)S(1)}, u32[]{:S(2)}, u32[]{:S(2)}) %all-to-all-start.2) | async-done | bytes 622624 | tf_op jit(solution)/shard_map/all_to_all | solution.py:41
  284.7 2.7 collective-permute-start
  287.5 2.7 collective-permute-done
  (134 shorter events, 12.6 us)
Async XLA Ops:
  7.2 277.3 %copy-start = (bf16[2432,64]{0,1:T(8,128)(2,1)S(1)}, bf16[2432,64]{0,1:T(8,128)(2,1)}, u32[]{:S(2)}) copy-start(bf16[2432,64]{0,1:T(8,128)(2,1)} %param.25) | copy-start | bytes 933892
  7.2 3.0 %copy-start.4 = (f32[1,4,10,2432]{3,1,2,0:T(4,128)S(1)}, f32[1,4,10,2432]{3,1,2,0:T(4,128)}, u32[]{:S(2)}) copy-start(f32[1,4,10,2432]{3,1,2,0:T(4,128)} %param.18) | copy-start | bytes 1167364
  7.2 86.9 %all-gather.7.cloned.1.call-start = ((), (), s32[]{:S(2)}) async-start(), calls=%async_computation.3 | async-start | bytes 10272768 | tf_op jit(solution)/shard_map/all_gather | solution.py:137
  10.1 164.3 %all-gather.9.cloned.1.call-start = ((), (), s32[]{:S(2)}) async-start(), calls=%async_computation.4 | async-start | bytes 5136384 | tf_op jit(solution)/shard_map/all_gather | solution.py:182
  11.6 1.5 copy-start.1
  13.1 3.7 %copy-start.16 = (f32[2,64]{1,0:T(2,128)S(1)}, f32[2,64]{1,0:T(2,128)}, u32[]{:S(2)}) copy-start(f32[2,64]{1,0:T(2,128)} %param.19) | copy-start | bytes 1540
  13.1 5.7 %copy-start.3 = (bf16[1,16,2432]{2,1,0:T(8,128)(2,1)S(1)}, bf16[1,16,2432]{2,1,0:T(8,128)(2,1)}, u32[]{:S(2)}) copy-start(bf16[1,16,2432]{2,1,0:T(8,128)(2,1)} %param.15) | copy-start | bytes 233476
  21.2 72.9 %copy-start.5 = (bf16[16,2432]{1,0:T(8,128)(2,1)S(1)}, bf16[16,2432]{1,0:T(8,128)(2,1)}, u32[]{:S(2)}) copy-start(bf16[16,2432]{1,0:T(8,128)(2,1)} %fusion.45) | copy-start | bytes 233476
  100.8 1.3 copy-start.15
  101.1 1.8 copy-start.11
  101.5 3.1 %copy-start.14 = (f32[64]{0:T(128)S(1)}, f32[64]{0:T(128)}, u32[]{:S(2)}) copy-start(f32[64]{0:T(128)} %get-tuple-element.21) | copy-start | bytes 772
  101.6 3.1 %copy-start.12 = (bf16[192,76]{0,1:T(8,128)(2,1)S(1)}, bf16[192,76]{0,1:T(8,128)(2,1)}, u32[]{:S(2)}) copy-start(bf16[192,76]{0,1:T(8,128)(2,1)} %param.22) | copy-start | bytes 87556
  102.9 148.5 %all-gather.11.cloned.1.call-start = ((), (), s32[]{:S(2)}) async-start(), calls=%async_computation.5 | async-start | bytes 8110080 | tf_op jit(solution)/shard_map/all_gather | solution.py:144
  176.0 10.7 %copy-start.2 = (bf16[2432,192]{1,0:T(8,128)(2,1)S(1)}, bf16[2432,192]{1,0:T(8,128)(2,1)}, u32[]{:S(2)}) copy-start(bf16[2432,192]{1,0:T(8,128)(2,1)} %reshape.335) | copy-start | bytes 2801668
  186.7 8.4 %copy-start.10 = (f32[4,2432]{1,0:T(4,128)S(1)}, f32[4,2432]{1,0:T(4,128)}, u32[]{:S(2)}) copy-start(f32[4,2432]{1,0:T(4,128)} %get-tuple-element.19) | copy-start | bytes 116740
  188.1 7.0 %copy-start.9 = (f32[4,2432]{1,0:T(4,128)S(1)}, f32[4,2432]{1,0:T(4,128)}, u32[]{:S(2)}) copy-start(f32[4,2432]{1,0:T(4,128)} %get-tuple-element.15) | copy-start | bytes 116740
  188.1 7.1 %copy-start.8 = (f32[4,2432]{1,0:T(4,128)S(1)}, f32[4,2432]{1,0:T(4,128)}, u32[]{:S(2)}) copy-start(f32[4,2432]{1,0:T(4,128)} %get-tuple-element.12) | copy-start | bytes 116740
  188.1 19.9 %all-to-all-start = ((bf16[8,16,2432]{2,1,0:T(8,128)(2,1)}), bf16[8,16,2432]{2,1,0:T(8,128)(2,1)S(1)}, u32[]{:S(2)}, u32[]{:S(2)}) async-start(bf16[8,16,2432]{2,1,0:T(8,128)(2,1)} %bitcast.23), calls=%async_computation | async-start | bytes 1245184 | tf_op jit(solution)/shard_map/all_to_all | solution.py:41
  261.4 9.4 %copy-start.7 = (f32[4,2432]{1,0:T(4,128)S(1)}, f32[4,2432]{1,0:T(4,128)}, u32[]{:S(2)}) copy-start(f32[4,2432]{1,0:T(4,128)} %get-tuple-element.16) | copy-start | bytes 116740
  264.2 6.7 %copy-start.6 = (f32[4,2432]{1,0:T(4,128)S(1)}, f32[4,2432]{1,0:T(4,128)}, u32[]{:S(2)}) copy-start(f32[4,2432]{1,0:T(4,128)} %get-tuple-element.13) | copy-start | bytes 116740
  264.2 19.7 %all-to-all-start.2 = ((bf16[8,16,2432]{2,1,0:T(8,128)(2,1)}), bf16[8,16,2432]{2,1,0:T(8,128)(2,1)S(1)}, u32[]{:S(2)}, u32[]{:S(2)}) async-start(bf16[8,16,2432]{2,1,0:T(8,128)(2,1)} %convert_element_type.158), calls=%async_computation.2 | async-start | bytes 1245184 | tf_op jit(solution)/shard_map/all_to_all | solution.py:41
  271.2 16.3 %copy-start.17 = (s32[4]{0:T(128)S(1)}, s32[4]{0:T(128)}, u32[]{:S(2)}) copy-start(s32[4]{0:T(128)} %param.17) | copy-start | bytes 52
  271.2 19.1 %copy-start.13 = (f32[4,2,64]{2,1,0:T(2,128)S(1)}, f32[4,2,64]{2,1,0:T(2,128)}, u32[]{:S(2)}) copy-start(f32[4,2,64]{2,1,0:T(2,128)} %param.13) | copy-start | bytes 6148
  284.7 5.5 %collective-permute-start = (f32[4,2,64]{2,1,0:T(2,128)S(1)}, f32[4,2,64]{2,1,0:T(2,128)S(1)}, u32[]{:S(2)}, u32[]{:S(2)}) collective-permute-start(f32[4,2,64]{2,1,0:T(2,128)S(1)} %constant_dynamic-slice_fusion), channel_id=1, source_target_pairs={{0,256},{256,0},{1,257},{257,1},{2,258},{258,2},{3,259},{259,3},{4... | collective-permute-start | bytes 6152 | tf_op jit(solution)/shard_map/ppermute | solution.py:20
Sparse Core Ops, SparseCore 0:
  10.2 83.8 all-gather.6
  103.0 71.3 all-gather.8
  176.5 74.7 all-gather.10

commit v3 on v2

--- a/solution.py
+++ b/solution.py
@@ -133,10 +133,14 @@
     text_normed = (
         layer_norm(txt_hidden[0].astype(jnp.float32)) * (1.0 + text_mod[:, 1]) + text_mod[:, 0]
     ).astype(jnp.bfloat16)
-    all_weights = jnp.concatenate([qkv_weight, text_weight], axis=0)
-    piece = lax.all_gather(all_weights, "seq", axis=1, tiled=True)
-    block_rows = expand_weight.shape[0]
+    block_rows = qkv_weight.shape[1]
     padded_rows = block_rows + (-block_rows) % 8
+    kinds = qkv_weight.shape[0] + text_weight.shape[0]
+    all_weights = jnp.transpose(
+        jnp.concatenate([qkv_weight, text_weight], axis=0), (1, 0, 2)
+    ).reshape(block_rows, kinds * local_cols)
+    all_weights = jnp.pad(all_weights, ((0, padded_rows - block_rows), (0, 0)))
+    piece = lax.all_gather(all_weights, "seq", axis=0, tiled=False)
     mlp_local = jnp.pad(
         jnp.stack([expand_weight, contract_weight.T], axis=0),
         ((0, 0), (0, padded_rows - block_rows), (0, 0)),
@@ -144,9 +148,14 @@
     mlp_full = lax.all_gather(mlp_local, "seq", axis=0, tiled=False)
     out_full = lax.all_gather(out_weight, "seq", axis=1, tiled=True)
     both_rows = jnp.concatenate([token_rows, text_normed], axis=0)
+    both_count = both_rows.shape[0]
+    both_rows = jnp.pad(
+        both_rows.reshape(both_count, seq_size, block_rows),
+        ((0, 0), (0, 0), (0, padded_rows - block_rows)),
+    )
     both_term = jnp.einsum(
-        "rd,kdc->rkc", both_rows, piece, preferred_element_type=jnp.float32
-    )
+        "rsd,sdn->rn", both_rows, piece, preferred_element_type=jnp.float32
+    ).reshape(both_count, kinds, local_cols)
     image_term = both_term[:row_count]
     text_term = both_term[row_count:]
     queries = head_norm(

time: 298 us -> 294 us (0.987)
  local copies, waits for them, and re-layouts: 21.2 us -> 53 us
  waiting for transfers between devices: 155 us -> 124 us
  matrix products: 17.2 us -> 13.8 us
    all_gather x1, waiting for transfers between devices: 71.3 us -> 40.6 us  [body(): piece = lax.all_gather(all_weights, 'seq', axis=0, tiled=False)]
    add x2 -> x3, local copies, waits for them, and re-layouts: 0.59 us -> 8.09 us  [body(): layer_norm(hidden) * (1.0 + modulate[:, 1]) + modulate[:, 0]]
    convert_element_type x1 -> x3, local copies, waits for them, and re-layouts: 0.08 us -> 6.89 us  [body(): hidden = img_hidden[0].astype(jnp.float32)]
    mul x2 -> x3, local copies, waits for them, and re-layouts: 1.63 us -> 8.15 us  [body(): layer_norm(hidden) * (1.0 + modulate[:, 1]) + modulate[:, 0]]
    convert_element_type x0 -> x2, local copies, waits for them, and re-layouts: none -> 4.1 us  [body(): txt_hidden[0].astype(jnp.float32)]
    squeeze x0 -> x2, local copies, waits for them, and re-layouts: none -> 3.22 us  [body(): text_mod[:, 0]]
  transfers between devices with their start and end apart: 6 -> 6, of which waited for: 6 -> 6; matrix products, arithmetic and copies ran while one was open for 9% -> 18% of each run, Pallas kernels for 3% -> 3%
where the time goes in v3:
time: 294 us; the launch traced here: 293 us
  waiting for transfers between devices  124 us (42%)
  local copies, waits for them, and re-layouts  53 us (18%)
  blocking collectives  49 us (17%)
  starting transfers between devices  16.1 us (5%)
  between operations  14.6 us (5%)
  matrix products  13.8 us (5%)
  other arithmetic  12.9 us (4%)
  Pallas kernels  9.68 us (3%)
    all_gather x1, waiting for transfers between devices, body(): piece = lax.all_gather(all_weights, 'seq', axis=0, tiled=False)  40.6 us
    all_gather x1, waiting for transfers between devices, body(): shared_piece = lax.all_gather(shared, 'seq', axis=0, tiled=False)  34 us
    all_gather x1, blocking collectives, body(): out_full = lax.all_gather(out_weight, 'seq', axis=1, tiled=True)  33.6 us
    all_to_all x2, waiting for transfers between devices, group_sum(): swapped = lax.all_to_all(partial, 'wgt', 0, 0, tiled=True)  24.2 us
    all_gather x1, waiting for transfers between devices, body(): mlp_full = lax.all_gather(mlp_local, 'seq', axis=0, tiled=False)  22.5 us
    all_to_all x1, blocking collectives, body(): lax.all_to_all(jnp.broadcast_to(branch_in.reshape(1, share_rows, feat_wid...  15.4 us
    all_to_all x2, starting transfers between devices, group_sum(): swapped = lax.all_to_all(partial, 'wgt', 0, 0, tiled=True)  13.3 us
    pallas_call x1, Pallas kernels, run(): pl.pallas_call(kernel, out_shape=jax.ShapeDtypeStruct(q.shape, jnp.bfloat...  9.68 us
  transfers between devices with their start and end apart: 6, of which 6 were waited for; matrix products, arithmetic and copies ran while one was open for 18% of the time, Pallas kernels for 3%

profile of v3, /device:TPU:32, one launch (start us, length us, event | category | flops | bytes accessed | tf_op | source)
XLA Modules:
  0.0 293.0 jit_solution(15228481704663987715)
XLA Ops:
  10.9 1.2 mul.315
  12.1 4.8 %mul.316 = f32[128,32,76]{2,1,0:T(8,128)S(1)} reshape(f32[32,4,2432]{2,1,0:T(4,128)} %mul.315) | data formatting | bytes 2490368 | tf_op jit(solution)/shard_map/mul | solution.py:123
  16.9 2.2 copy.133
  19.1 1.2 add.220
  20.3 4.8 %add.221 = f32[128,32,76]{2,1,0:T(8,128)S(1)} reshape(f32[32,4,2432]{2,1,0:T(4,128)} %add.220) | data formatting | bytes 2490368 | tf_op jit(solution)/shard_map/add | solution.py:123
  25.1 2.1 copy.134
  27.2 3.5 %reshape.365 = f32[128,32,76]{2,1,0:T(8,128)S(1)} reshape(bf16[1,32,4,2432]{3,2,1,0:T(4,128)(2,1)S(1)} %copy-done.1) | data formatting | bytes 1867776 | tf_op jit(solution)/shard_map/convert_element_type | solution.py:122
  31.8 2.2 copy.132
  34.8 1.2 copy.136
  37.1 2.1 copy.137
  40.4 3.0 %copy.135 = f32[16,32,76]{0,1,2:T(8,128)} copy(f32[16,32,76]{2,1,0:T(8,128)} %reshape.366) | data formatting | bytes 311296 | tf_op jit(solution)/shard_map/convert_element_type | solution.py:134
  43.7 1.9 add_convert_fusion
  46.9 1.5 copy.167
  48.7 40.6 %all-gather.8.cloned.1.call-done = bf16[2560,960]{1,0:T(8,128)(2,1)} async-done(((bf16[80,960]{1,0:T(8,128)(2,1)}), bf16[2560,960]{1,0:T(8,128)(2,1)}) %all-gather.8.cloned.1.call-update) | async-done | bytes 4915216 | tf_op jit(solution)/shard_map/all_gather | solution.py:143
  89.3 3.6 %convolution_bitcast_fusion = f32[144,960]{1,0:T(8,128)S(1)} fusion(bf16[32,80,960]{2,1,0:T(8,128)(2,1)} %bitcast.144, bf16[144,32,76]{2,0,1:T(8,128)(2,1)S(1)} %copy.167), kind=kOutput, calls=%fused_computation.6 | convolution fusion | flops 707788800 | bytes 6168576 | tf_op jit(solution)/shard_map/rsd,sdn->rn/dot_general | solution.py:156
  98.6 33.6 %all-gather.3 = bf16[32,76,192]{2,1,0:T(8,128)(2,1)S(1)} all-gather(bf16[1,76,192]{2,1,0:T(8,128)(2,1)S(1)} %bitcast.141), channel_id=1, replica_groups=mesh['cfg'=2,'seq'=32,'wgt'=8] {'seq'}, dimensions={0}, use_global_device_ids=true | all-gather | bytes 963072 | tf_op jit(solution)/shard_map/all_gather | solution.py:149
  135.6 34.0 %all-gather.10.cloned.1.call-done = bf16[9728,256]{1,0:T(8,128)(2,1)} async-done(((bf16[304,256]{1,0:T(8,128)(2,1)}), bf16[9728,256]{1,0:T(8,128)(2,1)}) %all-gather.10.cloned.1.call-update) | async-done | bytes 4980752 | tf_op jit(solution)/shard_map/all_gather | solution.py:191
  171.1 9.7 %shard_map.140 = bf16[4,32,256]{2,1,0:T(8,128)(2,1)} custom-call(bf16[4,32,256]{2,1,0:T(8,128)(2,1)} %pad.34.q_ref, bf16[32,304,256]{2,1,0:T(8,128)(2,1)} %bitcast.130, f32[4,512]{1,0:T(4,128)} %fusion.55.mask_ref), custom_call_target="tpu_custom_call" | custom-call | tf_op jit(solution)/shard_map/pallas_call | solution.py:87
  181.8 1.4 convolution_convert_fusion
  183.2 6.5 %all-to-all-start = ((bf16[8,16,2432]{2,1,0:T(8,128)(2,1)}), bf16[8,16,2432]{2,1,0:T(8,128)(2,1)S(1)}, u32[]{:S(2)}, u32[]{:S(2)}) async-start(bf16[8,16,2432]{2,1,0:T(8,128)(2,1)} %bitcast.25), calls=%async_computation | async-start | bytes 1245184 | tf_op jit(solution)/shard_map/all_to_all | solution.py:41
  189.7 1.2 reshape.364
  191.2 11.5 %all-to-all-done = bf16[8,16,2432]{2,1,0:T(8,128)(2,1)S(1)} async-done(((bf16[8,16,2432]{2,1,0:T(8,128)(2,1)}), bf16[8,16,2432]{2,1,0:T(8,128)(2,1)S(1)}, u32[]{:S(2)}, u32[]{:S(2)}) %all-to-all-start) | async-done | bytes 622624 | tf_op jit(solution)/shard_map/all_to_all | solution.py:41
  204.2 15.4 %all_to_all.20 = bf16[8,16,2432]{2,1,0:T(8,128)(2,1)S(1)} all-to-all(bf16[8,16,2432]{2,1,0:T(8,128)(2,1)S(1)} %broadcast_in_dim.8), channel_id=1, replica_groups=mesh['cfg'=2,'seq'=32,'wgt'=8] {'wgt'}, dimensions={0} | all-to-all | bytes 1245184 | tf_op jit(solution)/shard_map/all_to_all | solution.py:220
  219.6 3.5 %reshape_reshape.3 = bf16[128,32,76]{2,1,0:T(8,128)(2,1)S(1)} reshape(bf16[8,16,2432]{2,1,0:T(8,128)(2,1)S(1)} %all_to_all.20) | data formatting | bytes 1245184 | tf_op jit(solution)/shard_map/reshape;reshape | solution.py:230
  224.2 22.5 %all-gather.12.cloned.1.call-done = bf16[64,80,704]{2,1,0:T(8,128)(2,1)} async-done(((bf16[2,80,704]{2,1,0:T(8,128)(2,1)}), bf16[64,80,704]{2,1,0:T(8,128)(2,1)}) %all-gather.12.cloned.1.call-update) | async-done | bytes 7208976 | tf_op jit(solution)/shard_map/all_gather | solution.py:148
  246.7 8.2 %fusion = bf16[128,32,80]{0,2,1:T(8,128)(2,1)} fusion(bf16[32,2,80,704]{3,2,1,0:T(8,128)(2,1)} %bitcast.143, bf16[128,32,76]{0,2,1:T(8,128)(2,1)S(1)} %copy.160), kind=kOutput, calls=%fused_computation.1 | convolution fusion | flops 923557888 | bytes 8486912 | tf_op jit(solution)/shard_map/rf,sdf->rsd/dot_general | solution.py:237
  254.9 1.9 copy.163
  256.8 2.8 convert_element_type.180
  259.6 6.9 %all-to-all-start.2 = ((bf16[8,16,2432]{2,1,0:T(8,128)(2,1)}), bf16[8,16,2432]{2,1,0:T(8,128)(2,1)S(1)}, u32[]{:S(2)}, u32[]{:S(2)}) async-start(bf16[8,16,2432]{2,1,0:T(8,128)(2,1)} %convert_element_type.180), calls=%async_computation.2 | async-start | bytes 1245184 | tf_op jit(solution)/shard_map/all_to_all | solution.py:41
  266.8 12.7 %all-to-all-done.2 = bf16[8,16,2432]{2,1,0:T(8,128)(2,1)S(1)} async-done(((bf16[8,16,2432]{2,1,0:T(8,128)(2,1)}), bf16[8,16,2432]{2,1,0:T(8,128)(2,1)S(1)}, u32[]{:S(2)}, u32[]{:S(2)}) %all-to-all-start.2) | async-done | bytes 622624 | tf_op jit(solution)/shard_map/all_to_all | solution.py:41
  280.3 2.6 collective-permute-start
  283.0 2.8 collective-permute-done
  (166 shorter events, 25.6 us)
Async XLA Ops:
  7.2 272.9 %copy-start = (bf16[2432,64]{0,1:T(8,128)(2,1)S(1)}, bf16[2432,64]{0,1:T(8,128)(2,1)}, u32[]{:S(2)}) copy-start(bf16[2432,64]{0,1:T(8,128)(2,1)} %param.25) | copy-start | bytes 933892
  7.2 3.0 %copy-start.8 = (f32[1,4,10,2432]{3,1,2,0:T(4,128)S(1)}, f32[1,4,10,2432]{3,1,2,0:T(4,128)}, u32[]{:S(2)}) copy-start(f32[1,4,10,2432]{3,1,2,0:T(4,128)} %param.18) | copy-start | bytes 1167364
  7.2 82.1 %all-gather.8.cloned.1.call-start = ((), (), s32[]{:S(2)}) async-start(), calls=%async_computation.3 | async-start | bytes 5406720 | tf_op jit(solution)/shard_map/all_gather | solution.py:143
  10.2 159.4 %all-gather.10.cloned.1.call-start = ((), (), s32[]{:S(2)}) async-start(), calls=%async_computation.4 | async-start | bytes 5136384 | tf_op jit(solution)/shard_map/all_gather | solution.py:191
  25.0 2.1 copy-start.1
  31.8 2.2 copy-start.19
  36.0 3.2 %copy-start.5 = (bf16[1,16,2432]{2,1,0:T(8,128)(2,1)S(1)}, bf16[1,16,2432]{2,1,0:T(8,128)(2,1)}, u32[]{:S(2)}) copy-start(bf16[1,16,2432]{2,1,0:T(8,128)(2,1)} %param.15) | copy-start | bytes 233476
  43.7 1.9 copy-start.2
  43.7 2.1 copy-start.3
  43.7 2.4 copy-start.4
  46.9 1.6 copy-start.18
  92.9 0.8 copy-start.6
  93.8 0.9 slice-start
  95.8 1.9 copy-start.14
  95.8 1.9 copy-start.15
  96.3 2.3 copy-start.16
  97.7 149.0 %all-gather.12.cloned.1.call-start = ((), (), s32[]{:S(2)}) async-start(), calls=%async_computation.5 | async-start | bytes 8110080 | tf_op jit(solution)/shard_map/all_gather | solution.py:148
  132.7 2.1 copy-start.7
  183.2 19.5 %all-to-all-start = ((bf16[8,16,2432]{2,1,0:T(8,128)(2,1)}), bf16[8,16,2432]{2,1,0:T(8,128)(2,1)S(1)}, u32[]{:S(2)}, u32[]{:S(2)}) async-start(bf16[8,16,2432]{2,1,0:T(8,128)(2,1)} %bitcast.25), calls=%async_computation | async-start | bytes 1245184 | tf_op jit(solution)/shard_map/all_to_all | solution.py:41
  189.6 1.3 copy-start.13
  189.6 1.3 copy-start.12
  189.7 1.4 copy-start.11
  256.8 9.6 %copy-start.10 = (f32[4,2432]{1,0:T(4,128)S(1)}, f32[4,2432]{1,0:T(4,128)}, u32[]{:S(2)}) copy-start(f32[4,2432]{1,0:T(4,128)} %get-tuple-element.16) | copy-start | bytes 116740
  259.6 7.0 %copy-start.9 = (f32[4,2432]{1,0:T(4,128)S(1)}, f32[4,2432]{1,0:T(4,128)}, u32[]{:S(2)}) copy-start(f32[4,2432]{1,0:T(4,128)} %get-tuple-element.13) | copy-start | bytes 116740
  259.6 19.9 %all-to-all-start.2 = ((bf16[8,16,2432]{2,1,0:T(8,128)(2,1)}), bf16[8,16,2432]{2,1,0:T(8,128)(2,1)S(1)}, u32[]{:S(2)}, u32[]{:S(2)}) async-start(bf16[8,16,2432]{2,1,0:T(8,128)(2,1)} %convert_element_type.180), calls=%async_computation.2 | async-start | bytes 1245184 | tf_op jit(solution)/shard_map/all_to_all | solution.py:41
  266.7 16.2 %copy-start.20 = (s32[4]{0:T(128)S(1)}, s32[4]{0:T(128)}, u32[]{:S(2)}) copy-start(s32[4]{0:T(128)} %param.17) | copy-start | bytes 52
  266.7 19.1 %copy-start.17 = (f32[4,2,64]{2,1,0:T(2,128)S(1)}, f32[4,2,64]{2,1,0:T(2,128)}, u32[]{:S(2)}) copy-start(f32[4,2,64]{2,1,0:T(2,128)} %param.13) | copy-start | bytes 6148
  280.3 5.5 %collective-permute-start = (f32[4,2,64]{2,1,0:T(2,128)S(1)}, f32[4,2,64]{2,1,0:T(2,128)S(1)}, u32[]{:S(2)}, u32[]{:S(2)}) collective-permute-start(f32[4,2,64]{2,1,0:T(2,128)S(1)} %constant_dynamic-slice_fusion), channel_id=1, source_target_pairs={{0,256},{256,0},{1,257},{257,1},{2,258},{258,2},{3,259},{259,3},{4... | collective-permute-start | bytes 6152 | tf_op jit(solution)/shard_map/ppermute | solution.py:20
Sparse Core Ops, SparseCore 0:
  10.3 78.9 all-gather.7
  97.8 71.7 all-gather.9
  171.7 74.9 all-gather.11

commit v4 on v3

--- a/solution.py
+++ b/solution.py
@@ -35,6 +35,18 @@
 def sigma_of(index_row):
     time_left = 1.0 - index_row.astype(jnp.float32) / STEPS
     return flow_shift * time_left / (1.0 + (flow_shift - 1.0) * time_left)
+
+
+def permute_sum(partial, groups):
+    rows = partial.shape[0] // groups
+    chunks = partial.reshape(groups, rows, -1)
+    here = lax.axis_index("wgt")
+    total = lax.dynamic_index_in_dim(chunks, here, 0, keepdims=False).astype(jnp.float32)
+    for shift in range(1, groups):
+        sent = lax.dynamic_index_in_dim(chunks, (here + shift) % groups, 0, keepdims=False)
+        pairs = [(source, (source + shift) % groups) for source in range(groups)]
+        total = total + lax.ppermute(sent, "wgt", pairs).astype(jnp.float32)
+    return total
 
 
 def group_sum(partial, groups):
@@ -237,7 +249,7 @@
     contracted = jnp.einsum(
         "rf,sdf->rsd", expanded, mlp_full[:, 1], preferred_element_type=jnp.float32
     )[:, :, :block_rows].reshape(row_count, feat_width)
-    branch = group_sum(contracted.astype(jnp.bfloat16), wgt_size)
+    branch = permute_sum(contracted.astype(jnp.bfloat16), wgt_size)
     second = residual + modulate[:, 7] * branch.reshape(tokens_out, requests, feat_width)
     final_in = (layer_norm(second) * (1.0 + modulate[:, 9]) + modulate[:, 8]).astype(jnp.bfloat16)
     own_velocity = jnp.dot(

time: 294 us -> 305 us (1.037)
  starting transfers between devices: 16.1 us -> 41.2 us
  blocking collectives: 49 us -> 33.9 us
  waiting for transfers between devices: 124 us -> 128 us
    ppermute x0 -> x7, starting transfers between devices: none -> 27.9 us  [permute_sum(): total = total + lax.ppermute(sent, 'wgt', pairs).astype(jnp.float32)]
    all_to_all x1 -> x0, blocking collectives: 15.4 us -> none  [body(): lax.all_to_all(jnp.broadcast_to(branch_in.reshape(1, share_rows, feat_wid...]
    all_to_all x2 -> x1, waiting for transfers between devices: 24.2 us -> 12 us  [group_sum(): swapped = lax.all_to_all(partial, 'wgt', 0, 0, tiled=True)]
    all_to_all x0 -> x1, waiting for transfers between devices: none -> 11.6 us  [body(): lax.all_to_all(jnp.broadcast_to(branch_in.reshape(1, share_rows, feat_wid...]
    all_to_all x2 -> x1, starting transfers between devices: 13.3 us -> 6.95 us  [group_sum(): swapped = lax.all_to_all(partial, 'wgt', 0, 0, tiled=True)]
    ppermute x0 -> x7, waiting for transfers between devices: none -> 5.52 us  [permute_sum(): total = total + lax.ppermute(sent, 'wgt', pairs).astype(jnp.float32)]
    all_to_all x0 -> x1, starting transfers between devices: none -> 3.76 us  [body(): lax.all_to_all(jnp.broadcast_to(branch_in.reshape(1, share_rows, feat_wid...]
  transfers between devices with their start and end apart: 6 -> 13, of which waited for: 6 -> 8; matrix products, arithmetic and copies ran while one was open for 18% -> 17% of each run, Pallas kernels for 3% -> 3%
where the time goes in v4:
time: 305 us; the launch traced here: 304 us
  waiting for transfers between devices  128 us (42%)
  local copies, waits for them, and re-layouts  51.8 us (17%)
  starting transfers between devices  41.2 us (14%)
  blocking collectives  33.9 us (11%)
  between operations  14.8 us (5%)
  matrix products  12.9 us (4%)
  other arithmetic  12 us (4%)
  Pallas kernels  9.66 us (3%)
    all_gather x1, waiting for transfers between devices, body(): piece = lax.all_gather(all_weights, 'seq', axis=0, tiled=False)  40.2 us
    all_gather x1, blocking collectives, body(): out_full = lax.all_gather(out_weight, 'seq', axis=1, tiled=True)  33.9 us
    all_gather x1, waiting for transfers between devices, body(): shared_piece = lax.all_gather(shared, 'seq', axis=0, tiled=False)  33.7 us
    ppermute x7, starting transfers between devices, permute_sum(): total = total + lax.ppermute(sent, 'wgt', pairs).astype(jnp.float32)  27.9 us
    all_gather x1, waiting for transfers between devices, body(): mlp_full = lax.all_gather(mlp_local, 'seq', axis=0, tiled=False)  22.2 us
    all_to_all x1, waiting for transfers between devices, group_sum(): swapped = lax.all_to_all(partial, 'wgt', 0, 0, tiled=True)  12 us
    all_to_all x1, waiting for transfers between devices, body(): lax.all_to_all(jnp.broadcast_to(branch_in.reshape(1, share_rows, feat_wid...  11.6 us
    pallas_call x1, Pallas kernels, run(): pl.pallas_call(kernel, out_shape=jax.ShapeDtypeStruct(q.shape, jnp.bfloat...  9.66 us
  transfers between devices with their start and end apart: 13, of which 8 were waited for; matrix products, arithmetic and copies ran while one was open for 17% of the time, Pallas kernels for 3%

profile of v4, /device:TPU:32, one launch (start us, length us, event | category | flops | bytes accessed | tf_op | source)
XLA Modules:
  0.0 304.4 jit_solution(17847743375900669377)
XLA Ops:
  12.2 4.8 %mul.316 = f32[128,32,76]{2,1,0:T(8,128)S(1)} reshape(f32[32,4,2432]{2,1,0:T(4,128)} %mul.315) | data formatting | bytes 2490368 | tf_op jit(solution)/shard_map/mul | solution.py:135
  16.9 2.2 copy.140
  20.3 4.8 %add.310 = f32[128,32,76]{2,1,0:T(8,128)S(1)} reshape(f32[32,4,2432]{2,1,0:T(4,128)} %add.309) | data formatting | bytes 2490368 | tf_op jit(solution)/shard_map/add | solution.py:135
  25.1 2.1 copy.141
  27.2 3.5 %reshape.364 = f32[128,32,76]{2,1,0:T(8,128)S(1)} reshape(bf16[1,32,4,2432]{3,2,1,0:T(4,128)(2,1)S(1)} %copy-done.1) | data formatting | bytes 1867776 | tf_op jit(solution)/shard_map/convert_element_type | solution.py:134
  31.8 2.2 copy.139
  37.2 2.1 copy.144
  40.4 2.9 copy.142
  43.8 1.9 add_convert_fusion
  48.8 40.2 %all-gather.8.cloned.1.call-done = bf16[2560,960]{1,0:T(8,128)(2,1)} async-done(((bf16[80,960]{1,0:T(8,128)(2,1)}), bf16[2560,960]{1,0:T(8,128)(2,1)}) %all-gather.8.cloned.1.call-update) | async-done | bytes 4915216 | tf_op jit(solution)/shard_map/all_gather | solution.py:155
  89.0 3.6 %convolution_bitcast_fusion = f32[144,960]{1,0:T(8,128)S(1)} fusion(bf16[32,80,960]{2,1,0:T(8,128)(2,1)} %bitcast.162, bf16[144,32,76]{2,0,1:T(8,128)(2,1)S(1)} %copy.174), kind=kOutput, calls=%fused_computation.6 | convolution fusion | flops 707788800 | bytes 6168576 | tf_op jit(solution)/shard_map/rsd,sdn->rn/dot_general | solution.py:168
  98.3 33.9 %all-gather.3 = bf16[32,76,192]{2,1,0:T(8,128)(2,1)S(1)} all-gather(bf16[1,76,192]{2,1,0:T(8,128)(2,1)S(1)} %bitcast.159), channel_id=1, replica_groups=mesh['cfg'=2,'seq'=32,'wgt'=8] {'seq'}, dimensions={0}, use_global_device_ids=true | all-gather | bytes 963072 | tf_op jit(solution)/shard_map/all_gather | solution.py:161
  135.6 33.7 %all-gather.10.cloned.1.call-done = bf16[9728,256]{1,0:T(8,128)(2,1)} async-done(((bf16[304,256]{1,0:T(8,128)(2,1)}), bf16[9728,256]{1,0:T(8,128)(2,1)}) %all-gather.10.cloned.1.call-update) | async-done | bytes 4980752 | tf_op jit(solution)/shard_map/all_gather | solution.py:203
  170.9 9.7 %shard_map.140 = bf16[4,32,256]{2,1,0:T(8,128)(2,1)} custom-call(bf16[4,32,256]{2,1,0:T(8,128)(2,1)} %pad.34.q_ref, bf16[32,304,256]{2,1,0:T(8,128)(2,1)} %bitcast.148, f32[4,512]{1,0:T(4,128)} %fusion.63.mask_ref), custom_call_target="tpu_custom_call" | custom-call | tf_op jit(solution)/shard_map/pallas_call | solution.py:99
  182.9 7.0 %all-to-all-start = ((bf16[8,16,2432]{2,1,0:T(8,128)(2,1)}), bf16[8,16,2432]{2,1,0:T(8,128)(2,1)S(1)}, u32[]{:S(2)}, u32[]{:S(2)}) async-start(bf16[8,16,2432]{2,1,0:T(8,128)(2,1)} %bitcast.25), calls=%async_computation | async-start | bytes 1245184 | tf_op jit(solution)/shard_map/all_to_all | solution.py:53
  191.0 12.0 %all-to-all-done = bf16[8,16,2432]{2,1,0:T(8,128)(2,1)S(1)} async-done(((bf16[8,16,2432]{2,1,0:T(8,128)(2,1)}), bf16[8,16,2432]{2,1,0:T(8,128)(2,1)S(1)}, u32[]{:S(2)}, u32[]{:S(2)}) %all-to-all-start) | async-done | bytes 622624 | tf_op jit(solution)/shard_map/all_to_all | solution.py:53
  204.4 3.8 %all-to-all-start.1 = ((bf16[8,16,2432]{2,1,0:T(8,128)(2,1)}), bf16[8,16,2432]{2,1,0:T(8,128)(2,1)S(1)}, u32[]{:S(2)}, u32[]{:S(2)}) async-start(bf16[8,16,2432]{2,1,0:T(8,128)(2,1)} %broadcast_in_dim.8), calls=%async_computation.1 | async-start | bytes 1245184 | tf_op jit(solution)/shard_map/all_to_all | solution.py:232
  208.3 11.6 %all-to-all-done.1 = bf16[8,16,2432]{2,1,0:T(8,128)(2,1)S(1)} async-done(((bf16[8,16,2432]{2,1,0:T(8,128)(2,1)}), bf16[8,16,2432]{2,1,0:T(8,128)(2,1)S(1)}, u32[]{:S(2)}, u32[]{:S(2)}) %all-to-all-start.1) | async-done | bytes 622624 | tf_op jit(solution)/shard_map/all_to_all | solution.py:232
  219.9 3.5 %reshape_reshape.3 = bf16[128,32,76]{2,1,0:T(8,128)(2,1)S(1)} reshape(bf16[8,16,2432]{2,1,0:T(8,128)(2,1)S(1)} %all-to-all-done.1) | data formatting | bytes 1245184 | tf_op jit(solution)/shard_map/reshape;reshape | solution.py:242
  224.5 22.2 %all-gather.12.cloned.1.call-done = bf16[64,80,704]{2,1,0:T(8,128)(2,1)} async-done(((bf16[2,80,704]{2,1,0:T(8,128)(2,1)}), bf16[64,80,704]{2,1,0:T(8,128)(2,1)}) %all-gather.12.cloned.1.call-update) | async-done | bytes 7208976 | tf_op jit(solution)/shard_map/all_gather | solution.py:160
  246.7 7.3 %fusion = bf16[128,32,80]{0,2,1:T(8,128)(2,1)S(1)} fusion(bf16[32,2,80,704]{3,2,1,0:T(8,128)(2,1)} %bitcast.161, bf16[128,32,76]{0,2,1:T(8,128)(2,1)S(1)} %copy.167), kind=kOutput, calls=%fused_computation.1 | convolution fusion | flops 923557888 | bytes 8486912 | tf_op jit(solution)/shard_map/rf,sdf->rsd/dot_general | solution.py:249
  255.0 1.9 convert_element_type.204
  257.1 4.9 %collective-permute-start = (bf16[16,2432]{1,0:T(8,128)(2,1)S(1)}, bf16[16,2432]{1,0:T(8,128)(2,1)S(1)}, u32[]{:S(2)}, u32[]{:S(2)}) collective-permute-start(bf16[16,2432]{1,0:T(8,128)(2,1)S(1)} %get-tuple-element.8), channel_id=1, source_target_pairs={{0,1},{1,2},{2,3},{3,4},{4,5},{5,6},{6,7},{7,0},{8,9},{9,10},{10,1... | collective-permute-start | bytes 233480 | tf_op jit(solution)/shard_map/ppermute | solution.py:48
  262.0 3.4 %collective-permute-start.1 = (bf16[16,2432]{1,0:T(8,128)(2,1)S(1)}, bf16[16,2432]{1,0:T(8,128)(2,1)S(1)}, u32[]{:S(2)}, u32[]{:S(2)}) collective-permute-start(bf16[16,2432]{1,0:T(8,128)(2,1)S(1)} %get-tuple-element.14), channel_id=1, source_target_pairs={{0,2},{1,3},{2,4},{3,5},{4,6},{5,7},{6,0},{7,1},{8,10},{9,11},{10,... | collective-permute-start | bytes 233480 | tf_op jit(solution)/shard_map/ppermute | solution.py:48
  265.4 3.8 %collective-permute-start.2 = (bf16[16,2432]{1,0:T(8,128)(2,1)S(1)}, bf16[16,2432]{1,0:T(8,128)(2,1)S(1)}, u32[]{:S(2)}, u32[]{:S(2)}) collective-permute-start(bf16[16,2432]{1,0:T(8,128)(2,1)S(1)} %get-tuple-element.13), channel_id=1, source_target_pairs={{0,3},{1,4},{2,5},{3,6},{4,7},{5,0},{6,1},{7,2},{8,11},{9,12},{10,... | collective-permute-start | bytes 233480 | tf_op jit(solution)/shard_map/ppermute | solution.py:48
  269.1 4.2 %collective-permute-start.3 = (bf16[16,2432]{1,0:T(8,128)(2,1)S(1)}, bf16[16,2432]{1,0:T(8,128)(2,1)S(1)}, u32[]{:S(2)}, u32[]{:S(2)}) collective-permute-start(bf16[16,2432]{1,0:T(8,128)(2,1)S(1)} %get-tuple-element.12), channel_id=1, source_target_pairs={{0,4},{1,5},{2,6},{3,7},{4,0},{5,1},{6,2},{7,3},{8,12},{9,13},{10,... | collective-permute-start | bytes 233480 | tf_op jit(solution)/shard_map/ppermute | solution.py:48
  273.3 6.4 %collective-permute-start.4 = (bf16[16,2432]{1,0:T(8,128)(2,1)S(1)}, bf16[16,2432]{1,0:T(8,128)(2,1)S(1)}, u32[]{:S(2)}, u32[]{:S(2)}) collective-permute-start(bf16[16,2432]{1,0:T(8,128)(2,1)S(1)} %get-tuple-element.11), channel_id=1, source_target_pairs={{0,5},{1,6},{2,7},{3,0},{4,1},{5,2},{6,3},{7,4},{8,13},{9,14},{10,... | collective-permute-start | bytes 233480 | tf_op jit(solution)/shard_map/ppermute | solution.py:48
  279.8 3.3 %collective-permute-start.5 = (bf16[16,2432]{1,0:T(8,128)(2,1)S(1)}, bf16[16,2432]{1,0:T(8,128)(2,1)S(1)}, u32[]{:S(2)}, u32[]{:S(2)}) collective-permute-start(bf16[16,2432]{1,0:T(8,128)(2,1)S(1)} %get-tuple-element.10), channel_id=1, source_target_pairs={{0,6},{1,7},{2,0},{3,1},{4,2},{5,3},{6,4},{7,5},{8,14},{9,15},{10,... | collective-permute-start | bytes 233480 | tf_op jit(solution)/shard_map/ppermute | solution.py:48
  283.1 1.9 collective-permute-start.6
  286.1 4.9 %collective-permute-done.6 = bf16[16,2432]{1,0:T(8,128)(2,1)S(1)} collective-permute-done((bf16[16,2432]{1,0:T(8,128)(2,1)S(1)}, bf16[16,2432]{1,0:T(8,128)(2,1)S(1)}, u32[]{:S(2)}, u32[]{:S(2)}) %collective-permute-start.6) | collective-permute-done | bytes 77856 | tf_op jit(solution)/shard_map/ppermute | solution.py:48
  291.7 2.5 collective-permute-start.7
  294.3 2.9 collective-permute-done.7
  (179 shorter events, 34.7 us)
Async XLA Ops:
  7.2 284.4 %copy-start = (bf16[2432,64]{0,1:T(8,128)(2,1)S(1)}, bf16[2432,64]{0,1:T(8,128)(2,1)}, u32[]{:S(2)}) copy-start(bf16[2432,64]{0,1:T(8,128)(2,1)} %param.25) | copy-start | bytes 933892
  7.2 3.0 copy-start.8
  7.2 81.8 %all-gather.8.cloned.1.call-start = ((), (), s32[]{:S(2)}) async-start(), calls=%async_computation.2 | async-start | bytes 5406720 | tf_op jit(solution)/shard_map/all_gather | solution.py:155
  10.2 159.1 %all-gather.10.cloned.1.call-start = ((), (), s32[]{:S(2)}) async-start(), calls=%async_computation.3 | async-start | bytes 5136384 | tf_op jit(solution)/shard_map/all_gather | solution.py:203
  25.1 2.1 copy-start.1
  31.8 2.2 copy-start.19
  36.0 3.3 %copy-start.5 = (bf16[1,16,2432]{2,1,0:T(8,128)(2,1)S(1)}, bf16[1,16,2432]{2,1,0:T(8,128)(2,1)}, u32[]{:S(2)}) copy-start(bf16[1,16,2432]{2,1,0:T(8,128)(2,1)} %param.15) | copy-start | bytes 233476
  43.7 1.9 copy-start.2
  43.8 2.1 copy-start.3
  43.8 2.4 copy-start.4
  47.0 1.6 copy-start.18
  93.4 0.9 slice-start
  95.5 1.9 copy-start.14
  95.5 1.9 copy-start.15
  95.9 2.3 copy-start.16
  97.3 149.4 %all-gather.12.cloned.1.call-start = ((), (), s32[]{:S(2)}) async-start(), calls=%async_computation.4 | async-start | bytes 8110080 | tf_op jit(solution)/shard_map/all_gather | solution.py:160
  132.7 2.1 copy-start.7
  182.9 20.0 %all-to-all-start = ((bf16[8,16,2432]{2,1,0:T(8,128)(2,1)}), bf16[8,16,2432]{2,1,0:T(8,128)(2,1)S(1)}, u32[]{:S(2)}, u32[]{:S(2)}) async-start(bf16[8,16,2432]{2,1,0:T(8,128)(2,1)} %bitcast.25), calls=%async_computation | async-start | bytes 1245184 | tf_op jit(solution)/shard_map/all_to_all | solution.py:53
  189.9 0.9 copy-start.11
  204.4 15.5 %all-to-all-start.1 = ((bf16[8,16,2432]{2,1,0:T(8,128)(2,1)}), bf16[8,16,2432]{2,1,0:T(8,128)(2,1)S(1)}, u32[]{:S(2)}, u32[]{:S(2)}) async-start(bf16[8,16,2432]{2,1,0:T(8,128)(2,1)} %broadcast_in_dim.8), calls=%async_computation.1 | async-start | bytes 1245184 | tf_op jit(solution)/shard_map/all_to_all | solution.py:232
  255.0 30.0 %copy-start.10 = (f32[4,2432]{1,0:T(4,128)S(1)}, f32[4,2432]{1,0:T(4,128)}, u32[]{:S(2)}) copy-start(f32[4,2432]{1,0:T(4,128)} %get-tuple-element.23) | copy-start | bytes 116740
  255.0 30.1 %copy-start.9 = (f32[4,2432]{1,0:T(4,128)S(1)}, f32[4,2432]{1,0:T(4,128)}, u32[]{:S(2)}) copy-start(f32[4,2432]{1,0:T(4,128)} %get-tuple-element.20) | copy-start | bytes 116740
  257.1 22.7 %collective-permute-start = (bf16[16,2432]{1,0:T(8,128)(2,1)S(1)}, bf16[16,2432]{1,0:T(8,128)(2,1)S(1)}, u32[]{:S(2)}, u32[]{:S(2)}) collective-permute-start(bf16[16,2432]{1,0:T(8,128)(2,1)S(1)} %get-tuple-element.8), channel_id=1, source_target_pairs={{0,1},{1,2},{2,3},{3,4},{4,5},{5,6},{6,7},{7,0},{8,9},{9,10},{10,1... | collective-permute-start | bytes 233480 | tf_op jit(solution)/shard_map/ppermute | solution.py:48
  262.0 21.2 %collective-permute-start.1 = (bf16[16,2432]{1,0:T(8,128)(2,1)S(1)}, bf16[16,2432]{1,0:T(8,128)(2,1)S(1)}, u32[]{:S(2)}, u32[]{:S(2)}) collective-permute-start(bf16[16,2432]{1,0:T(8,128)(2,1)S(1)} %get-tuple-element.14), channel_id=1, source_target_pairs={{0,2},{1,3},{2,4},{3,5},{4,6},{5,7},{6,0},{7,1},{8,10},{9,11},{10,... | collective-permute-start | bytes 233480 | tf_op jit(solution)/shard_map/ppermute | solution.py:48
  265.4 20.0 %collective-permute-start.2 = (bf16[16,2432]{1,0:T(8,128)(2,1)S(1)}, bf16[16,2432]{1,0:T(8,128)(2,1)S(1)}, u32[]{:S(2)}, u32[]{:S(2)}) collective-permute-start(bf16[16,2432]{1,0:T(8,128)(2,1)S(1)} %get-tuple-element.13), channel_id=1, source_target_pairs={{0,3},{1,4},{2,5},{3,6},{4,7},{5,0},{6,1},{7,2},{8,11},{9,12},{10,... | collective-permute-start | bytes 233480 | tf_op jit(solution)/shard_map/ppermute | solution.py:48
  269.1 16.3 %collective-permute-start.3 = (bf16[16,2432]{1,0:T(8,128)(2,1)S(1)}, bf16[16,2432]{1,0:T(8,128)(2,1)S(1)}, u32[]{:S(2)}, u32[]{:S(2)}) collective-permute-start(bf16[16,2432]{1,0:T(8,128)(2,1)S(1)} %get-tuple-element.12), channel_id=1, source_target_pairs={{0,4},{1,5},{2,6},{3,7},{4,0},{5,1},{6,2},{7,3},{8,12},{9,13},{10,... | collective-permute-start | bytes 233480 | tf_op jit(solution)/shard_map/ppermute | solution.py:48
  273.3 12.1 %collective-permute-start.4 = (bf16[16,2432]{1,0:T(8,128)(2,1)S(1)}, bf16[16,2432]{1,0:T(8,128)(2,1)S(1)}, u32[]{:S(2)}, u32[]{:S(2)}) collective-permute-start(bf16[16,2432]{1,0:T(8,128)(2,1)S(1)} %get-tuple-element.11), channel_id=1, source_target_pairs={{0,5},{1,6},{2,7},{3,0},{4,1},{5,2},{6,3},{7,4},{8,13},{9,14},{10,... | collective-permute-start | bytes 233480 | tf_op jit(solution)/shard_map/ppermute | solution.py:48
  279.8 6.3 %collective-permute-start.5 = (bf16[16,2432]{1,0:T(8,128)(2,1)S(1)}, bf16[16,2432]{1,0:T(8,128)(2,1)S(1)}, u32[]{:S(2)}, u32[]{:S(2)}) collective-permute-start(bf16[16,2432]{1,0:T(8,128)(2,1)S(1)} %get-tuple-element.10), channel_id=1, source_target_pairs={{0,6},{1,7},{2,0},{3,1},{4,2},{5,3},{6,4},{7,5},{8,14},{9,15},{10,... | collective-permute-start | bytes 233480 | tf_op jit(solution)/shard_map/ppermute | solution.py:48
  283.1 7.8 %collective-permute-start.6 = (bf16[16,2432]{1,0:T(8,128)(2,1)S(1)}, bf16[16,2432]{1,0:T(8,128)(2,1)S(1)}, u32[]{:S(2)}, u32[]{:S(2)}) collective-permute-start(bf16[16,2432]{1,0:T(8,128)(2,1)S(1)} %get-tuple-element.9), channel_id=1, source_target_pairs={{0,7},{1,0},{2,1},{3,2},{4,3},{5,4},{6,5},{7,6},{8,15},{9,8},{10,9... | collective-permute-start | bytes 233480 | tf_op jit(solution)/shard_map/ppermute | solution.py:48
  285.4 8.9 %copy-start.20 = (s32[4]{0:T(128)S(1)}, s32[4]{0:T(128)}, u32[]{:S(2)}) copy-start(s32[4]{0:T(128)} %param.17) | copy-start | bytes 52
  285.4 11.9 %copy-start.17 = (f32[4,2,64]{2,1,0:T(2,128)S(1)}, f32[4,2,64]{2,1,0:T(2,128)}, u32[]{:S(2)}) copy-start(f32[4,2,64]{2,1,0:T(2,128)} %param.13) | copy-start | bytes 6148
  291.7 5.5 %collective-permute-start.7 = (f32[4,2,64]{2,1,0:T(2,128)S(1)}, f32[4,2,64]{2,1,0:T(2,128)S(1)}, u32[]{:S(2)}, u32[]{:S(2)}) collective-permute-start(f32[4,2,64]{2,1,0:T(2,128)S(1)} %constant_dynamic-slice_fusion), channel_id=1, source_target_pairs={{0,256},{256,0},{1,257},{257,1},{2,258},{258,2},{3,259},{259,3},{4... | collective-permute-start | bytes 6152 | tf_op jit(solution)/shard_map/ppermute | solution.py:20
  (3 other events, 2.4 us)
Sparse Core Ops, SparseCore 0:
  10.3 78.6 all-gather.7
  97.5 71.8 all-gather.9
  171.4 75.2 all-gather.11

commit v5 on v3

--- a/solution.py
+++ b/solution.py
@@ -236,8 +236,11 @@
     expanded = jax.nn.gelu(expanded, approximate=True).astype(jnp.bfloat16)
     contracted = jnp.einsum(
         "rf,sdf->rsd", expanded, mlp_full[:, 1], preferred_element_type=jnp.float32
-    )[:, :, :block_rows].reshape(row_count, feat_width)
-    branch = group_sum(contracted.astype(jnp.bfloat16), wgt_size)
+    ).astype(jnp.bfloat16)
+    branch = group_sum(contracted.reshape(row_count, seq_size * padded_rows), wgt_size)
+    branch = branch.reshape(share_rows, seq_size, padded_rows)[:, :, :block_rows].reshape(
+        share_rows, feat_width
+    )
     second = residual + modulate[:, 7] * branch.reshape(tokens_out, requests, feat_width)
     final_in = (layer_norm(second) * (1.0 + modulate[:, 9]) + modulate[:, 8]).astype(jnp.bfloat16)
     own_velocity = jnp.dot(

time: 294 us -> 295 us (level)
  no operation moved by 1% of the time
where the time goes in v5:
time: 295 us; the launch traced here: 294 us
  waiting for transfers between devices  124 us (42%)
  local copies, waits for them, and re-layouts  53.4 us (18%)
  blocking collectives  49 us (17%)
  starting transfers between devices  16.1 us (5%)
  between operations  14.6 us (5%)
  matrix products  13.8 us (5%)
  other arithmetic  12.9 us (4%)
  Pallas kernels  9.68 us (3%)
    all_gather x1, waiting for transfers between devices, body(): piece = lax.all_gather(all_weights, 'seq', axis=0, tiled=False)  40.6 us
    all_gather x1, waiting for transfers between devices, body(): shared_piece = lax.all_gather(shared, 'seq', axis=0, tiled=False)  34 us
    all_gather x1, blocking collectives, body(): out_full = lax.all_gather(out_weight, 'seq', axis=1, tiled=True)  33.6 us
    all_to_all x2, waiting for transfers between devices, group_sum(): swapped = lax.all_to_all(partial, 'wgt', 0, 0, tiled=True)  24.6 us
    all_gather x1, waiting for transfers between devices, body(): mlp_full = lax.all_gather(mlp_local, 'seq', axis=0, tiled=False)  22.5 us
    all_to_all x1, blocking collectives, body(): lax.all_to_all(jnp.broadcast_to(branch_in.reshape(1, share_rows, feat_wid...  15.4 us
    all_to_all x2, starting transfers between devices, group_sum(): swapped = lax.all_to_all(partial, 'wgt', 0, 0, tiled=True)  13.3 us
    pallas_call x1, Pallas kernels, run(): pl.pallas_call(kernel, out_shape=jax.ShapeDtypeStruct(q.shape, jnp.bfloat...  9.68 us
  transfers between devices with their start and end apart: 6, of which 6 were waited for; matrix products, arithmetic and copies ran while one was open for 18% of the time, Pallas kernels for 3%

profile of v5, /device:TPU:32, one launch (start us, length us, event | category | flops | bytes accessed | tf_op | source)
XLA Modules:
  0.0 293.8 jit_solution(10107652534281435076)
XLA Ops:
  10.9 1.2 mul.315
  12.1 4.8 %mul.316 = f32[128,32,76]{2,1,0:T(8,128)S(1)} reshape(f32[32,4,2432]{2,1,0:T(4,128)} %mul.315) | data formatting | bytes 2490368 | tf_op jit(solution)/shard_map/mul | solution.py:123
  16.9 2.2 copy.133
  19.1 1.2 add.220
  20.3 4.8 %add.221 = f32[128,32,76]{2,1,0:T(8,128)S(1)} reshape(f32[32,4,2432]{2,1,0:T(4,128)} %add.220) | data formatting | bytes 2490368 | tf_op jit(solution)/shard_map/add | solution.py:123
  25.1 2.1 copy.134
  27.2 3.5 %reshape.370 = f32[128,32,76]{2,1,0:T(8,128)S(1)} reshape(bf16[1,32,4,2432]{3,2,1,0:T(4,128)(2,1)S(1)} %copy-done.1) | data formatting | bytes 1867776 | tf_op jit(solution)/shard_map/convert_element_type | solution.py:122
  31.8 2.2 copy.132
  34.8 1.2 copy.136
  37.1 2.1 copy.137
  40.4 3.0 %copy.135 = f32[16,32,76]{0,1,2:T(8,128)} copy(f32[16,32,76]{2,1,0:T(8,128)} %reshape.371) | data formatting | bytes 311296 | tf_op jit(solution)/shard_map/convert_element_type | solution.py:134
  43.7 1.9 add_convert_fusion
  46.9 1.5 copy.167
  48.7 40.6 %all-gather.8.cloned.1.call-done = bf16[2560,960]{1,0:T(8,128)(2,1)} async-done(((bf16[80,960]{1,0:T(8,128)(2,1)}), bf16[2560,960]{1,0:T(8,128)(2,1)}) %all-gather.8.cloned.1.call-update) | async-done | bytes 4915216 | tf_op jit(solution)/shard_map/all_gather | solution.py:143
  89.3 3.6 %convolution_bitcast_fusion = f32[144,960]{1,0:T(8,128)S(1)} fusion(bf16[32,80,960]{2,1,0:T(8,128)(2,1)} %bitcast.146, bf16[144,32,76]{2,0,1:T(8,128)(2,1)S(1)} %copy.167), kind=kOutput, calls=%fused_computation.7 | convolution fusion | flops 707788800 | bytes 6168576 | tf_op jit(solution)/shard_map/rsd,sdn->rn/dot_general | solution.py:156
  98.6 33.6 %all-gather.3 = bf16[32,76,192]{2,1,0:T(8,128)(2,1)S(1)} all-gather(bf16[1,76,192]{2,1,0:T(8,128)(2,1)S(1)} %bitcast.143), channel_id=1, replica_groups=mesh['cfg'=2,'seq'=32,'wgt'=8] {'seq'}, dimensions={0}, use_global_device_ids=true | all-gather | bytes 963072 | tf_op jit(solution)/shard_map/all_gather | solution.py:149
  135.6 34.0 %all-gather.10.cloned.1.call-done = bf16[9728,256]{1,0:T(8,128)(2,1)} async-done(((bf16[304,256]{1,0:T(8,128)(2,1)}), bf16[9728,256]{1,0:T(8,128)(2,1)}) %all-gather.10.cloned.1.call-update) | async-done | bytes 4980752 | tf_op jit(solution)/shard_map/all_gather | solution.py:191
  171.1 9.7 %shard_map.140 = bf16[4,32,256]{2,1,0:T(8,128)(2,1)} custom-call(bf16[4,32,256]{2,1,0:T(8,128)(2,1)} %pad.34.q_ref, bf16[32,304,256]{2,1,0:T(8,128)(2,1)} %bitcast.132, f32[4,512]{1,0:T(4,128)} %fusion.56.mask_ref), custom_call_target="tpu_custom_call" | custom-call | tf_op jit(solution)/shard_map/pallas_call | solution.py:87
  181.8 1.4 convolution_convert_fusion
  183.2 6.5 %all-to-all-start = ((bf16[8,16,2432]{2,1,0:T(8,128)(2,1)}), bf16[8,16,2432]{2,1,0:T(8,128)(2,1)S(1)}, u32[]{:S(2)}, u32[]{:S(2)}) async-start(bf16[8,16,2432]{2,1,0:T(8,128)(2,1)} %bitcast.25), calls=%async_computation | async-start | bytes 1245184 | tf_op jit(solution)/shard_map/all_to_all | solution.py:41
  189.7 1.2 reshape.369
  191.2 11.5 %all-to-all-done = bf16[8,16,2432]{2,1,0:T(8,128)(2,1)S(1)} async-done(((bf16[8,16,2432]{2,1,0:T(8,128)(2,1)}), bf16[8,16,2432]{2,1,0:T(8,128)(2,1)S(1)}, u32[]{:S(2)}, u32[]{:S(2)}) %all-to-all-start) | async-done | bytes 622624 | tf_op jit(solution)/shard_map/all_to_all | solution.py:41
  204.2 15.4 %all_to_all.23 = bf16[8,16,2432]{2,1,0:T(8,128)(2,1)S(1)} all-to-all(bf16[8,16,2432]{2,1,0:T(8,128)(2,1)S(1)} %broadcast_in_dim.8), channel_id=1, replica_groups=mesh['cfg'=2,'seq'=32,'wgt'=8] {'wgt'}, dimensions={0} | all-to-all | bytes 1245184 | tf_op jit(solution)/shard_map/all_to_all | solution.py:220
  219.6 3.5 %reshape_reshape.6 = bf16[128,32,76]{2,1,0:T(8,128)(2,1)S(1)} reshape(bf16[8,16,2432]{2,1,0:T(8,128)(2,1)S(1)} %all_to_all.23) | data formatting | bytes 1245184 | tf_op jit(solution)/shard_map/reshape;reshape | solution.py:230
  224.2 22.5 %all-gather.12.cloned.1.call-done = bf16[64,80,704]{2,1,0:T(8,128)(2,1)} async-done(((bf16[2,80,704]{2,1,0:T(8,128)(2,1)}), bf16[64,80,704]{2,1,0:T(8,128)(2,1)}) %all-gather.12.cloned.1.call-update) | async-done | bytes 7208976 | tf_op jit(solution)/shard_map/all_gather | solution.py:148
  246.7 8.2 %fusion.2 = bf16[128,32,80]{0,2,1:T(8,128)(2,1)} fusion(bf16[32,2,80,704]{3,2,1,0:T(8,128)(2,1)} %bitcast.145, bf16[128,32,76]{0,2,1:T(8,128)(2,1)S(1)} %copy.160), kind=kOutput, calls=%fused_computation.5 | convolution fusion | flops 923885568 | bytes 8486912 | tf_op jit(solution)/shard_map/rf,sdf->rsd/dot_general | solution.py:237
  254.9 1.9 copy.163
  256.7 2.9 all_to_all.18
  259.7 6.9 %all-to-all-start.2 = ((bf16[8,16,2560]{2,1,0:T(8,128)(2,1)}), bf16[8,16,2560]{2,1,0:T(8,128)(2,1)S(1)}, u32[]{:S(2)}, u32[]{:S(2)}) async-start(bf16[8,16,2560]{2,1,0:T(8,128)(2,1)} %all_to_all.18), calls=%async_computation.2 | async-start | bytes 1310720 | tf_op jit(solution)/shard_map/all_to_all | solution.py:41
  266.8 13.1 %all-to-all-done.2 = bf16[8,16,2560]{2,1,0:T(8,128)(2,1)S(1)} async-done(((bf16[8,16,2560]{2,1,0:T(8,128)(2,1)}), bf16[8,16,2560]{2,1,0:T(8,128)(2,1)S(1)}, u32[]{:S(2)}, u32[]{:S(2)}) %all-to-all-start.2) | async-done | bytes 655392 | tf_op jit(solution)/shard_map/all_to_all | solution.py:41
  281.1 2.6 collective-permute-start
  283.8 2.8 collective-permute-done
  (168 shorter events, 26.0 us)
Async XLA Ops:
  7.2 273.7 %copy-start = (bf16[2432,64]{0,1:T(8,128)(2,1)S(1)}, bf16[2432,64]{0,1:T(8,128)(2,1)}, u32[]{:S(2)}) copy-start(bf16[2432,64]{0,1:T(8,128)(2,1)} %param.25) | copy-start | bytes 933892
  7.2 3.0 %copy-start.8 = (f32[1,4,10,2432]{3,1,2,0:T(4,128)S(1)}, f32[1,4,10,2432]{3,1,2,0:T(4,128)}, u32[]{:S(2)}) copy-start(f32[1,4,10,2432]{3,1,2,0:T(4,128)} %param.18) | copy-start | bytes 1167364
  7.2 82.1 %all-gather.8.cloned.1.call-start = ((), (), s32[]{:S(2)}) async-start(), calls=%async_computation.3 | async-start | bytes 5406720 | tf_op jit(solution)/shard_map/all_gather | solution.py:143
  10.2 159.4 %all-gather.10.cloned.1.call-start = ((), (), s32[]{:S(2)}) async-start(), calls=%async_computation.4 | async-start | bytes 5136384 | tf_op jit(solution)/shard_map/all_gather | solution.py:191
  25.0 2.1 copy-start.1
  31.8 2.2 copy-start.19
  36.0 3.2 %copy-start.5 = (bf16[1,16,2432]{2,1,0:T(8,128)(2,1)S(1)}, bf16[1,16,2432]{2,1,0:T(8,128)(2,1)}, u32[]{:S(2)}) copy-start(bf16[1,16,2432]{2,1,0:T(8,128)(2,1)} %param.15) | copy-start | bytes 233476
  43.7 1.9 copy-start.2
  43.7 2.1 copy-start.3
  43.7 2.4 copy-start.4
  46.9 1.6 copy-start.18
  92.9 0.8 copy-start.6
  93.8 0.9 slice-start
  95.8 1.9 copy-start.14
  95.8 1.9 copy-start.15
  96.3 2.3 copy-start.16
  97.7 149.0 %all-gather.12.cloned.1.call-start = ((), (), s32[]{:S(2)}) async-start(), calls=%async_computation.5 | async-start | bytes 8110080 | tf_op jit(solution)/shard_map/all_gather | solution.py:148
  132.7 2.1 copy-start.7
  183.2 19.5 %all-to-all-start = ((bf16[8,16,2432]{2,1,0:T(8,128)(2,1)}), bf16[8,16,2432]{2,1,0:T(8,128)(2,1)S(1)}, u32[]{:S(2)}, u32[]{:S(2)}) async-start(bf16[8,16,2432]{2,1,0:T(8,128)(2,1)} %bitcast.25), calls=%async_computation | async-start | bytes 1245184 | tf_op jit(solution)/shard_map/all_to_all | solution.py:41
  189.6 1.3 copy-start.13
  189.6 1.3 copy-start.12
  189.7 1.4 copy-start.11
  256.7 9.8 %copy-start.10 = (f32[4,2432]{1,0:T(4,128)S(1)}, f32[4,2432]{1,0:T(4,128)}, u32[]{:S(2)}) copy-start(f32[4,2432]{1,0:T(4,128)} %get-tuple-element.16) | copy-start | bytes 116740
  259.7 7.0 %copy-start.9 = (f32[4,2432]{1,0:T(4,128)S(1)}, f32[4,2432]{1,0:T(4,128)}, u32[]{:S(2)}) copy-start(f32[4,2432]{1,0:T(4,128)} %get-tuple-element.13) | copy-start | bytes 116740
  259.7 20.2 %all-to-all-start.2 = ((bf16[8,16,2560]{2,1,0:T(8,128)(2,1)}), bf16[8,16,2560]{2,1,0:T(8,128)(2,1)S(1)}, u32[]{:S(2)}, u32[]{:S(2)}) async-start(bf16[8,16,2560]{2,1,0:T(8,128)(2,1)} %all_to_all.18), calls=%async_computation.2 | async-start | bytes 1310720 | tf_op jit(solution)/shard_map/all_to_all | solution.py:41
  280.2 3.6 %copy-start.20 = (s32[4]{0:T(128)S(1)}, s32[4]{0:T(128)}, u32[]{:S(2)}) copy-start(s32[4]{0:T(128)} %param.17) | copy-start | bytes 52
  280.2 6.4 %copy-start.17 = (f32[4,2,64]{2,1,0:T(2,128)S(1)}, f32[4,2,64]{2,1,0:T(2,128)}, u32[]{:S(2)}) copy-start(f32[4,2,64]{2,1,0:T(2,128)} %param.13) | copy-start | bytes 6148
  281.1 5.5 %collective-permute-start = (f32[4,2,64]{2,1,0:T(2,128)S(1)}, f32[4,2,64]{2,1,0:T(2,128)S(1)}, u32[]{:S(2)}, u32[]{:S(2)}) collective-permute-start(f32[4,2,64]{2,1,0:T(2,128)S(1)} %constant_dynamic-slice_fusion), channel_id=1, source_target_pairs={{0,256},{256,0},{1,257},{257,1},{2,258},{258,2},{3,259},{259,3},{4... | collective-permute-start | bytes 6152 | tf_op jit(solution)/shard_map/ppermute | solution.py:20
Sparse Core Ops, SparseCore 0:
  10.3 78.9 all-gather.7
  97.8 71.7 all-gather.9
  171.7 74.9 all-gather.11

commit v6 on v5

--- a/solution.py
+++ b/solution.py
@@ -149,12 +149,12 @@
     out_full = lax.all_gather(out_weight, "seq", axis=1, tiled=True)
     both_rows = jnp.concatenate([token_rows, text_normed], axis=0)
     both_count = both_rows.shape[0]
-    both_rows = jnp.pad(
-        both_rows.reshape(both_count, seq_size, block_rows),
-        ((0, 0), (0, 0), (0, padded_rows - block_rows)),
+    both_cols = jnp.pad(
+        both_rows.T.reshape(seq_size, block_rows, both_count),
+        ((0, 0), (0, padded_rows - block_rows), (0, 0)),
     )
     both_term = jnp.einsum(
-        "rsd,sdn->rn", both_rows, piece, preferred_element_type=jnp.float32
+        "sdr,sdn->rn", both_cols, piece, preferred_element_type=jnp.float32
     ).reshape(both_count, kinds, local_cols)
     image_term = both_term[:row_count]
     text_term = both_term[row_count:]

time: 295 us -> 291 us (0.986)
  local copies, waits for them, and re-layouts: 53.4 us -> 27.6 us
  waiting for transfers between devices: 124 us -> 148 us
    all_gather x1, waiting for transfers between devices: 40.6 us -> 63.2 us  [body(): piece = lax.all_gather(all_weights, 'seq', axis=0, tiled=False)]
    add x3 -> x2, local copies, waits for them, and re-layouts: 8.09 us -> 0.59 us  [body(): layer_norm(hidden) * (1.0 + modulate[:, 1]) + modulate[:, 0]]
    convert_element_type x3 -> x1, local copies, waits for them, and re-layouts: 6.89 us -> 0.08 us  [body(): hidden = img_hidden[0].astype(jnp.float32)]
    mul x3 -> x2, local copies, waits for them, and re-layouts: 8.15 us -> 1.65 us  [body(): layer_norm(hidden) * (1.0 + modulate[:, 1]) + modulate[:, 0]]
    reshape x0 -> x2, local copies, waits for them, and re-layouts: none -> 5.49 us  [body(): both_rows.T.reshape(seq_size, block_rows, both_count)]
    convert_element_type x2 -> x0, local copies, waits for them, and re-layouts: 4.1 us -> none  [body(): txt_hidden[0].astype(jnp.float32)]
    squeeze x2 -> x0, local copies, waits for them, and re-layouts: 3.22 us -> none  [body(): text_mod[:, 0]]
  transfers between devices with their start and end apart: 6 -> 6, of which waited for: 6 -> 6; matrix products, arithmetic and copies ran while one was open for 18% -> 10% of each run, Pallas kernels for 3% -> 3%
where the time goes in v6:
time: 291 us
  waiting for transfers between devices  148 us (51%)
  blocking collectives  49 us (17%)
  local copies, waits for them, and re-layouts  27.6 us (9%)
  starting transfers between devices  17.1 us (6%)
  between operations  14.6 us (5%)
  matrix products  14.1 us (5%)
  other arithmetic  10.3 us (4%)
  Pallas kernels  9.76 us (3%)
    all_gather x1, waiting for transfers between devices, body(): piece = lax.all_gather(all_weights, 'seq', axis=0, tiled=False)  63.2 us
    all_gather x1, blocking collectives, body(): out_full = lax.all_gather(out_weight, 'seq', axis=1, tiled=True)  33.6 us
    all_gather x1, waiting for transfers between devices, body(): shared_piece = lax.all_gather(shared, 'seq', axis=0, tiled=False)  33.5 us
    all_to_all x2, waiting for transfers between devices, group_sum(): swapped = lax.all_to_all(partial, 'wgt', 0, 0, tiled=True)  25.8 us
    all_gather x1, waiting for transfers between devices, body(): mlp_full = lax.all_gather(mlp_local, 'seq', axis=0, tiled=False)  22.7 us
    all_to_all x1, blocking collectives, body(): lax.all_to_all(jnp.broadcast_to(branch_in.reshape(1, share_rows, feat_wid...  15.4 us
    all_to_all x2, starting transfers between devices, group_sum(): swapped = lax.all_to_all(partial, 'wgt', 0, 0, tiled=True)  14.5 us
    pallas_call x1, Pallas kernels, run(): pl.pallas_call(kernel, out_shape=jax.ShapeDtypeStruct(q.shape, jnp.bfloat...  9.76 us
  transfers between devices with their start and end apart: 6, of which 6 were waited for; matrix products, arithmetic and copies ran while one was open for 10% of the time, Pallas kernels for 3%

profile of v6, /device:TPU:32, one launch (start us, length us, event | category | flops | bytes accessed | tf_op | source)
XLA Modules:
  0.0 290.8 jit_solution(6779074209154201111)
XLA Ops:
  7.2 1.0 copy.86
  8.2 0.9 maximum_bitcast_fusion.1
  10.2 0.7 fusion.56
  11.7 1.5 mul.312
  14.8 1.3 fusion.52
  16.1 1.6 add_convert_fusion
  17.8 4.0 %reshape.334 = bf16[32,76,144]{1,0,2:T(8,128)(2,1)S(1)} reshape(bf16[2432,144]{0,1:T(8,128)(2,1)S(1)} %maximum_bitcast_fusion) | data formatting | bytes 1400832 | tf_op jit(solution)/shard_map/reshape | solution.py:153
  21.8 1.5 copy.85
  25.7 63.2 %all-gather.8.cloned.1.call-done = bf16[2560,960]{1,0:T(8,128)(2,1)} async-done(((bf16[80,960]{1,0:T(8,128)(2,1)}), bf16[2560,960]{1,0:T(8,128)(2,1)}) %all-gather.8.cloned.1.call-update) | async-done | bytes 4915216 | tf_op jit(solution)/shard_map/all_gather | solution.py:143
  88.9 3.9 %convolution_bitcast_fusion = f32[144,960]{1,0:T(8,128)S(1)} fusion(bf16[32,80,960]{2,1,0:T(8,128)(2,1)} %bitcast.164, bf16[32,76,144]{1,2,0:T(8,128)(2,1)} %copy.85), kind=kOutput, calls=%fused_computation.7 | convolution fusion | flops 707788800 | bytes 6168576 | tf_op jit(solution)/shard_map/sdr,sdn->rn/dot_general | solution.py:156
  95.5 0.8 fusion.46
  96.3 0.7 fusion.32
  97.2 33.6 %all-gather.3 = bf16[32,76,192]{2,1,0:T(8,128)(2,1)S(1)} all-gather(bf16[1,76,192]{2,1,0:T(8,128)(2,1)S(1)} %bitcast.161), channel_id=1, replica_groups=mesh['cfg'=2,'seq'=32,'wgt'=8] {'seq'}, dimensions={0}, use_global_device_ids=true | all-gather | bytes 963072 | tf_op jit(solution)/shard_map/all_gather | solution.py:149
  130.9 1.3 reshape.352
  134.2 33.5 %all-gather.10.cloned.1.call-done = bf16[9728,256]{1,0:T(8,128)(2,1)} async-done(((bf16[304,256]{1,0:T(8,128)(2,1)}), bf16[9728,256]{1,0:T(8,128)(2,1)}) %all-gather.10.cloned.1.call-update) | async-done | bytes 4980752 | tf_op jit(solution)/shard_map/all_gather | solution.py:191
  167.7 0.9 fusion.58
  169.3 9.8 %shard_map.140 = bf16[4,32,256]{2,1,0:T(8,128)(2,1)} custom-call(bf16[4,32,256]{2,1,0:T(8,128)(2,1)} %pad.34.q_ref, bf16[32,304,256]{2,1,0:T(8,128)(2,1)} %bitcast.150, f32[4,512]{1,0:T(4,128)} %fusion.62.mask_ref), custom_call_target="tpu_custom_call" | custom-call | tf_op jit(solution)/shard_map/pallas_call | solution.py:87
  179.0 0.8 slice_bitcast_fusion.17
  180.0 1.4 convolution_convert_fusion
  181.4 7.4 %all-to-all-start = ((bf16[8,16,2432]{2,1,0:T(8,128)(2,1)}), bf16[8,16,2432]{2,1,0:T(8,128)(2,1)S(1)}, u32[]{:S(2)}, u32[]{:S(2)}) async-start(bf16[8,16,2432]{2,1,0:T(8,128)(2,1)} %bitcast.28), calls=%async_computation | async-start | bytes 1245184 | tf_op jit(solution)/shard_map/all_to_all | solution.py:41
  189.1 12.7 %all-to-all-done = bf16[8,16,2432]{2,1,0:T(8,128)(2,1)S(1)} async-done(((bf16[8,16,2432]{2,1,0:T(8,128)(2,1)}), bf16[8,16,2432]{2,1,0:T(8,128)(2,1)S(1)}, u32[]{:S(2)}, u32[]{:S(2)}) %all-to-all-start) | async-done | bytes 622624 | tf_op jit(solution)/shard_map/all_to_all | solution.py:41
  202.5 15.4 %all_to_all.23 = bf16[8,16,2432]{2,1,0:T(8,128)(2,1)S(1)} all-to-all(bf16[8,16,2432]{2,1,0:T(8,128)(2,1)S(1)} %broadcast_in_dim.8), channel_id=1, replica_groups=mesh['cfg'=2,'seq'=32,'wgt'=8] {'wgt'}, dimensions={0} | all-to-all | bytes 1245184 | tf_op jit(solution)/shard_map/all_to_all | solution.py:220
  217.9 3.5 %reshape_reshape.6 = bf16[128,32,76]{2,1,0:T(8,128)(2,1)S(1)} reshape(bf16[8,16,2432]{2,1,0:T(8,128)(2,1)S(1)} %all_to_all.23) | data formatting | bytes 1245184 | tf_op jit(solution)/shard_map/reshape;reshape | solution.py:230
  221.4 1.1 copy.107
  222.5 22.7 %all-gather.12.cloned.1.call-done = bf16[64,80,704]{2,1,0:T(8,128)(2,1)} async-done(((bf16[2,80,704]{2,1,0:T(8,128)(2,1)}), bf16[64,80,704]{2,1,0:T(8,128)(2,1)}) %all-gather.12.cloned.1.call-update) | async-done | bytes 7208976 | tf_op jit(solution)/shard_map/all_gather | solution.py:148
  245.1 7.3 %fusion.2 = bf16[128,32,80]{0,2,1:T(8,128)(2,1)S(1)} fusion(bf16[32,2,80,704]{3,2,1,0:T(8,128)(2,1)} %bitcast.163, bf16[128,32,76]{0,2,1:T(8,128)(2,1)S(1)} %copy.107), kind=kOutput, calls=%fused_computation.5 | convolution fusion | flops 923885568 | bytes 8486912 | tf_op jit(solution)/shard_map/rf,sdf->rsd/dot_general | solution.py:237
  252.5 1.0 copy.110
  253.4 2.9 %all_to_all.18 = bf16[8,16,2560]{2,1,0:T(8,128)(2,1)} reshape(bf16[128,32,80]{2,1,0:T(8,128)(2,1)S(1)} %copy.110) | data formatting | bytes 1310720 | tf_op jit(solution)/shard_map/all_to_all | solution.py:41
  256.4 7.1 %all-to-all-start.2 = ((bf16[8,16,2560]{2,1,0:T(8,128)(2,1)}), bf16[8,16,2560]{2,1,0:T(8,128)(2,1)S(1)}, u32[]{:S(2)}, u32[]{:S(2)}) async-start(bf16[8,16,2560]{2,1,0:T(8,128)(2,1)} %all_to_all.18), calls=%async_computation.2 | async-start | bytes 1310720 | tf_op jit(solution)/shard_map/all_to_all | solution.py:41
  263.8 13.1 %all-to-all-done.2 = bf16[8,16,2560]{2,1,0:T(8,128)(2,1)S(1)} async-done(((bf16[8,16,2560]{2,1,0:T(8,128)(2,1)}), bf16[8,16,2560]{2,1,0:T(8,128)(2,1)S(1)}, u32[]{:S(2)}, u32[]{:S(2)}) %all-to-all-start.2) | async-done | bytes 655392 | tf_op jit(solution)/shard_map/all_to_all | solution.py:41
  278.1 2.5 collective-permute-start
  280.7 2.9 collective-permute-done
  (159 shorter events, 14.1 us)
Async XLA Ops:
  7.2 270.7 %copy-start = (bf16[2432,64]{0,1:T(8,128)(2,1)S(1)}, bf16[2432,64]{0,1:T(8,128)(2,1)}, u32[]{:S(2)}) copy-start(bf16[2432,64]{0,1:T(8,128)(2,1)} %param.25) | copy-start | bytes 933892
  7.2 3.0 %copy-start.4 = (f32[1,4,10,2432]{3,1,2,0:T(4,128)S(1)}, f32[1,4,10,2432]{3,1,2,0:T(4,128)}, u32[]{:S(2)}) copy-start(f32[1,4,10,2432]{3,1,2,0:T(4,128)} %param.18) | copy-start | bytes 1167364
  7.2 81.8 %all-gather.8.cloned.1.call-start = ((), (), s32[]{:S(2)}) async-start(), calls=%async_computation.3 | async-start | bytes 5406720 | tf_op jit(solution)/shard_map/all_gather | solution.py:143
  10.1 157.5 %all-gather.10.cloned.1.call-start = ((), (), s32[]{:S(2)}) async-start(), calls=%async_computation.4 | async-start | bytes 5136384 | tf_op jit(solution)/shard_map/all_gather | solution.py:191
  11.7 1.5 copy-start.1
  13.2 1.2 copy-start.3
  13.3 1.5 copy-start.20
  21.8 1.5 copy-start.19
  93.3 1.6 copy-start.14
  94.1 1.3 copy-start.15
  94.1 1.3 copy-start.18
  94.4 2.0 copy-start.11
  94.4 2.0 copy-start.12
  94.8 2.3 copy-start.17
  94.9 2.4 copy-start.13
  96.3 148.9 %all-gather.12.cloned.1.call-start = ((), (), s32[]{:S(2)}) async-start(), calls=%async_computation.5 | async-start | bytes 8110080 | tf_op jit(solution)/shard_map/all_gather | solution.py:148
  169.3 10.7 %copy-start.2 = (bf16[2432,192]{1,0:T(8,128)(2,1)S(1)}, bf16[2432,192]{1,0:T(8,128)(2,1)}, u32[]{:S(2)}) copy-start(bf16[2432,192]{1,0:T(8,128)(2,1)} %reshape.352) | copy-start | bytes 2801668
  180.0 8.8 %copy-start.10 = (f32[4,2432]{1,0:T(4,128)S(1)}, f32[4,2432]{1,0:T(4,128)}, u32[]{:S(2)}) copy-start(f32[4,2432]{1,0:T(4,128)} %get-tuple-element.19) | copy-start | bytes 116740
  181.4 7.5 %copy-start.9 = (f32[4,2432]{1,0:T(4,128)S(1)}, f32[4,2432]{1,0:T(4,128)}, u32[]{:S(2)}) copy-start(f32[4,2432]{1,0:T(4,128)} %get-tuple-element.15) | copy-start | bytes 116740
  181.4 7.6 %copy-start.8 = (f32[4,2432]{1,0:T(4,128)S(1)}, f32[4,2432]{1,0:T(4,128)}, u32[]{:S(2)}) copy-start(f32[4,2432]{1,0:T(4,128)} %get-tuple-element.12) | copy-start | bytes 116740
  181.4 20.4 %all-to-all-start = ((bf16[8,16,2432]{2,1,0:T(8,128)(2,1)}), bf16[8,16,2432]{2,1,0:T(8,128)(2,1)S(1)}, u32[]{:S(2)}, u32[]{:S(2)}) async-start(bf16[8,16,2432]{2,1,0:T(8,128)(2,1)} %bitcast.28), calls=%async_computation | async-start | bytes 1245184 | tf_op jit(solution)/shard_map/all_to_all | solution.py:41
  253.4 10.1 %copy-start.7 = (f32[4,2432]{1,0:T(4,128)S(1)}, f32[4,2432]{1,0:T(4,128)}, u32[]{:S(2)}) copy-start(f32[4,2432]{1,0:T(4,128)} %get-tuple-element.16) | copy-start | bytes 116740
  256.3 7.2 %copy-start.6 = (f32[4,2432]{1,0:T(4,128)S(1)}, f32[4,2432]{1,0:T(4,128)}, u32[]{:S(2)}) copy-start(f32[4,2432]{1,0:T(4,128)} %get-tuple-element.13) | copy-start | bytes 116740
  256.4 7.3 %copy-start.5 = (f32[4,2432]{1,0:T(4,128)S(1)}, f32[4,2432]{1,0:T(4,128)}, u32[]{:S(2)}) copy-start(f32[4,2432]{1,0:T(4,128)} %get-tuple-element.14) | copy-start | bytes 116740
  256.4 20.5 %all-to-all-start.2 = ((bf16[8,16,2560]{2,1,0:T(8,128)(2,1)}), bf16[8,16,2560]{2,1,0:T(8,128)(2,1)S(1)}, u32[]{:S(2)}, u32[]{:S(2)}) async-start(bf16[8,16,2560]{2,1,0:T(8,128)(2,1)} %all_to_all.18), calls=%async_computation.2 | async-start | bytes 1310720 | tf_op jit(solution)/shard_map/all_to_all | solution.py:41
  277.1 3.4 %copy-start.21 = (s32[4]{0:T(128)S(1)}, s32[4]{0:T(128)}, u32[]{:S(2)}) copy-start(s32[4]{0:T(128)} %param.17) | copy-start | bytes 52
  277.1 6.4 %copy-start.16 = (f32[4,2,64]{2,1,0:T(2,128)S(1)}, f32[4,2,64]{2,1,0:T(2,128)}, u32[]{:S(2)}) copy-start(f32[4,2,64]{2,1,0:T(2,128)} %param.13) | copy-start | bytes 6148
  278.1 5.5 %collective-permute-start = (f32[4,2,64]{2,1,0:T(2,128)S(1)}, f32[4,2,64]{2,1,0:T(2,128)S(1)}, u32[]{:S(2)}, u32[]{:S(2)}) collective-permute-start(f32[4,2,64]{2,1,0:T(2,128)S(1)} %constant_dynamic-slice_fusion), channel_id=1, source_target_pairs={{0,256},{256,0},{1,257},{257,1},{2,258},{258,2},{3,259},{259,3},{4... | collective-permute-start | bytes 6152 | tf_op jit(solution)/shard_map/ppermute | solution.py:20
Sparse Core Ops, SparseCore 0:
  10.3 78.6 all-gather.7
  96.4 71.2 all-gather.9
  169.8 75.3 all-gather.11

commit v7 on v6

--- a/solution.py
+++ b/solution.py
@@ -234,10 +234,11 @@
         "rsd,sdf->rf", padded_rows_in, mlp_full[:, 0], preferred_element_type=jnp.float32
     )
     expanded = jax.nn.gelu(expanded, approximate=True).astype(jnp.bfloat16)
-    contracted = jnp.einsum(
-        "rf,sdf->rsd", expanded, mlp_full[:, 1], preferred_element_type=jnp.float32
-    ).astype(jnp.bfloat16)
-    branch = group_sum(contracted.reshape(row_count, seq_size * padded_rows), wgt_size)
+    contract_rows = mlp_full[:, 1].reshape(seq_size * padded_rows, -1)
+    contracted = lax.dot_general(
+        expanded, contract_rows, (((1,), (1,)), ((), ())), preferred_element_type=jnp.float32
+    ).astype(jnp.bfloat16)
+    branch = group_sum(contracted, wgt_size)
     branch = branch.reshape(share_rows, seq_size, padded_rows)[:, :, :block_rows].reshape(
         share_rows, feat_width
     )

time: 291 us -> 297 us (1.021)
  waiting for transfers between devices: 148 us -> 166 us
  blocking collectives: 49 us -> 32.1 us
    all_gather x1, waiting for transfers between devices: 22.7 us -> 38.5 us  [body(): mlp_full = lax.all_gather(mlp_local, 'seq', axis=0, tiled=False)]
    all_to_all x1 -> x0, blocking collectives: 15.4 us -> none  [body(): lax.all_to_all(jnp.broadcast_to(branch_in.reshape(1, share_rows, feat_wid...]
    slice x0 -> x1, local copies, waits for them, and re-layouts: none -> 4.35 us  [body(): contract_rows = mlp_full[:, 1].reshape(seq_size * padded_rows, -1)]
    all_to_all x0 -> x1, starting transfers between devices: none -> 3.54 us  [body(): lax.all_to_all(jnp.broadcast_to(branch_in.reshape(1, share_rows, feat_wid...]
  transfers between devices with their start and end apart: 6 -> 7, of which waited for: 6 -> 6; matrix products, arithmetic and copies ran while one was open for 10% -> 10% of each run, Pallas kernels for 3% -> 3%
where the time goes in v7:
time: 297 us; the launch traced here: 296 us
  waiting for transfers between devices  166 us (56%)
  blocking collectives  32.1 us (11%)
  local copies, waits for them, and re-layouts  27.4 us (9%)
  starting transfers between devices  19.8 us (7%)
  matrix products  14.8 us (5%)
  between operations  14.5 us (5%)
  other arithmetic  11.6 us (4%)
  Pallas kernels  9.76 us (3%)
    all_gather x1, waiting for transfers between devices, body(): piece = lax.all_gather(all_weights, 'seq', axis=0, tiled=False)  64 us
    all_gather x1, waiting for transfers between devices, body(): mlp_full = lax.all_gather(mlp_local, 'seq', axis=0, tiled=False)  38.5 us
    all_gather x1, waiting for transfers between devices, body(): shared_piece = lax.all_gather(shared, 'seq', axis=0, tiled=False)  35.1 us
    all_gather x1, blocking collectives, body(): out_full = lax.all_gather(out_weight, 'seq', axis=1, tiled=True)  32.1 us
    all_to_all x2, waiting for transfers between devices, group_sum(): swapped = lax.all_to_all(partial, 'wgt', 0, 0, tiled=True)  25.8 us
    all_to_all x2, starting transfers between devices, group_sum(): swapped = lax.all_to_all(partial, 'wgt', 0, 0, tiled=True)  13.8 us
    pallas_call x1, Pallas kernels, run(): pl.pallas_call(kernel, out_shape=jax.ShapeDtypeStruct(q.shape, jnp.bfloat...  9.76 us
    dot_general x1, matrix products, body(): lax.dot_general(expanded, contract_rows, (((1,), (1,)), ((), ())), prefer...  8 us
  transfers between devices with their start and end apart: 7, of which 6 were waited for; matrix products, arithmetic and copies ran while one was open for 10% of the time, Pallas kernels for 3%

profile of v7, /device:TPU:32, one launch (start us, length us, event | category | flops | bytes accessed | tf_op | source)
XLA Modules:
  0.0 296.4 jit_solution(6470545771057426926)
XLA Ops:
  7.2 1.0 copy.80
  8.2 0.9 maximum_bitcast_fusion.1
  11.7 1.5 mul.312
  14.2 0.8 div.51
  15.0 1.3 fusion.2
  16.8 1.3 fusion.47
  18.1 1.6 add_convert_fusion
  19.8 4.0 %reshape.332 = bf16[32,76,144]{1,0,2:T(8,128)(2,1)S(1)} reshape(bf16[2432,144]{0,1:T(8,128)(2,1)S(1)} %maximum_bitcast_fusion) | data formatting | bytes 1400832 | tf_op jit(solution)/shard_map/reshape | solution.py:153
  23.8 1.5 copy.79
  25.5 64.0 %all-gather.8.cloned.1.call-done = bf16[2560,960]{1,0:T(8,128)(2,1)} async-done(((bf16[80,960]{1,0:T(8,128)(2,1)}), bf16[2560,960]{1,0:T(8,128)(2,1)}) %all-gather.8.cloned.1.call-update) | async-done | bytes 4915216 | tf_op jit(solution)/shard_map/all_gather | solution.py:143
  89.5 3.9 %convolution_bitcast_fusion = f32[144,960]{1,0:T(8,128)S(1)} fusion(bf16[32,80,960]{2,1,0:T(8,128)(2,1)} %bitcast.154, bf16[32,76,144]{1,2,0:T(8,128)(2,1)} %copy.79), kind=kOutput, calls=%fused_computation.5 | convolution fusion | flops 707788800 | bytes 6168576 | tf_op jit(solution)/shard_map/sdr,sdn->rn/dot_general | solution.py:156
  95.9 0.8 fusion.41
  97.7 32.1 %all-gather.3 = bf16[32,76,192]{2,1,0:T(8,128)(2,1)S(1)} all-gather(bf16[1,76,192]{2,1,0:T(8,128)(2,1)S(1)} %bitcast.152), channel_id=1, replica_groups=mesh['cfg'=2,'seq'=32,'wgt'=8] {'seq'}, dimensions={0}, use_global_device_ids=true | all-gather | bytes 963072 | tf_op jit(solution)/shard_map/all_gather | solution.py:149
  129.7 1.3 reshape.349
  133.0 35.1 %all-gather.10.cloned.1.call-done = bf16[9728,256]{1,0:T(8,128)(2,1)} async-done(((bf16[304,256]{1,0:T(8,128)(2,1)}), bf16[9728,256]{1,0:T(8,128)(2,1)}) %all-gather.10.cloned.1.call-update) | async-done | bytes 4980752 | tf_op jit(solution)/shard_map/all_gather | solution.py:191
  168.1 0.9 fusion.53
  169.7 9.8 %shard_map.140 = bf16[4,32,256]{2,1,0:T(8,128)(2,1)} custom-call(bf16[4,32,256]{2,1,0:T(8,128)(2,1)} %pad.34.q_ref, bf16[32,304,256]{2,1,0:T(8,128)(2,1)} %bitcast.138, f32[4,512]{1,0:T(4,128)} %fusion.57.mask_ref), custom_call_target="tpu_custom_call" | custom-call | tf_op jit(solution)/shard_map/pallas_call | solution.py:87
  179.5 0.8 slice_bitcast_fusion.11
  180.5 1.4 convolution_convert_fusion.1
  181.9 7.0 %all-to-all-start = ((bf16[8,16,2432]{2,1,0:T(8,128)(2,1)}), bf16[8,16,2432]{2,1,0:T(8,128)(2,1)S(1)}, u32[]{:S(2)}, u32[]{:S(2)}) async-start(bf16[8,16,2432]{2,1,0:T(8,128)(2,1)} %bitcast.28), calls=%async_computation | async-start | bytes 1245184 | tf_op jit(solution)/shard_map/all_to_all | solution.py:41
  189.2 12.7 %all-to-all-done = bf16[8,16,2432]{2,1,0:T(8,128)(2,1)S(1)} async-done(((bf16[8,16,2432]{2,1,0:T(8,128)(2,1)}), bf16[8,16,2432]{2,1,0:T(8,128)(2,1)S(1)}, u32[]{:S(2)}, u32[]{:S(2)}) %all-to-all-start) | async-done | bytes 622624 | tf_op jit(solution)/shard_map/all_to_all | solution.py:41
  202.5 0.9 broadcast_in_dim.8
  203.4 3.5 %all-to-all-start.1 = ((bf16[8,16,2432]{2,1,0:T(8,128)(2,1)}), bf16[8,16,2432]{2,1,0:T(8,128)(2,1)S(1)}, u32[]{:S(2)}, u32[]{:S(2)}) async-start(bf16[8,16,2432]{2,1,0:T(8,128)(2,1)} %broadcast_in_dim.8), calls=%async_computation.1 | async-start | bytes 1245184 | tf_op jit(solution)/shard_map/all_to_all | solution.py:220
  206.9 38.5 %all-gather.12.cloned.1.call-done = bf16[64,80,704]{2,1,0:T(8,128)(2,1)} async-done(((bf16[2,80,704]{2,1,0:T(8,128)(2,1)}), bf16[64,80,704]{2,1,0:T(8,128)(2,1)}) %all-gather.12.cloned.1.call-update) | async-done | bytes 7208976 | tf_op jit(solution)/shard_map/all_gather | solution.py:148
  245.4 4.4 %slice.130 = bf16[32,1,80,704]{3,2,1,0:T(8,128)(2,1)} slice(bf16[32,2,80,704]{3,2,1,0:T(8,128)(2,1)} %bitcast.140), slice={[0:32], [1:2], [0:80], [0:704]} | slice | bytes 7208960 | tf_op jit(solution)/shard_map/slice | solution.py:237
  249.7 3.5 %reshape_reshape.6 = bf16[128,32,76]{2,1,0:T(8,128)(2,1)S(1)} reshape(bf16[8,16,2432]{2,1,0:T(8,128)(2,1)S(1)} %all-to-all-done.1) | data formatting | bytes 1245184 | tf_op jit(solution)/shard_map/reshape;reshape | solution.py:230
  253.3 1.1 copy.101
  254.3 8.0 %convolution_convert_fusion = bf16[128,2560]{1,0:T(8,128)(2,1)} fusion(bf16[2560,704]{1,0:T(8,128)(2,1)} %bitcast.139, bf16[32,2,80,704]{3,2,1,0:T(8,128)(2,1)} %bitcast.141, bf16[128,32,76]{0,2,1:T(8,128)(2,1)S(1)} %copy.101), kind=kOutput, calls=%fused_computation.2 | convolution fusion | flops 923885568 | bytes 9142272 | tf_op jit(solution)/shard_map/dot_general | solution.py:238
  262.3 6.8 %all-to-all-start.2 = ((bf16[8,16,2560]{2,1,0:T(8,128)(2,1)}), bf16[8,16,2560]{2,1,0:T(8,128)(2,1)S(1)}, u32[]{:S(2)}, u32[]{:S(2)}) async-start(bf16[8,16,2560]{2,1,0:T(8,128)(2,1)} %bitcast.39), calls=%async_computation.2 | async-start | bytes 1310720 | tf_op jit(solution)/shard_map/all_to_all | solution.py:41
  269.5 13.1 %all-to-all-done.2 = bf16[8,16,2560]{2,1,0:T(8,128)(2,1)S(1)} async-done(((bf16[8,16,2560]{2,1,0:T(8,128)(2,1)}), bf16[8,16,2560]{2,1,0:T(8,128)(2,1)S(1)}, u32[]{:S(2)}, u32[]{:S(2)}) %all-to-all-start.2) | async-done | bytes 655392 | tf_op jit(solution)/shard_map/all_to_all | solution.py:41
  283.7 2.3 collective-permute-start
  286.2 3.1 %collective-permute-done = f32[4,2,64]{2,1,0:T(2,128)S(1)} collective-permute-done((f32[4,2,64]{2,1,0:T(2,128)S(1)}, f32[4,2,64]{2,1,0:T(2,128)S(1)}, u32[]{:S(2)}, u32[]{:S(2)}) %collective-permute-start) | collective-permute-done | bytes 2080 | tf_op jit(solution)/shard_map/ppermute | solution.py:20
  (149 shorter events, 13.2 us)
Async XLA Ops:
  7.2 276.3 %copy-start = (bf16[2432,64]{0,1:T(8,128)(2,1)S(1)}, bf16[2432,64]{0,1:T(8,128)(2,1)}, u32[]{:S(2)}) copy-start(bf16[2432,64]{0,1:T(8,128)(2,1)} %param.25) | copy-start | bytes 933892
  7.2 3.0 %copy-start.4 = (f32[1,4,10,2432]{3,1,2,0:T(4,128)S(1)}, f32[1,4,10,2432]{3,1,2,0:T(4,128)}, u32[]{:S(2)}) copy-start(f32[1,4,10,2432]{3,1,2,0:T(4,128)} %param.18) | copy-start | bytes 1167364
  7.2 82.3 %all-gather.8.cloned.1.call-start = ((), (), s32[]{:S(2)}) async-start(), calls=%async_computation.3 | async-start | bytes 5406720 | tf_op jit(solution)/shard_map/all_gather | solution.py:143
  10.1 158.0 %all-gather.10.cloned.1.call-start = ((), (), s32[]{:S(2)}) async-start(), calls=%async_computation.4 | async-start | bytes 5136384 | tf_op jit(solution)/shard_map/all_gather | solution.py:191
  11.7 1.5 copy-start.1
  13.2 3.2 %copy-start.3 = (bf16[1,16,2432]{2,1,0:T(8,128)(2,1)S(1)}, bf16[1,16,2432]{2,1,0:T(8,128)(2,1)}, u32[]{:S(2)}) copy-start(bf16[1,16,2432]{2,1,0:T(8,128)(2,1)} %param.15) | copy-start | bytes 233476
  13.3 3.5 %copy-start.15 = (s32[1,16]{1,0:T(1,128)S(1)}, s32[1,16]{1,0:T(1,128)}, u32[]{:S(2)}) copy-start(s32[1,16]{1,0:T(1,128)} %param.16) | copy-start | bytes 196
  23.8 1.5 copy-start.14
  94.9 1.9 copy-start.10
  94.9 1.9 copy-start.11
  95.3 2.3 copy-start.12
  96.7 148.6 %all-gather.12.cloned.1.call-start = ((), (), s32[]{:S(2)}) async-start(), calls=%async_computation.5 | async-start | bytes 8110080 | tf_op jit(solution)/shard_map/all_gather | solution.py:148
  169.7 10.7 %copy-start.2 = (bf16[2432,192]{1,0:T(8,128)(2,1)S(1)}, bf16[2432,192]{1,0:T(8,128)(2,1)}, u32[]{:S(2)}) copy-start(bf16[2432,192]{1,0:T(8,128)(2,1)} %reshape.349) | copy-start | bytes 2801668
  180.5 8.4 %copy-start.9 = (f32[4,2432]{1,0:T(4,128)S(1)}, f32[4,2432]{1,0:T(4,128)}, u32[]{:S(2)}) copy-start(f32[4,2432]{1,0:T(4,128)} %get-tuple-element.19) | copy-start | bytes 116740
  181.9 7.1 %copy-start.8 = (f32[4,2432]{1,0:T(4,128)S(1)}, f32[4,2432]{1,0:T(4,128)}, u32[]{:S(2)}) copy-start(f32[4,2432]{1,0:T(4,128)} %get-tuple-element.15) | copy-start | bytes 116740
  181.9 7.2 %copy-start.7 = (f32[4,2432]{1,0:T(4,128)S(1)}, f32[4,2432]{1,0:T(4,128)}, u32[]{:S(2)}) copy-start(f32[4,2432]{1,0:T(4,128)} %get-tuple-element.12) | copy-start | bytes 116740
  181.9 20.0 %all-to-all-start = ((bf16[8,16,2432]{2,1,0:T(8,128)(2,1)}), bf16[8,16,2432]{2,1,0:T(8,128)(2,1)S(1)}, u32[]{:S(2)}, u32[]{:S(2)}) async-start(bf16[8,16,2432]{2,1,0:T(8,128)(2,1)} %bitcast.28), calls=%async_computation | async-start | bytes 1245184 | tf_op jit(solution)/shard_map/all_to_all | solution.py:41
  203.4 46.4 %all-to-all-start.1 = ((bf16[8,16,2432]{2,1,0:T(8,128)(2,1)}), bf16[8,16,2432]{2,1,0:T(8,128)(2,1)S(1)}, u32[]{:S(2)}, u32[]{:S(2)}) async-start(bf16[8,16,2432]{2,1,0:T(8,128)(2,1)} %broadcast_in_dim.8), calls=%async_computation.1 | async-start | bytes 1245184 | tf_op jit(solution)/shard_map/all_to_all | solution.py:220
  262.3 6.8 %copy-start.6 = (f32[4,2432]{1,0:T(4,128)S(1)}, f32[4,2432]{1,0:T(4,128)}, u32[]{:S(2)}) copy-start(f32[4,2432]{1,0:T(4,128)} %get-tuple-element.16) | copy-start | bytes 116740
  262.3 6.9 %copy-start.5 = (f32[4,2432]{1,0:T(4,128)S(1)}, f32[4,2432]{1,0:T(4,128)}, u32[]{:S(2)}) copy-start(f32[4,2432]{1,0:T(4,128)} %get-tuple-element.13) | copy-start | bytes 116740
  262.3 20.2 %all-to-all-start.2 = ((bf16[8,16,2560]{2,1,0:T(8,128)(2,1)}), bf16[8,16,2560]{2,1,0:T(8,128)(2,1)S(1)}, u32[]{:S(2)}, u32[]{:S(2)}) async-start(bf16[8,16,2560]{2,1,0:T(8,128)(2,1)} %bitcast.39), calls=%async_computation.2 | async-start | bytes 1310720 | tf_op jit(solution)/shard_map/all_to_all | solution.py:41
  282.8 3.3 %copy-start.16 = (s32[4]{0:T(128)S(1)}, s32[4]{0:T(128)}, u32[]{:S(2)}) copy-start(s32[4]{0:T(128)} %param.17) | copy-start | bytes 52
  282.8 6.4 %copy-start.13 = (f32[4,2,64]{2,1,0:T(2,128)S(1)}, f32[4,2,64]{2,1,0:T(2,128)}, u32[]{:S(2)}) copy-start(f32[4,2,64]{2,1,0:T(2,128)} %param.13) | copy-start | bytes 6148
  283.7 5.5 %collective-permute-start = (f32[4,2,64]{2,1,0:T(2,128)S(1)}, f32[4,2,64]{2,1,0:T(2,128)S(1)}, u32[]{:S(2)}, u32[]{:S(2)}) collective-permute-start(f32[4,2,64]{2,1,0:T(2,128)S(1)} %constant_dynamic-slice_fusion), channel_id=1, source_target_pairs={{0,256},{256,0},{1,257},{257,1},{2,258},{258,2},{3,259},{259,3},{4... | collective-permute-start | bytes 6152 | tf_op jit(solution)/shard_map/ppermute | solution.py:20
Sparse Core Ops, SparseCore 0:
  10.3 79.1 all-gather.7
  96.8 71.2 all-gather.9
  170.3 75.0 all-gather.11

commit v8 on v7

--- a/solution.py
+++ b/solution.py
@@ -145,7 +145,7 @@
         jnp.stack([expand_weight, contract_weight.T], axis=0),
         ((0, 0), (0, padded_rows - block_rows), (0, 0)),
     )
-    mlp_full = lax.all_gather(mlp_local, "seq", axis=0, tiled=False)
+    mlp_full = lax.all_gather(mlp_local, "seq", axis=1, tiled=False)
     out_full = lax.all_gather(out_weight, "seq", axis=1, tiled=True)
     both_rows = jnp.concatenate([token_rows, text_normed], axis=0)
     both_count = both_rows.shape[0]
@@ -231,10 +231,10 @@
         ((0, 0), (0, 0), (0, padded_rows - block_rows)),
     )
     expanded = jnp.einsum(
-        "rsd,sdf->rf", padded_rows_in, mlp_full[:, 0], preferred_element_type=jnp.float32
+        "rsd,sdf->rf", padded_rows_in, mlp_full[0], preferred_element_type=jnp.float32
     )
     expanded = jax.nn.gelu(expanded, approximate=True).astype(jnp.bfloat16)
-    contract_rows = mlp_full[:, 1].reshape(seq_size * padded_rows, -1)
+    contract_rows = mlp_full[1].reshape(seq_size * padded_rows, -1)
     contracted = lax.dot_general(
         expanded, contract_rows, (((1,), (1,)), ((), ())), preferred_element_type=jnp.float32
     ).astype(jnp.bfloat16)

time: 297 us -> 297 us (level)
  no operation moved by 1% of the time
where the time goes in v8:
time: 297 us; the launch traced here: 296 us
  waiting for transfers between devices  166 us (56%)
  blocking collectives  32.1 us (11%)
  local copies, waits for them, and re-layouts  27.4 us (9%)
  starting transfers between devices  19.9 us (7%)
  matrix products  14.8 us (5%)
  between operations  14.5 us (5%)
  other arithmetic  11.6 us (4%)
  Pallas kernels  9.76 us (3%)
    all_gather x1, waiting for transfers between devices, body(): piece = lax.all_gather(all_weights, 'seq', axis=0, tiled=False)  64 us
    all_gather x1, waiting for transfers between devices, body(): mlp_full = lax.all_gather(mlp_local, 'seq', axis=1, tiled=False)  38.3 us
    all_gather x1, waiting for transfers between devices, body(): shared_piece = lax.all_gather(shared, 'seq', axis=0, tiled=False)  35.1 us
    all_gather x1, blocking collectives, body(): out_full = lax.all_gather(out_weight, 'seq', axis=1, tiled=True)  32.1 us
    all_to_all x2, waiting for transfers between devices, group_sum(): swapped = lax.all_to_all(partial, 'wgt', 0, 0, tiled=True)  25.8 us
    all_to_all x2, starting transfers between devices, group_sum(): swapped = lax.all_to_all(partial, 'wgt', 0, 0, tiled=True)  14 us
    pallas_call x1, Pallas kernels, run(): pl.pallas_call(kernel, out_shape=jax.ShapeDtypeStruct(q.shape, jnp.bfloat...  9.76 us
    dot_general x1, matrix products, body(): lax.dot_general(expanded, contract_rows, (((1,), (1,)), ((), ())), prefer...  7.99 us
  transfers between devices with their start and end apart: 7, of which 6 were waited for; matrix products, arithmetic and copies ran while one was open for 10% of the time, Pallas kernels for 3%

profile of v8, /device:TPU:32, one launch (start us, length us, event | category | flops | bytes accessed | tf_op | source)
XLA Modules:
  0.0 296.5 jit_solution(17035905270137350520)
XLA Ops:
  7.2 1.0 copy.77
  8.2 0.9 maximum_bitcast_fusion.1
  11.7 1.5 mul.312
  14.2 0.8 div.51
  15.0 1.3 fusion.3
  16.8 1.3 fusion.47
  18.1 1.6 add_convert_fusion
  19.8 4.0 %reshape.332 = bf16[32,76,144]{1,0,2:T(8,128)(2,1)S(1)} reshape(bf16[2432,144]{0,1:T(8,128)(2,1)S(1)} %maximum_bitcast_fusion) | data formatting | bytes 1400832 | tf_op jit(solution)/shard_map/reshape | solution.py:153
  23.8 1.5 copy.76
  25.5 64.0 %all-gather.8.cloned.1.call-done = bf16[2560,960]{1,0:T(8,128)(2,1)} async-done(((bf16[80,960]{1,0:T(8,128)(2,1)}), bf16[2560,960]{1,0:T(8,128)(2,1)}) %all-gather.8.cloned.1.call-update) | async-done | bytes 4915216 | tf_op jit(solution)/shard_map/all_gather | solution.py:143
  89.5 3.9 %convolution_bitcast_fusion = f32[144,960]{1,0:T(8,128)S(1)} fusion(bf16[32,80,960]{2,1,0:T(8,128)(2,1)} %bitcast.143, bf16[32,76,144]{1,2,0:T(8,128)(2,1)} %copy.76), kind=kOutput, calls=%fused_computation.5 | convolution fusion | flops 707788800 | bytes 6168576 | tf_op jit(solution)/shard_map/sdr,sdn->rn/dot_general | solution.py:156
  95.9 0.8 fusion.41
  97.7 32.1 %all-gather.3 = bf16[32,76,192]{2,1,0:T(8,128)(2,1)S(1)} all-gather(bf16[1,76,192]{2,1,0:T(8,128)(2,1)S(1)} %bitcast.141), channel_id=1, replica_groups=mesh['cfg'=2,'seq'=32,'wgt'=8] {'seq'}, dimensions={0}, use_global_device_ids=true | all-gather | bytes 963072 | tf_op jit(solution)/shard_map/all_gather | solution.py:149
  129.7 1.3 reshape.353
  133.0 35.1 %all-gather.10.cloned.1.call-done = bf16[9728,256]{1,0:T(8,128)(2,1)} async-done(((bf16[304,256]{1,0:T(8,128)(2,1)}), bf16[9728,256]{1,0:T(8,128)(2,1)}) %all-gather.10.cloned.1.call-update) | async-done | bytes 4980752 | tf_op jit(solution)/shard_map/all_gather | solution.py:191
  168.1 0.9 fusion.53
  169.7 9.8 %shard_map.140 = bf16[4,32,256]{2,1,0:T(8,128)(2,1)} custom-call(bf16[4,32,256]{2,1,0:T(8,128)(2,1)} %pad.34.q_ref, bf16[32,304,256]{2,1,0:T(8,128)(2,1)} %bitcast.129, f32[4,512]{1,0:T(4,128)} %fusion.57.mask_ref), custom_call_target="tpu_custom_call" | custom-call | tf_op jit(solution)/shard_map/pallas_call | solution.py:87
  179.5 0.8 slice_bitcast_fusion.5
  180.5 1.4 convolution_convert_fusion
  181.9 7.0 %all-to-all-start = ((bf16[8,16,2432]{2,1,0:T(8,128)(2,1)}), bf16[8,16,2432]{2,1,0:T(8,128)(2,1)S(1)}, u32[]{:S(2)}, u32[]{:S(2)}) async-start(bf16[8,16,2432]{2,1,0:T(8,128)(2,1)} %bitcast.28), calls=%async_computation | async-start | bytes 1245184 | tf_op jit(solution)/shard_map/all_to_all | solution.py:41
  189.2 12.7 %all-to-all-done = bf16[8,16,2432]{2,1,0:T(8,128)(2,1)S(1)} async-done(((bf16[8,16,2432]{2,1,0:T(8,128)(2,1)}), bf16[8,16,2432]{2,1,0:T(8,128)(2,1)S(1)}, u32[]{:S(2)}, u32[]{:S(2)}) %all-to-all-start) | async-done | bytes 622624 | tf_op jit(solution)/shard_map/all_to_all | solution.py:41
  202.5 0.9 broadcast_in_dim.8
  203.4 3.5 %all-to-all-start.1 = ((bf16[8,16,2432]{2,1,0:T(8,128)(2,1)}), bf16[8,16,2432]{2,1,0:T(8,128)(2,1)S(1)}, u32[]{:S(2)}, u32[]{:S(2)}) async-start(bf16[8,16,2432]{2,1,0:T(8,128)(2,1)} %broadcast_in_dim.8), calls=%async_computation.1 | async-start | bytes 1245184 | tf_op jit(solution)/shard_map/all_to_all | solution.py:220
  206.9 38.3 %all-gather.12.cloned.1.call-done = bf16[2,2560,704]{2,1,0:T(8,128)(2,1)} async-done(((bf16[2,80,704]{2,1,0:T(8,128)(2,1)}), bf16[2,2560,704]{2,1,0:T(8,128)(2,1)}) %all-gather.12.cloned.1.call-update) | async-done | bytes 7208976 | tf_op jit(solution)/shard_map/all_gather | solution.py:148
  245.2 4.3 %slice.131 = bf16[1,2560,704]{2,1,0:T(8,128)(2,1)} slice(bf16[2,2560,704]{2,1,0:T(8,128)(2,1)} %all-gather.12.cloned.1.call-done), slice={[0:1], [0:2560], [0:704]} | slice | bytes 7208960 | tf_op jit(solution)/shard_map/slice | solution.py:234
  249.5 3.5 %reshape_reshape.6 = bf16[128,32,76]{2,1,0:T(8,128)(2,1)S(1)} reshape(bf16[8,16,2432]{2,1,0:T(8,128)(2,1)S(1)} %all-to-all-done.1) | data formatting | bytes 1245184 | tf_op jit(solution)/shard_map/reshape;reshape | solution.py:230
  253.1 1.1 copy.98
  254.1 8.0 %fusion.1 = bf16[128,2560]{1,0:T(8,128)(2,1)} fusion(bf16[2,2560,704]{2,1,0:T(8,128)(2,1)} %all-gather.12.cloned.1.call-done, bf16[32,80,704]{2,1,0:T(8,128)(2,1)} %bitcast.130, bf16[128,32,76]{0,2,1:T(8,128)(2,1)S(1)} %copy.98), kind=kOutput, calls=%fused_computation.2 | convolution fusion | flops 923885568 | bytes 9142272 | tf_op jit(solution)/shard_map/dot_general | solution.py:238
  262.1 7.0 %all-to-all-start.2 = ((bf16[8,16,2560]{2,1,0:T(8,128)(2,1)}), bf16[8,16,2560]{2,1,0:T(8,128)(2,1)S(1)}, u32[]{:S(2)}, u32[]{:S(2)}) async-start(bf16[8,16,2560]{2,1,0:T(8,128)(2,1)} %bitcast.38), calls=%async_computation.2 | async-start | bytes 1310720 | tf_op jit(solution)/shard_map/all_to_all | solution.py:41
  269.5 13.1 %all-to-all-done.2 = bf16[8,16,2560]{2,1,0:T(8,128)(2,1)S(1)} async-done(((bf16[8,16,2560]{2,1,0:T(8,128)(2,1)}), bf16[8,16,2560]{2,1,0:T(8,128)(2,1)S(1)}, u32[]{:S(2)}, u32[]{:S(2)}) %all-to-all-start.2) | async-done | bytes 655392 | tf_op jit(solution)/shard_map/all_to_all | solution.py:41
  283.8 2.2 collective-permute-start
  286.1 3.2 %collective-permute-done = f32[4,2,64]{2,1,0:T(2,128)S(1)} collective-permute-done((f32[4,2,64]{2,1,0:T(2,128)S(1)}, f32[4,2,64]{2,1,0:T(2,128)S(1)}, u32[]{:S(2)}, u32[]{:S(2)}) %collective-permute-start) | collective-permute-done | bytes 2080 | tf_op jit(solution)/shard_map/ppermute | solution.py:20
  (149 shorter events, 13.2 us)
Async XLA Ops:
  7.2 276.4 %copy-start = (bf16[2432,64]{0,1:T(8,128)(2,1)S(1)}, bf16[2432,64]{0,1:T(8,128)(2,1)}, u32[]{:S(2)}) copy-start(bf16[2432,64]{0,1:T(8,128)(2,1)} %param.25) | copy-start | bytes 933892
  7.2 3.0 %copy-start.4 = (f32[1,4,10,2432]{3,1,2,0:T(4,128)S(1)}, f32[1,4,10,2432]{3,1,2,0:T(4,128)}, u32[]{:S(2)}) copy-start(f32[1,4,10,2432]{3,1,2,0:T(4,128)} %param.18) | copy-start | bytes 1167364
  7.2 82.3 %all-gather.8.cloned.1.call-start = ((), (), s32[]{:S(2)}) async-start(), calls=%async_computation.3 | async-start | bytes 5406720 | tf_op jit(solution)/shard_map/all_gather | solution.py:143
  10.1 158.0 %all-gather.10.cloned.1.call-start = ((), (), s32[]{:S(2)}) async-start(), calls=%async_computation.4 | async-start | bytes 5136384 | tf_op jit(solution)/shard_map/all_gather | solution.py:191
  11.7 1.5 copy-start.1
  13.2 3.2 %copy-start.3 = (bf16[1,16,2432]{2,1,0:T(8,128)(2,1)S(1)}, bf16[1,16,2432]{2,1,0:T(8,128)(2,1)}, u32[]{:S(2)}) copy-start(bf16[1,16,2432]{2,1,0:T(8,128)(2,1)} %param.15) | copy-start | bytes 233476
  13.3 3.5 %copy-start.15 = (s32[1,16]{1,0:T(1,128)S(1)}, s32[1,16]{1,0:T(1,128)}, u32[]{:S(2)}) copy-start(s32[1,16]{1,0:T(1,128)} %param.16) | copy-start | bytes 196
  23.8 1.5 copy-start.14
  94.9 1.9 copy-start.10
  94.9 1.9 copy-start.11
  95.3 2.3 copy-start.12
  96.7 148.5 %all-gather.12.cloned.1.call-start = ((), (), s32[]{:S(2)}) async-start(), calls=%async_computation.5 | async-start | bytes 8110080 | tf_op jit(solution)/shard_map/all_gather | solution.py:148
  169.7 10.7 %copy-start.2 = (bf16[2432,192]{1,0:T(8,128)(2,1)S(1)}, bf16[2432,192]{1,0:T(8,128)(2,1)}, u32[]{:S(2)}) copy-start(bf16[2432,192]{1,0:T(8,128)(2,1)} %reshape.353) | copy-start | bytes 2801668
  180.5 8.4 %copy-start.9 = (f32[4,2432]{1,0:T(4,128)S(1)}, f32[4,2432]{1,0:T(4,128)}, u32[]{:S(2)}) copy-start(f32[4,2432]{1,0:T(4,128)} %get-tuple-element.19) | copy-start | bytes 116740
  181.9 7.1 %copy-start.8 = (f32[4,2432]{1,0:T(4,128)S(1)}, f32[4,2432]{1,0:T(4,128)}, u32[]{:S(2)}) copy-start(f32[4,2432]{1,0:T(4,128)} %get-tuple-element.15) | copy-start | bytes 116740
  181.9 7.2 %copy-start.7 = (f32[4,2432]{1,0:T(4,128)S(1)}, f32[4,2432]{1,0:T(4,128)}, u32[]{:S(2)}) copy-start(f32[4,2432]{1,0:T(4,128)} %get-tuple-element.12) | copy-start | bytes 116740
  181.9 20.0 %all-to-all-start = ((bf16[8,16,2432]{2,1,0:T(8,128)(2,1)}), bf16[8,16,2432]{2,1,0:T(8,128)(2,1)S(1)}, u32[]{:S(2)}, u32[]{:S(2)}) async-start(bf16[8,16,2432]{2,1,0:T(8,128)(2,1)} %bitcast.28), calls=%async_computation | async-start | bytes 1245184 | tf_op jit(solution)/shard_map/all_to_all | solution.py:41
  203.4 46.2 %all-to-all-start.1 = ((bf16[8,16,2432]{2,1,0:T(8,128)(2,1)}), bf16[8,16,2432]{2,1,0:T(8,128)(2,1)S(1)}, u32[]{:S(2)}, u32[]{:S(2)}) async-start(bf16[8,16,2432]{2,1,0:T(8,128)(2,1)} %broadcast_in_dim.8), calls=%async_computation.1 | async-start | bytes 1245184 | tf_op jit(solution)/shard_map/all_to_all | solution.py:220
  262.1 7.0 %copy-start.6 = (f32[4,2432]{1,0:T(4,128)S(1)}, f32[4,2432]{1,0:T(4,128)}, u32[]{:S(2)}) copy-start(f32[4,2432]{1,0:T(4,128)} %get-tuple-element.16) | copy-start | bytes 116740
  262.1 7.1 %copy-start.5 = (f32[4,2432]{1,0:T(4,128)S(1)}, f32[4,2432]{1,0:T(4,128)}, u32[]{:S(2)}) copy-start(f32[4,2432]{1,0:T(4,128)} %get-tuple-element.13) | copy-start | bytes 116740
  262.1 20.4 %all-to-all-start.2 = ((bf16[8,16,2560]{2,1,0:T(8,128)(2,1)}), bf16[8,16,2560]{2,1,0:T(8,128)(2,1)S(1)}, u32[]{:S(2)}, u32[]{:S(2)}) async-start(bf16[8,16,2560]{2,1,0:T(8,128)(2,1)} %bitcast.38), calls=%async_computation.2 | async-start | bytes 1310720 | tf_op jit(solution)/shard_map/all_to_all | solution.py:41
  282.8 3.2 %copy-start.16 = (s32[4]{0:T(128)S(1)}, s32[4]{0:T(128)}, u32[]{:S(2)}) copy-start(s32[4]{0:T(128)} %param.17) | copy-start | bytes 52
  282.8 6.4 %copy-start.13 = (f32[4,2,64]{2,1,0:T(2,128)S(1)}, f32[4,2,64]{2,1,0:T(2,128)}, u32[]{:S(2)}) copy-start(f32[4,2,64]{2,1,0:T(2,128)} %param.13) | copy-start | bytes 6148
  283.8 5.5 %collective-permute-start = (f32[4,2,64]{2,1,0:T(2,128)S(1)}, f32[4,2,64]{2,1,0:T(2,128)S(1)}, u32[]{:S(2)}, u32[]{:S(2)}) collective-permute-start(f32[4,2,64]{2,1,0:T(2,128)S(1)} %constant_dynamic-slice_fusion), channel_id=1, source_target_pairs={{0,256},{256,0},{1,257},{257,1},{2,258},{258,2},{3,259},{259,3},{4... | collective-permute-start | bytes 6152 | tf_op jit(solution)/shard_map/ppermute | solution.py:20
Sparse Core Ops, SparseCore 0:
  10.3 79.1 all-gather.7
  96.8 71.2 all-gather.9
  170.3 74.8 all-gather.11

commit v9 on v7

--- a/solution.py
+++ b/solution.py
@@ -94,6 +94,27 @@
     return run
 
 
+def mlp_kernel(x_ref, w_ref, o_ref):
+    blocks, _, rows, units = w_ref.shape
+    expand = w_ref[:, 0].reshape(blocks * rows, units)
+    grown = jnp.dot(x_ref[...], expand, preferred_element_type=jnp.float32)
+    grown = jax.nn.gelu(grown, approximate=True).astype(jnp.bfloat16)
+    contract = w_ref[:, 1].reshape(blocks * rows, units)
+    o_ref[...] = lax.dot_general(
+        grown, contract, (((1,), (1,)), ((), ())), preferred_element_type=jnp.float32
+    ).astype(o_ref.dtype)
+
+
+def run_mlp(rows_in, weights):
+    blocks, _, rows, _ = weights.shape
+    return pl.pallas_call(
+        mlp_kernel,
+        out_shape=jax.ShapeDtypeStruct((rows_in.shape[0], blocks * rows), jnp.bfloat16),
+        in_specs=[pl.BlockSpec(memory_space=pltpu.VMEM)] * 2,
+        out_specs=pl.BlockSpec(memory_space=pltpu.VMEM),
+    )(rows_in, weights)
+
+
 def body(
     latent,
     img_hidden,
@@ -230,14 +251,7 @@
         branch_rows.reshape(row_count, seq_size, block_rows),
         ((0, 0), (0, 0), (0, padded_rows - block_rows)),
     )
-    expanded = jnp.einsum(
-        "rsd,sdf->rf", padded_rows_in, mlp_full[:, 0], preferred_element_type=jnp.float32
-    )
-    expanded = jax.nn.gelu(expanded, approximate=True).astype(jnp.bfloat16)
-    contract_rows = mlp_full[:, 1].reshape(seq_size * padded_rows, -1)
-    contracted = lax.dot_general(
-        expanded, contract_rows, (((1,), (1,)), ((), ())), preferred_element_type=jnp.float32
-    ).astype(jnp.bfloat16)
+    contracted = run_mlp(padded_rows_in.reshape(row_count, seq_size * padded_rows), mlp_full)
     branch = group_sum(contracted, wgt_size)
     branch = branch.reshape(share_rows, seq_size, padded_rows)[:, :, :block_rows].reshape(
         share_rows, feat_width

time: 297 us -> 287 us (0.966)
  waiting for transfers between devices: 166 us -> 150 us
  blocking collectives: 32.1 us -> 47.4 us
  matrix products: 14.8 us -> 6.83 us
  Pallas kernels: 9.76 us -> 16.3 us
  local copies, waits for them, and re-layouts: 27.4 us -> 23.4 us
  starting transfers between devices: 19.8 us -> 16.3 us
    all_gather x1, waiting for transfers between devices: 38.5 us -> 21.6 us  [body(): mlp_full = lax.all_gather(mlp_local, 'seq', axis=0, tiled=False)]
    all_to_all x0 -> x1, blocking collectives: none -> 15.4 us  [body(): lax.all_to_all(jnp.broadcast_to(branch_in.reshape(1, share_rows, feat_wid...]
    dot_general x1 -> x0, matrix products: 8 us -> none  [body(): lax.dot_general(expanded, contract_rows, (((1,), (1,)), ((), ())), prefer...]
    pallas_call x0 -> x1, Pallas kernels: none -> 6.52 us  [run_mlp(): pl.pallas_call(mlp_kernel, out_shape=jax.ShapeDtypeStruct((rows_in.shape[...]
    slice x1 -> x0, local copies, waits for them, and re-layouts: 4.35 us -> none  [body(): contract_rows = mlp_full[:, 1].reshape(seq_size * padded_rows, -1)]
    all_to_all x1 -> x0, starting transfers between devices: 3.54 us -> none  [body(): lax.all_to_all(jnp.broadcast_to(branch_in.reshape(1, share_rows, feat_wid...]
  transfers between devices with their start and end apart: 7 -> 6, of which waited for: 6 -> 6; matrix products, arithmetic and copies ran while one was open for 10% -> 11% of each run, Pallas kernels for 3% -> 3%
where the time goes in v9:
time: 287 us; the launch traced here: 286 us
  waiting for transfers between devices  150 us (52%)
  blocking collectives  47.4 us (17%)
  local copies, waits for them, and re-layouts  23.4 us (8%)
  starting transfers between devices  16.3 us (6%)
  Pallas kernels  16.3 us (6%)
  between operations  14.5 us (5%)
  other arithmetic  11.6 us (4%)
  matrix products  6.83 us (2%)
    all_gather x1, waiting for transfers between devices, body(): piece = lax.all_gather(all_weights, 'seq', axis=0, tiled=False)  64 us
    all_gather x1, waiting for transfers between devices, body(): shared_piece = lax.all_gather(shared, 'seq', axis=0, tiled=False)  35.1 us
    all_gather x1, blocking collectives, body(): out_full = lax.all_gather(out_weight, 'seq', axis=1, tiled=True)  32.1 us
    all_to_all x2, waiting for transfers between devices, group_sum(): swapped = lax.all_to_all(partial, 'wgt', 0, 0, tiled=True)  25.8 us
    all_gather x1, waiting for transfers between devices, body(): mlp_full = lax.all_gather(mlp_local, 'seq', axis=0, tiled=False)  21.6 us
    all_to_all x1, blocking collectives, body(): lax.all_to_all(jnp.broadcast_to(branch_in.reshape(1, share_rows, feat_wid...  15.4 us
    all_to_all x2, starting transfers between devices, group_sum(): swapped = lax.all_to_all(partial, 'wgt', 0, 0, tiled=True)  13.8 us
    pallas_call x1, Pallas kernels, run(): pl.pallas_call(kernel, out_shape=jax.ShapeDtypeStruct(q.shape, jnp.bfloat...  9.76 us
  transfers between devices with their start and end apart: 6, of which 6 were waited for; matrix products, arithmetic and copies ran while one was open for 11% of the time, Pallas kernels for 3%

profile of v9, /device:TPU:32, one launch (start us, length us, event | category | flops | bytes accessed | tf_op | source)
XLA Modules:
  0.0 286.0 jit_solution(9812775910410051806)
XLA Ops:
  7.2 1.0 copy.79
  8.2 0.9 maximum_bitcast_fusion.1
  11.7 1.5 mul.291
  14.2 0.8 div.51
  15.0 1.3 fusion.1
  16.8 1.3 fusion.26
  18.1 1.6 add_convert_fusion
  19.8 4.0 %reshape.335 = bf16[32,76,144]{1,0,2:T(8,128)(2,1)S(1)} reshape(bf16[2432,144]{0,1:T(8,128)(2,1)S(1)} %maximum_bitcast_fusion) | data formatting | bytes 1400832 | tf_op jit(solution)/shard_map/reshape | solution.py:174
  23.8 1.5 copy.78
  25.5 64.0 %all-gather.8.cloned.1.call-done = bf16[2560,960]{1,0:T(8,128)(2,1)} async-done(((bf16[80,960]{1,0:T(8,128)(2,1)}), bf16[2560,960]{1,0:T(8,128)(2,1)}) %all-gather.8.cloned.1.call-update) | async-done | bytes 4915216 | tf_op jit(solution)/shard_map/all_gather | solution.py:164
  89.5 3.9 %convolution_bitcast_fusion = f32[144,960]{1,0:T(8,128)S(1)} fusion(bf16[32,80,960]{2,1,0:T(8,128)(2,1)} %bitcast.132, bf16[32,76,144]{1,2,0:T(8,128)(2,1)} %copy.78), kind=kOutput, calls=%fused_computation.2 | convolution fusion | flops 707788800 | bytes 6168576 | tf_op jit(solution)/shard_map/sdr,sdn->rn/dot_general | solution.py:177
  95.9 0.8 fusion.20
  96.8 0.7 fusion.10
  97.7 32.1 %all-gather.3 = bf16[32,76,192]{2,1,0:T(8,128)(2,1)S(1)} all-gather(bf16[1,76,192]{2,1,0:T(8,128)(2,1)S(1)} %bitcast.130), channel_id=1, replica_groups=mesh['cfg'=2,'seq'=32,'wgt'=8] {'seq'}, dimensions={0}, use_global_device_ids=true | all-gather | bytes 963072 | tf_op jit(solution)/shard_map/all_gather | solution.py:170
  129.7 1.3 reshape.352
  133.0 35.1 %all-gather.10.cloned.1.call-done = bf16[9728,256]{1,0:T(8,128)(2,1)} async-done(((bf16[304,256]{1,0:T(8,128)(2,1)}), bf16[9728,256]{1,0:T(8,128)(2,1)}) %all-gather.10.cloned.1.call-update) | async-done | bytes 4980752 | tf_op jit(solution)/shard_map/all_gather | solution.py:212
  168.1 0.9 fusion.32
  169.7 9.8 %shard_map.140 = bf16[4,32,256]{2,1,0:T(8,128)(2,1)} custom-call(bf16[4,32,256]{2,1,0:T(8,128)(2,1)} %pad.34.q_ref, bf16[32,304,256]{2,1,0:T(8,128)(2,1)} %bitcast.117, f32[4,512]{1,0:T(4,128)} %fusion.36.mask_ref), custom_call_target="tpu_custom_call" | custom-call | tf_op jit(solution)/shard_map/pallas_call | solution.py:87
  179.5 0.8 slice_bitcast_fusion.1
  180.5 1.4 convolution_convert_fusion
  181.9 7.0 %all-to-all-start = ((bf16[8,16,2432]{2,1,0:T(8,128)(2,1)}), bf16[8,16,2432]{2,1,0:T(8,128)(2,1)S(1)}, u32[]{:S(2)}, u32[]{:S(2)}) async-start(bf16[8,16,2432]{2,1,0:T(8,128)(2,1)} %bitcast.28), calls=%async_computation | async-start | bytes 1245184 | tf_op jit(solution)/shard_map/all_to_all | solution.py:41
  189.2 12.7 %all-to-all-done = bf16[8,16,2432]{2,1,0:T(8,128)(2,1)S(1)} async-done(((bf16[8,16,2432]{2,1,0:T(8,128)(2,1)}), bf16[8,16,2432]{2,1,0:T(8,128)(2,1)S(1)}, u32[]{:S(2)}, u32[]{:S(2)}) %all-to-all-start) | async-done | bytes 622624 | tf_op jit(solution)/shard_map/all_to_all | solution.py:41
  202.5 15.4 %all_to_all.23 = bf16[8,16,2432]{2,1,0:T(8,128)(2,1)S(1)} all-to-all(bf16[8,16,2432]{2,1,0:T(8,128)(2,1)S(1)} %broadcast_in_dim.8), channel_id=1, replica_groups=mesh['cfg'=2,'seq'=32,'wgt'=8] {'wgt'}, dimensions={0} | all-to-all | bytes 1245184 | tf_op jit(solution)/shard_map/all_to_all | solution.py:241
  217.9 3.5 %reshape_reshape.6 = bf16[128,32,76]{2,1,0:T(8,128)(2,1)S(1)} reshape(bf16[8,16,2432]{2,1,0:T(8,128)(2,1)S(1)} %all_to_all.23) | data formatting | bytes 1245184 | tf_op jit(solution)/shard_map/reshape;reshape | solution.py:251
  221.5 1.1 copy.103
  222.6 1.1 copy.101.x_ref
  223.7 21.6 %all-gather.12.cloned.1.call-done = bf16[64,80,704]{2,1,0:T(8,128)(2,1)} async-done(((bf16[2,80,704]{2,1,0:T(8,128)(2,1)}), bf16[64,80,704]{2,1,0:T(8,128)(2,1)}) %all-gather.12.cloned.1.call-update) | async-done | bytes 7208976 | tf_op jit(solution)/shard_map/all_gather | solution.py:169
  245.4 6.5 %shard_map.141 = bf16[128,2560]{1,0:T(8,128)(2,1)} custom-call(bf16[128,2560]{1,0:T(8,128)(2,1)} %copy.101.x_ref, bf16[32,2,80,704]{3,2,1,0:T(8,128)(2,1)} %bitcast.115), custom_call_target="tpu_custom_call" | custom-call | tf_op jit(solution)/shard_map/pallas_call | solution.py:110
  251.9 6.8 %all-to-all-start.2 = ((bf16[8,16,2560]{2,1,0:T(8,128)(2,1)}), bf16[8,16,2560]{2,1,0:T(8,128)(2,1)S(1)}, u32[]{:S(2)}, u32[]{:S(2)}) async-start(bf16[8,16,2560]{2,1,0:T(8,128)(2,1)} %bitcast.118), calls=%async_computation.2 | async-start | bytes 1310720 | tf_op jit(solution)/shard_map/all_to_all | solution.py:41
  259.0 13.1 %all-to-all-done.2 = bf16[8,16,2560]{2,1,0:T(8,128)(2,1)S(1)} async-done(((bf16[8,16,2560]{2,1,0:T(8,128)(2,1)}), bf16[8,16,2560]{2,1,0:T(8,128)(2,1)S(1)}, u32[]{:S(2)}, u32[]{:S(2)}) %all-to-all-start.2) | async-done | bytes 655392 | tf_op jit(solution)/shard_map/all_to_all | solution.py:41
  273.3 2.3 collective-permute-start
  275.7 3.1 %collective-permute-done = f32[4,2,64]{2,1,0:T(2,128)S(1)} collective-permute-done((f32[4,2,64]{2,1,0:T(2,128)S(1)}, f32[4,2,64]{2,1,0:T(2,128)S(1)}, u32[]{:S(2)}, u32[]{:S(2)}) %collective-permute-start) | collective-permute-done | bytes 2080 | tf_op jit(solution)/shard_map/ppermute | solution.py:20
  (149 shorter events, 12.6 us)
Async XLA Ops:
  7.2 265.9 %copy-start = (bf16[2432,64]{0,1:T(8,128)(2,1)S(1)}, bf16[2432,64]{0,1:T(8,128)(2,1)}, u32[]{:S(2)}) copy-start(bf16[2432,64]{0,1:T(8,128)(2,1)} %param.25) | copy-start | bytes 933892
  7.2 3.0 %copy-start.4 = (f32[1,4,10,2432]{3,1,2,0:T(4,128)S(1)}, f32[1,4,10,2432]{3,1,2,0:T(4,128)}, u32[]{:S(2)}) copy-start(f32[1,4,10,2432]{3,1,2,0:T(4,128)} %param.18) | copy-start | bytes 1167364
  7.2 82.3 %all-gather.8.cloned.1.call-start = ((), (), s32[]{:S(2)}) async-start(), calls=%async_computation.3 | async-start | bytes 5406720 | tf_op jit(solution)/shard_map/all_gather | solution.py:164
  10.1 158.0 %all-gather.10.cloned.1.call-start = ((), (), s32[]{:S(2)}) async-start(), calls=%async_computation.4 | async-start | bytes 5136384 | tf_op jit(solution)/shard_map/all_gather | solution.py:212
  11.7 1.5 copy-start.1
  13.2 3.2 %copy-start.3 = (bf16[1,16,2432]{2,1,0:T(8,128)(2,1)S(1)}, bf16[1,16,2432]{2,1,0:T(8,128)(2,1)}, u32[]{:S(2)}) copy-start(bf16[1,16,2432]{2,1,0:T(8,128)(2,1)} %param.15) | copy-start | bytes 233476
  13.3 3.5 %copy-start.15 = (s32[1,16]{1,0:T(1,128)S(1)}, s32[1,16]{1,0:T(1,128)}, u32[]{:S(2)}) copy-start(s32[1,16]{1,0:T(1,128)} %param.16) | copy-start | bytes 196
  23.8 1.5 copy-start.14
  94.9 1.9 copy-start.10
  94.9 1.9 copy-start.11
  95.3 2.3 copy-start.12
  96.7 148.6 %all-gather.12.cloned.1.call-start = ((), (), s32[]{:S(2)}) async-start(), calls=%async_computation.5 | async-start | bytes 8110080 | tf_op jit(solution)/shard_map/all_gather | solution.py:169
  169.7 10.7 %copy-start.2 = (bf16[2432,192]{1,0:T(8,128)(2,1)S(1)}, bf16[2432,192]{1,0:T(8,128)(2,1)}, u32[]{:S(2)}) copy-start(bf16[2432,192]{1,0:T(8,128)(2,1)} %reshape.352) | copy-start | bytes 2801668
  180.5 8.4 %copy-start.9 = (f32[4,2432]{1,0:T(4,128)S(1)}, f32[4,2432]{1,0:T(4,128)}, u32[]{:S(2)}) copy-start(f32[4,2432]{1,0:T(4,128)} %get-tuple-element.19) | copy-start | bytes 116740
  181.9 7.1 %copy-start.8 = (f32[4,2432]{1,0:T(4,128)S(1)}, f32[4,2432]{1,0:T(4,128)}, u32[]{:S(2)}) copy-start(f32[4,2432]{1,0:T(4,128)} %get-tuple-element.15) | copy-start | bytes 116740
  181.9 7.2 %copy-start.7 = (f32[4,2432]{1,0:T(4,128)S(1)}, f32[4,2432]{1,0:T(4,128)}, u32[]{:S(2)}) copy-start(f32[4,2432]{1,0:T(4,128)} %get-tuple-element.12) | copy-start | bytes 116740
  181.9 20.0 %all-to-all-start = ((bf16[8,16,2432]{2,1,0:T(8,128)(2,1)}), bf16[8,16,2432]{2,1,0:T(8,128)(2,1)S(1)}, u32[]{:S(2)}, u32[]{:S(2)}) async-start(bf16[8,16,2432]{2,1,0:T(8,128)(2,1)} %bitcast.28), calls=%async_computation | async-start | bytes 1245184 | tf_op jit(solution)/shard_map/all_to_all | solution.py:41
  251.9 6.8 %copy-start.6 = (f32[4,2432]{1,0:T(4,128)S(1)}, f32[4,2432]{1,0:T(4,128)}, u32[]{:S(2)}) copy-start(f32[4,2432]{1,0:T(4,128)} %get-tuple-element.16) | copy-start | bytes 116740
  251.9 6.9 %copy-start.5 = (f32[4,2432]{1,0:T(4,128)S(1)}, f32[4,2432]{1,0:T(4,128)}, u32[]{:S(2)}) copy-start(f32[4,2432]{1,0:T(4,128)} %get-tuple-element.13) | copy-start | bytes 116740
  251.9 20.2 %all-to-all-start.2 = ((bf16[8,16,2560]{2,1,0:T(8,128)(2,1)}), bf16[8,16,2560]{2,1,0:T(8,128)(2,1)S(1)}, u32[]{:S(2)}, u32[]{:S(2)}) async-start(bf16[8,16,2560]{2,1,0:T(8,128)(2,1)} %bitcast.118), calls=%async_computation.2 | async-start | bytes 1310720 | tf_op jit(solution)/shard_map/all_to_all | solution.py:41
  272.3 3.3 %copy-start.16 = (s32[4]{0:T(128)S(1)}, s32[4]{0:T(128)}, u32[]{:S(2)}) copy-start(s32[4]{0:T(128)} %param.17) | copy-start | bytes 52
  272.4 6.4 %copy-start.13 = (f32[4,2,64]{2,1,0:T(2,128)S(1)}, f32[4,2,64]{2,1,0:T(2,128)}, u32[]{:S(2)}) copy-start(f32[4,2,64]{2,1,0:T(2,128)} %param.13) | copy-start | bytes 6148
  273.3 5.5 %collective-permute-start = (f32[4,2,64]{2,1,0:T(2,128)S(1)}, f32[4,2,64]{2,1,0:T(2,128)S(1)}, u32[]{:S(2)}, u32[]{:S(2)}) collective-permute-start(f32[4,2,64]{2,1,0:T(2,128)S(1)} %constant_dynamic-slice_fusion), channel_id=1, source_target_pairs={{0,256},{256,0},{1,257},{257,1},{2,258},{258,2},{3,259},{259,3},{4... | collective-permute-start | bytes 6152 | tf_op jit(solution)/shard_map/ppermute | solution.py:20
Sparse Core Ops, SparseCore 0:
  10.3 79.1 all-gather.7
  96.8 71.2 all-gather.9
  170.3 75.0 all-gather.11

commit v10 on v9

--- a/solution.py
+++ b/solution.py
@@ -94,24 +94,35 @@
     return run
 
 
-def mlp_kernel(x_ref, w_ref, o_ref):
-    blocks, _, rows, units = w_ref.shape
-    expand = w_ref[:, 0].reshape(blocks * rows, units)
+def mlp_kernel(x_ref, w_hbm, o_ref, expand_buf, contract_buf, sems):
+    blocks, rows, units = expand_buf.shape
+    expand_copy = pltpu.make_async_copy(w_hbm.at[:, 0], expand_buf, sems.at[0])
+    contract_copy = pltpu.make_async_copy(w_hbm.at[:, 1], contract_buf, sems.at[1])
+    expand_copy.start()
+    contract_copy.start()
+    expand_copy.wait()
+    expand = expand_buf[...].reshape(blocks * rows, units)
     grown = jnp.dot(x_ref[...], expand, preferred_element_type=jnp.float32)
     grown = jax.nn.gelu(grown, approximate=True).astype(jnp.bfloat16)
-    contract = w_ref[:, 1].reshape(blocks * rows, units)
+    contract_copy.wait()
+    contract = contract_buf[...].reshape(blocks * rows, units)
     o_ref[...] = lax.dot_general(
         grown, contract, (((1,), (1,)), ((), ())), preferred_element_type=jnp.float32
     ).astype(o_ref.dtype)
 
 
 def run_mlp(rows_in, weights):
-    blocks, _, rows, _ = weights.shape
+    blocks, _, rows, units = weights.shape
     return pl.pallas_call(
         mlp_kernel,
         out_shape=jax.ShapeDtypeStruct((rows_in.shape[0], blocks * rows), jnp.bfloat16),
-        in_specs=[pl.BlockSpec(memory_space=pltpu.VMEM)] * 2,
+        in_specs=[pl.BlockSpec(memory_space=pltpu.VMEM), pl.BlockSpec(memory_space=pl.ANY)],
         out_specs=pl.BlockSpec(memory_space=pltpu.VMEM),
+        scratch_shapes=[
+            pltpu.VMEM((blocks, rows, units), weights.dtype),
+            pltpu.VMEM((blocks, rows, units), weights.dtype),
+            pltpu.SemaphoreType.DMA((2,)),
+        ],
     )(rows_in, weights)
 
 

time: 287 us -> 287 us (level)
  no operation moved by 1% of the time
where the time goes in v10:
time: 287 us; the launch traced here: 286 us
  waiting for transfers between devices  150 us (52%)
  blocking collectives  47.4 us (17%)
  local copies, waits for them, and re-layouts  23.4 us (8%)
  Pallas kernels  16.6 us (6%)
  starting transfers between devices  16.3 us (6%)
  between operations  14.5 us (5%)
  other arithmetic  11.6 us (4%)
  matrix products  6.83 us (2%)
    all_gather x1, waiting for transfers between devices, body(): piece = lax.all_gather(all_weights, 'seq', axis=0, tiled=False)  64 us
    all_gather x1, waiting for transfers between devices, body(): shared_piece = lax.all_gather(shared, 'seq', axis=0, tiled=False)  35.1 us
    all_gather x1, blocking collectives, body(): out_full = lax.all_gather(out_weight, 'seq', axis=1, tiled=True)  32.1 us
    all_to_all x2, waiting for transfers between devices, group_sum(): swapped = lax.all_to_all(partial, 'wgt', 0, 0, tiled=True)  25.8 us
    all_gather x1, waiting for transfers between devices, body(): mlp_full = lax.all_gather(mlp_local, 'seq', axis=0, tiled=False)  21.6 us
    all_to_all x1, blocking collectives, body(): lax.all_to_all(jnp.broadcast_to(branch_in.reshape(1, share_rows, feat_wid...  15.4 us
    all_to_all x2, starting transfers between devices, group_sum(): swapped = lax.all_to_all(partial, 'wgt', 0, 0, tiled=True)  13.8 us
    pallas_call x1, Pallas kernels, run(): pl.pallas_call(kernel, out_shape=jax.ShapeDtypeStruct(q.shape, jnp.bfloat...  9.76 us
  transfers between devices with their start and end apart: 6, of which 6 were waited for; matrix products, arithmetic and copies ran while one was open for 11% of the time, Pallas kernels for 3%

profile of v10, /device:TPU:32, one launch (start us, length us, event | category | flops | bytes accessed | tf_op | source)
XLA Modules:
  0.0 286.4 jit_solution(12019425849055037657)
XLA Ops:
  7.2 1.0 copy.79
  8.2 0.9 maximum_bitcast_fusion.1
  11.7 1.5 mul.291
  14.2 0.8 div.51
  15.0 1.3 fusion.1
  16.8 1.3 fusion.26
  18.1 1.6 add_convert_fusion
  19.8 4.0 %reshape.335 = bf16[32,76,144]{1,0,2:T(8,128)(2,1)S(1)} reshape(bf16[2432,144]{0,1:T(8,128)(2,1)S(1)} %maximum_bitcast_fusion) | data formatting | bytes 1400832 | tf_op jit(solution)/shard_map/reshape | solution.py:185
  23.8 1.5 copy.78
  25.5 64.0 %all-gather.8.cloned.1.call-done = bf16[2560,960]{1,0:T(8,128)(2,1)} async-done(((bf16[80,960]{1,0:T(8,128)(2,1)}), bf16[2560,960]{1,0:T(8,128)(2,1)}) %all-gather.8.cloned.1.call-update) | async-done | bytes 4915216 | tf_op jit(solution)/shard_map/all_gather | solution.py:175
  89.5 3.9 %convolution_bitcast_fusion = f32[144,960]{1,0:T(8,128)S(1)} fusion(bf16[32,80,960]{2,1,0:T(8,128)(2,1)} %bitcast.132, bf16[32,76,144]{1,2,0:T(8,128)(2,1)} %copy.78), kind=kOutput, calls=%fused_computation.2 | convolution fusion | flops 707788800 | bytes 6168576 | tf_op jit(solution)/shard_map/sdr,sdn->rn/dot_general | solution.py:188
  95.9 0.8 fusion.20
  96.8 0.7 fusion.10
  97.7 32.1 %all-gather.3 = bf16[32,76,192]{2,1,0:T(8,128)(2,1)S(1)} all-gather(bf16[1,76,192]{2,1,0:T(8,128)(2,1)S(1)} %bitcast.130), channel_id=1, replica_groups=mesh['cfg'=2,'seq'=32,'wgt'=8] {'seq'}, dimensions={0}, use_global_device_ids=true | all-gather | bytes 963072 | tf_op jit(solution)/shard_map/all_gather | solution.py:181
  129.7 1.3 reshape.352
  133.0 35.1 %all-gather.10.cloned.1.call-done = bf16[9728,256]{1,0:T(8,128)(2,1)} async-done(((bf16[304,256]{1,0:T(8,128)(2,1)}), bf16[9728,256]{1,0:T(8,128)(2,1)}) %all-gather.10.cloned.1.call-update) | async-done | bytes 4980752 | tf_op jit(solution)/shard_map/all_gather | solution.py:223
  168.1 0.9 fusion.32
  169.7 9.8 %shard_map.140 = bf16[4,32,256]{2,1,0:T(8,128)(2,1)} custom-call(bf16[4,32,256]{2,1,0:T(8,128)(2,1)} %pad.34.q_ref, bf16[32,304,256]{2,1,0:T(8,128)(2,1)} %bitcast.117, f32[4,512]{1,0:T(4,128)} %fusion.36.mask_ref), custom_call_target="tpu_custom_call" | custom-call | tf_op jit(solution)/shard_map/pallas_call | solution.py:87
  179.5 0.8 slice_bitcast_fusion.1
  180.5 1.4 convolution_convert_fusion
  181.9 7.0 %all-to-all-start = ((bf16[8,16,2432]{2,1,0:T(8,128)(2,1)}), bf16[8,16,2432]{2,1,0:T(8,128)(2,1)S(1)}, u32[]{:S(2)}, u32[]{:S(2)}) async-start(bf16[8,16,2432]{2,1,0:T(8,128)(2,1)} %bitcast.28), calls=%async_computation | async-start | bytes 1245184 | tf_op jit(solution)/shard_map/all_to_all | solution.py:41
  189.2 12.7 %all-to-all-done = bf16[8,16,2432]{2,1,0:T(8,128)(2,1)S(1)} async-done(((bf16[8,16,2432]{2,1,0:T(8,128)(2,1)}), bf16[8,16,2432]{2,1,0:T(8,128)(2,1)S(1)}, u32[]{:S(2)}, u32[]{:S(2)}) %all-to-all-start) | async-done | bytes 622624 | tf_op jit(solution)/shard_map/all_to_all | solution.py:41
  202.5 15.4 %all_to_all.23 = bf16[8,16,2432]{2,1,0:T(8,128)(2,1)S(1)} all-to-all(bf16[8,16,2432]{2,1,0:T(8,128)(2,1)S(1)} %broadcast_in_dim.8), channel_id=1, replica_groups=mesh['cfg'=2,'seq'=32,'wgt'=8] {'wgt'}, dimensions={0} | all-to-all | bytes 1245184 | tf_op jit(solution)/shard_map/all_to_all | solution.py:252
  217.9 3.5 %reshape_reshape.6 = bf16[128,32,76]{2,1,0:T(8,128)(2,1)S(1)} reshape(bf16[8,16,2432]{2,1,0:T(8,128)(2,1)S(1)} %all_to_all.23) | data formatting | bytes 1245184 | tf_op jit(solution)/shard_map/reshape;reshape | solution.py:262
  221.5 1.1 copy.103
  222.6 1.1 copy.101.x_ref
  223.7 21.6 %all-gather.12.cloned.1.call-done = bf16[64,80,704]{2,1,0:T(8,128)(2,1)} async-done(((bf16[2,80,704]{2,1,0:T(8,128)(2,1)}), bf16[64,80,704]{2,1,0:T(8,128)(2,1)}) %all-gather.12.cloned.1.call-update) | async-done | bytes 7208976 | tf_op jit(solution)/shard_map/all_gather | solution.py:180
  245.4 6.9 %shard_map.141 = bf16[128,2560]{1,0:T(8,128)(2,1)} custom-call(bf16[128,2560]{1,0:T(8,128)(2,1)} %copy.101.x_ref, bf16[32,2,80,704]{3,2,1,0:T(8,128)(2,1)} %bitcast.115), custom_call_target="tpu_custom_call" | custom-call | tf_op jit(solution)/shard_map/pallas_call | solution.py:116
  252.2 6.8 %all-to-all-start.2 = ((bf16[8,16,2560]{2,1,0:T(8,128)(2,1)}), bf16[8,16,2560]{2,1,0:T(8,128)(2,1)S(1)}, u32[]{:S(2)}, u32[]{:S(2)}) async-start(bf16[8,16,2560]{2,1,0:T(8,128)(2,1)} %bitcast.118), calls=%async_computation.2 | async-start | bytes 1310720 | tf_op jit(solution)/shard_map/all_to_all | solution.py:41
  259.4 13.1 %all-to-all-done.2 = bf16[8,16,2560]{2,1,0:T(8,128)(2,1)S(1)} async-done(((bf16[8,16,2560]{2,1,0:T(8,128)(2,1)}), bf16[8,16,2560]{2,1,0:T(8,128)(2,1)S(1)}, u32[]{:S(2)}, u32[]{:S(2)}) %all-to-all-start.2) | async-done | bytes 655392 | tf_op jit(solution)/shard_map/all_to_all | solution.py:41
  273.7 2.3 collective-permute-start
  276.1 3.1 %collective-permute-done = f32[4,2,64]{2,1,0:T(2,128)S(1)} collective-permute-done((f32[4,2,64]{2,1,0:T(2,128)S(1)}, f32[4,2,64]{2,1,0:T(2,128)S(1)}, u32[]{:S(2)}, u32[]{:S(2)}) %collective-permute-start) | collective-permute-done | bytes 2080 | tf_op jit(solution)/shard_map/ppermute | solution.py:20
  (149 shorter events, 12.6 us)
Async XLA Ops:
  7.2 266.3 %copy-start = (bf16[2432,64]{0,1:T(8,128)(2,1)S(1)}, bf16[2432,64]{0,1:T(8,128)(2,1)}, u32[]{:S(2)}) copy-start(bf16[2432,64]{0,1:T(8,128)(2,1)} %param.25) | copy-start | bytes 933892
  7.2 3.0 %copy-start.4 = (f32[1,4,10,2432]{3,1,2,0:T(4,128)S(1)}, f32[1,4,10,2432]{3,1,2,0:T(4,128)}, u32[]{:S(2)}) copy-start(f32[1,4,10,2432]{3,1,2,0:T(4,128)} %param.18) | copy-start | bytes 1167364
  7.2 82.3 %all-gather.8.cloned.1.call-start = ((), (), s32[]{:S(2)}) async-start(), calls=%async_computation.3 | async-start | bytes 5406720 | tf_op jit(solution)/shard_map/all_gather | solution.py:175
  10.1 158.0 %all-gather.10.cloned.1.call-start = ((), (), s32[]{:S(2)}) async-start(), calls=%async_computation.4 | async-start | bytes 5136384 | tf_op jit(solution)/shard_map/all_gather | solution.py:223
  11.7 1.5 copy-start.1
  13.2 3.2 %copy-start.3 = (bf16[1,16,2432]{2,1,0:T(8,128)(2,1)S(1)}, bf16[1,16,2432]{2,1,0:T(8,128)(2,1)}, u32[]{:S(2)}) copy-start(bf16[1,16,2432]{2,1,0:T(8,128)(2,1)} %param.15) | copy-start | bytes 233476
  13.3 3.5 %copy-start.15 = (s32[1,16]{1,0:T(1,128)S(1)}, s32[1,16]{1,0:T(1,128)}, u32[]{:S(2)}) copy-start(s32[1,16]{1,0:T(1,128)} %param.16) | copy-start | bytes 196
  23.8 1.5 copy-start.14
  94.9 1.9 copy-start.10
  94.9 1.9 copy-start.11
  95.3 2.3 copy-start.12
  96.7 148.6 %all-gather.12.cloned.1.call-start = ((), (), s32[]{:S(2)}) async-start(), calls=%async_computation.5 | async-start | bytes 8110080 | tf_op jit(solution)/shard_map/all_gather | solution.py:180
  169.7 10.7 %copy-start.2 = (bf16[2432,192]{1,0:T(8,128)(2,1)S(1)}, bf16[2432,192]{1,0:T(8,128)(2,1)}, u32[]{:S(2)}) copy-start(bf16[2432,192]{1,0:T(8,128)(2,1)} %reshape.352) | copy-start | bytes 2801668
  180.5 8.4 %copy-start.9 = (f32[4,2432]{1,0:T(4,128)S(1)}, f32[4,2432]{1,0:T(4,128)}, u32[]{:S(2)}) copy-start(f32[4,2432]{1,0:T(4,128)} %get-tuple-element.19) | copy-start | bytes 116740
  181.9 7.1 %copy-start.8 = (f32[4,2432]{1,0:T(4,128)S(1)}, f32[4,2432]{1,0:T(4,128)}, u32[]{:S(2)}) copy-start(f32[4,2432]{1,0:T(4,128)} %get-tuple-element.15) | copy-start | bytes 116740
  181.9 7.2 %copy-start.7 = (f32[4,2432]{1,0:T(4,128)S(1)}, f32[4,2432]{1,0:T(4,128)}, u32[]{:S(2)}) copy-start(f32[4,2432]{1,0:T(4,128)} %get-tuple-element.12) | copy-start | bytes 116740
  181.9 20.0 %all-to-all-start = ((bf16[8,16,2432]{2,1,0:T(8,128)(2,1)}), bf16[8,16,2432]{2,1,0:T(8,128)(2,1)S(1)}, u32[]{:S(2)}, u32[]{:S(2)}) async-start(bf16[8,16,2432]{2,1,0:T(8,128)(2,1)} %bitcast.28), calls=%async_computation | async-start | bytes 1245184 | tf_op jit(solution)/shard_map/all_to_all | solution.py:41
  252.2 6.9 %copy-start.6 = (f32[4,2432]{1,0:T(4,128)S(1)}, f32[4,2432]{1,0:T(4,128)}, u32[]{:S(2)}) copy-start(f32[4,2432]{1,0:T(4,128)} %get-tuple-element.16) | copy-start | bytes 116740
  252.2 6.9 %copy-start.5 = (f32[4,2432]{1,0:T(4,128)S(1)}, f32[4,2432]{1,0:T(4,128)}, u32[]{:S(2)}) copy-start(f32[4,2432]{1,0:T(4,128)} %get-tuple-element.13) | copy-start | bytes 116740
  252.2 20.2 %all-to-all-start.2 = ((bf16[8,16,2560]{2,1,0:T(8,128)(2,1)}), bf16[8,16,2560]{2,1,0:T(8,128)(2,1)S(1)}, u32[]{:S(2)}, u32[]{:S(2)}) async-start(bf16[8,16,2560]{2,1,0:T(8,128)(2,1)} %bitcast.118), calls=%async_computation.2 | async-start | bytes 1310720 | tf_op jit(solution)/shard_map/all_to_all | solution.py:41
  272.7 3.3 %copy-start.16 = (s32[4]{0:T(128)S(1)}, s32[4]{0:T(128)}, u32[]{:S(2)}) copy-start(s32[4]{0:T(128)} %param.17) | copy-start | bytes 52
  272.7 6.4 %copy-start.13 = (f32[4,2,64]{2,1,0:T(2,128)S(1)}, f32[4,2,64]{2,1,0:T(2,128)}, u32[]{:S(2)}) copy-start(f32[4,2,64]{2,1,0:T(2,128)} %param.13) | copy-start | bytes 6148
  273.7 5.5 %collective-permute-start = (f32[4,2,64]{2,1,0:T(2,128)S(1)}, f32[4,2,64]{2,1,0:T(2,128)S(1)}, u32[]{:S(2)}, u32[]{:S(2)}) collective-permute-start(f32[4,2,64]{2,1,0:T(2,128)S(1)} %constant_dynamic-slice_fusion), channel_id=1, source_target_pairs={{0,256},{256,0},{1,257},{257,1},{2,258},{258,2},{3,259},{259,3},{4... | collective-permute-start | bytes 6152 | tf_op jit(solution)/shard_map/ppermute | solution.py:20
Sparse Core Ops, SparseCore 0:
  10.3 79.1 all-gather.7
  96.8 71.2 all-gather.9
  170.3 75.0 all-gather.11

commit v11 on v9

--- a/solution.py
+++ b/solution.py
@@ -158,7 +158,7 @@
     padded_rows = block_rows + (-block_rows) % 8
     kinds = qkv_weight.shape[0] + text_weight.shape[0]
     all_weights = jnp.transpose(
-        jnp.concatenate([qkv_weight, text_weight], axis=0), (1, 0, 2)
+        jnp.concatenate([qkv_weight[1:], text_weight, qkv_weight[:1]], axis=0), (1, 0, 2)
     ).reshape(block_rows, kinds * local_cols)
     all_weights = jnp.pad(all_weights, ((0, padded_rows - block_rows), (0, 0)))
     piece = lax.all_gather(all_weights, "seq", axis=0, tiled=False)
@@ -174,9 +174,14 @@
         both_rows.T.reshape(seq_size, block_rows, both_count),
         ((0, 0), (0, padded_rows - block_rows), (0, 0)),
     )
-    both_term = jnp.einsum(
-        "sdr,sdn->rn", both_cols, piece, preferred_element_type=jnp.float32
-    ).reshape(both_count, kinds, local_cols)
+    split = (kinds - 1) * local_cols
+    kv_term = jnp.einsum(
+        "sdr,sdn->rn", both_cols, piece[:, :, :split], preferred_element_type=jnp.float32
+    )
+    q_term = jnp.einsum(
+        "sdr,sdn->rn", both_cols, piece[:, :, split:], preferred_element_type=jnp.float32
+    )
+    both_term = jnp.concatenate([q_term, kv_term], axis=1).reshape(both_count, kinds, local_cols)
     image_term = both_term[:row_count]
     text_term = both_term[row_count:]
     queries = head_norm(

time: 287 us -> 289 us (level)
  transfers between devices with their start and end apart: 6 -> 6, of which waited for: 6 -> 6; matrix products, arithmetic and copies ran while one was open for 11% -> 10% of each run, Pallas kernels for 3% -> 3%
where the time goes in v11:
time: 289 us
  waiting for transfers between devices  148 us (51%)
  blocking collectives  49 us (17%)
  local copies, waits for them, and re-layouts  24.2 us (8%)
  starting transfers between devices  16.5 us (6%)
  Pallas kernels  16.3 us (6%)
  between operations  14.5 us (5%)
  other arithmetic  12.1 us (4%)
  matrix products  8.19 us (3%)
    all_gather x1, waiting for transfers between devices, body(): piece = lax.all_gather(all_weights, 'seq', axis=0, tiled=False)  64 us
    all_gather x1, blocking collectives, body(): out_full = lax.all_gather(out_weight, 'seq', axis=1, tiled=True)  33.6 us
    all_gather x1, waiting for transfers between devices, body(): shared_piece = lax.all_gather(shared, 'seq', axis=0, tiled=False)  33 us
    all_to_all x2, waiting for transfers between devices, group_sum(): swapped = lax.all_to_all(partial, 'wgt', 0, 0, tiled=True)  25.8 us
    all_gather x1, waiting for transfers between devices, body(): mlp_full = lax.all_gather(mlp_local, 'seq', axis=0, tiled=False)  22 us
    all_to_all x1, blocking collectives, body(): lax.all_to_all(jnp.broadcast_to(branch_in.reshape(1, share_rows, feat_wid...  15.4 us
    all_to_all x2, starting transfers between devices, group_sum(): swapped = lax.all_to_all(partial, 'wgt', 0, 0, tiled=True)  13.9 us
    pallas_call x1, Pallas kernels, run(): pl.pallas_call(kernel, out_shape=jax.ShapeDtypeStruct(q.shape, jnp.bfloat...  9.77 us
  transfers between devices with their start and end apart: 6, of which 6 were waited for; matrix products, arithmetic and copies ran while one was open for 10% of the time, Pallas kernels for 3%

profile of v11, /device:TPU:32, one launch (start us, length us, event | category | flops | bytes accessed | tf_op | source)
XLA Modules:
  0.0 288.6 jit_solution(4646455373692066767)
XLA Ops:
  7.2 1.0 slice.96
  8.2 0.8 slice.97
  9.1 1.2 maximum_bitcast_fusion.1
  12.7 1.5 mul.291
  15.3 0.8 div.51
  16.1 1.3 fusion.5
  17.8 1.3 fusion.38
  19.2 1.6 add_convert_fusion
  20.8 4.0 %reshape.335 = bf16[32,76,144]{1,0,2:T(8,128)(2,1)S(1)} reshape(bf16[2432,144]{0,1:T(8,128)(2,1)S(1)} %maximum_bitcast_fusion) | data formatting | bytes 1400832 | tf_op jit(solution)/shard_map/reshape | solution.py:174
  24.8 1.5 copy.79
  26.6 64.0 %all-gather.8.cloned.1.call-done = bf16[2560,960]{1,0:T(8,128)(2,1)} async-done(((bf16[80,960]{1,0:T(8,128)(2,1)}), bf16[2560,960]{1,0:T(8,128)(2,1)}) %all-gather.8.cloned.1.call-update) | async-done | bytes 4915216 | tf_op jit(solution)/shard_map/all_gather | solution.py:164
  90.6 3.5 %fusion.6 = f32[144,768]{1,0:T(8,128)S(1)} fusion(bf16[32,80,960]{2,1,0:T(8,128)(2,1)} %bitcast.133, bf16[32,76,144]{1,2,0:T(8,128)(2,1)} %copy.79), kind=kOutput, calls=%fused_computation.11 | convolution fusion | flops 566231040 | bytes 5554176 | tf_op jit(solution)/shard_map/sdr,sdn->rn/dot_general | solution.py:178
  94.0 1.8 fusion.9
  100.3 33.6 %all-gather.3 = bf16[32,76,192]{2,1,0:T(8,128)(2,1)S(1)} all-gather(bf16[1,76,192]{2,1,0:T(8,128)(2,1)S(1)} %bitcast.131), channel_id=1, replica_groups=mesh['cfg'=2,'seq'=32,'wgt'=8] {'seq'}, dimensions={0}, use_global_device_ids=true | all-gather | bytes 963072 | tf_op jit(solution)/shard_map/all_gather | solution.py:170
  133.9 1.3 reshape.353
  137.2 33.0 %all-gather.10.cloned.1.call-done = bf16[9728,256]{1,0:T(8,128)(2,1)} async-done(((bf16[304,256]{1,0:T(8,128)(2,1)}), bf16[9728,256]{1,0:T(8,128)(2,1)}) %all-gather.10.cloned.1.call-update) | async-done | bytes 4980752 | tf_op jit(solution)/shard_map/all_gather | solution.py:217
  170.3 0.9 fusion.44
  171.9 9.8 %shard_map.140 = bf16[4,32,256]{2,1,0:T(8,128)(2,1)} custom-call(bf16[4,32,256]{2,1,0:T(8,128)(2,1)} %pad.34.q_ref, bf16[32,304,256]{2,1,0:T(8,128)(2,1)} %bitcast.118, f32[4,512]{1,0:T(4,128)} %fusion.48.mask_ref), custom_call_target="tpu_custom_call" | custom-call | tf_op jit(solution)/shard_map/pallas_call | solution.py:87
  181.7 0.8 slice_bitcast_fusion.1
  182.6 1.4 convolution_convert_fusion
  184.1 7.0 %all-to-all-start = ((bf16[8,16,2432]{2,1,0:T(8,128)(2,1)}), bf16[8,16,2432]{2,1,0:T(8,128)(2,1)S(1)}, u32[]{:S(2)}, u32[]{:S(2)}) async-start(bf16[8,16,2432]{2,1,0:T(8,128)(2,1)} %bitcast.29), calls=%async_computation | async-start | bytes 1245184 | tf_op jit(solution)/shard_map/all_to_all | solution.py:41
  191.4 12.7 %all-to-all-done = bf16[8,16,2432]{2,1,0:T(8,128)(2,1)S(1)} async-done(((bf16[8,16,2432]{2,1,0:T(8,128)(2,1)}), bf16[8,16,2432]{2,1,0:T(8,128)(2,1)S(1)}, u32[]{:S(2)}, u32[]{:S(2)}) %all-to-all-start) | async-done | bytes 622624 | tf_op jit(solution)/shard_map/all_to_all | solution.py:41
  204.7 15.4 %all_to_all.23 = bf16[8,16,2432]{2,1,0:T(8,128)(2,1)S(1)} all-to-all(bf16[8,16,2432]{2,1,0:T(8,128)(2,1)S(1)} %broadcast_in_dim.8), channel_id=1, replica_groups=mesh['cfg'=2,'seq'=32,'wgt'=8] {'wgt'}, dimensions={0} | all-to-all | bytes 1245184 | tf_op jit(solution)/shard_map/all_to_all | solution.py:246
  220.1 3.5 %reshape_reshape.6 = bf16[128,32,76]{2,1,0:T(8,128)(2,1)S(1)} reshape(bf16[8,16,2432]{2,1,0:T(8,128)(2,1)S(1)} %all_to_all.23) | data formatting | bytes 1245184 | tf_op jit(solution)/shard_map/reshape;reshape | solution.py:256
  223.6 1.1 copy.106
  224.8 1.1 copy.102.x_ref
  225.9 22.0 %all-gather.12.cloned.1.call-done = bf16[64,80,704]{2,1,0:T(8,128)(2,1)} async-done(((bf16[2,80,704]{2,1,0:T(8,128)(2,1)}), bf16[64,80,704]{2,1,0:T(8,128)(2,1)}) %all-gather.12.cloned.1.call-update) | async-done | bytes 7208976 | tf_op jit(solution)/shard_map/all_gather | solution.py:169
  247.8 6.5 %shard_map.141 = bf16[128,2560]{1,0:T(8,128)(2,1)} custom-call(bf16[128,2560]{1,0:T(8,128)(2,1)} %copy.102.x_ref, bf16[32,2,80,704]{3,2,1,0:T(8,128)(2,1)} %bitcast.116), custom_call_target="tpu_custom_call" | custom-call | tf_op jit(solution)/shard_map/pallas_call | solution.py:110
  254.4 6.9 %all-to-all-start.2 = ((bf16[8,16,2560]{2,1,0:T(8,128)(2,1)}), bf16[8,16,2560]{2,1,0:T(8,128)(2,1)S(1)}, u32[]{:S(2)}, u32[]{:S(2)}) async-start(bf16[8,16,2560]{2,1,0:T(8,128)(2,1)} %bitcast.119), calls=%async_computation.2 | async-start | bytes 1310720 | tf_op jit(solution)/shard_map/all_to_all | solution.py:41
  261.6 13.1 %all-to-all-done.2 = bf16[8,16,2560]{2,1,0:T(8,128)(2,1)S(1)} async-done(((bf16[8,16,2560]{2,1,0:T(8,128)(2,1)}), bf16[8,16,2560]{2,1,0:T(8,128)(2,1)S(1)}, u32[]{:S(2)}, u32[]{:S(2)}) %all-to-all-start.2) | async-done | bytes 655392 | tf_op jit(solution)/shard_map/all_to_all | solution.py:41
  275.9 2.5 collective-permute-start
  278.5 2.9 %collective-permute-done = f32[4,2,64]{2,1,0:T(2,128)S(1)} collective-permute-done((f32[4,2,64]{2,1,0:T(2,128)S(1)}, f32[4,2,64]{2,1,0:T(2,128)S(1)}, u32[]{:S(2)}, u32[]{:S(2)}) %collective-permute-start) | collective-permute-done | bytes 2080 | tf_op jit(solution)/shard_map/ppermute | solution.py:20
  (154 shorter events, 14.4 us)
Async XLA Ops:
  7.2 268.5 %copy-start = (bf16[2432,64]{0,1:T(8,128)(2,1)S(1)}, bf16[2432,64]{0,1:T(8,128)(2,1)}, u32[]{:S(2)}) copy-start(bf16[2432,64]{0,1:T(8,128)(2,1)} %param.25) | copy-start | bytes 933892
  7.2 4.1 %copy-start.5 = (f32[1,4,10,2432]{3,1,2,0:T(4,128)S(1)}, f32[1,4,10,2432]{3,1,2,0:T(4,128)}, u32[]{:S(2)}) copy-start(f32[1,4,10,2432]{3,1,2,0:T(4,128)} %param.18) | copy-start | bytes 1167364
  7.2 83.4 %all-gather.8.cloned.1.call-start = ((), (), s32[]{:S(2)}) async-start(), calls=%async_computation.3 | async-start | bytes 5406720 | tf_op jit(solution)/shard_map/all_gather | solution.py:164
  11.2 159.1 %all-gather.10.cloned.1.call-start = ((), (), s32[]{:S(2)}) async-start(), calls=%async_computation.4 | async-start | bytes 5136384 | tf_op jit(solution)/shard_map/all_gather | solution.py:217
  12.7 1.5 copy-start.1
  14.2 3.2 %copy-start.4 = (bf16[1,16,2432]{2,1,0:T(8,128)(2,1)S(1)}, bf16[1,16,2432]{2,1,0:T(8,128)(2,1)}, u32[]{:S(2)}) copy-start(bf16[1,16,2432]{2,1,0:T(8,128)(2,1)} %param.15) | copy-start | bytes 233476
  14.3 3.5 %copy-start.16 = (s32[1,16]{1,0:T(1,128)S(1)}, s32[1,16]{1,0:T(1,128)}, u32[]{:S(2)}) copy-start(s32[1,16]{1,0:T(1,128)} %param.16) | copy-start | bytes 196
  24.8 1.5 copy-start.15
  90.6 3.5 %copy-start.3 = (bf16[32,76,144]{1,2,0:T(8,128)(2,1)S(1)}, bf16[32,76,144]{1,2,0:T(8,128)(2,1)}, u32[]{:S(2)}) copy-start(bf16[32,76,144]{1,2,0:T(8,128)(2,1)} %copy.79) | copy-start | bytes 2101252
  97.5 1.9 copy-start.11
  97.5 1.9 copy-start.12
  98.0 2.3 copy-start.13
  99.4 148.4 %all-gather.12.cloned.1.call-start = ((), (), s32[]{:S(2)}) async-start(), calls=%async_computation.5 | async-start | bytes 8110080 | tf_op jit(solution)/shard_map/all_gather | solution.py:169
  171.9 10.7 %copy-start.2 = (bf16[2432,192]{1,0:T(8,128)(2,1)S(1)}, bf16[2432,192]{1,0:T(8,128)(2,1)}, u32[]{:S(2)}) copy-start(bf16[2432,192]{1,0:T(8,128)(2,1)} %reshape.353) | copy-start | bytes 2801668
  182.6 8.4 %copy-start.10 = (f32[4,2432]{1,0:T(4,128)S(1)}, f32[4,2432]{1,0:T(4,128)}, u32[]{:S(2)}) copy-start(f32[4,2432]{1,0:T(4,128)} %get-tuple-element.19) | copy-start | bytes 116740
  184.1 7.1 %copy-start.9 = (f32[4,2432]{1,0:T(4,128)S(1)}, f32[4,2432]{1,0:T(4,128)}, u32[]{:S(2)}) copy-start(f32[4,2432]{1,0:T(4,128)} %get-tuple-element.15) | copy-start | bytes 116740
  184.1 7.2 %copy-start.8 = (f32[4,2432]{1,0:T(4,128)S(1)}, f32[4,2432]{1,0:T(4,128)}, u32[]{:S(2)}) copy-start(f32[4,2432]{1,0:T(4,128)} %get-tuple-element.12) | copy-start | bytes 116740
  184.1 20.0 %all-to-all-start = ((bf16[8,16,2432]{2,1,0:T(8,128)(2,1)}), bf16[8,16,2432]{2,1,0:T(8,128)(2,1)S(1)}, u32[]{:S(2)}, u32[]{:S(2)}) async-start(bf16[8,16,2432]{2,1,0:T(8,128)(2,1)} %bitcast.29), calls=%async_computation | async-start | bytes 1245184 | tf_op jit(solution)/shard_map/all_to_all | solution.py:41
  254.4 6.9 %copy-start.7 = (f32[4,2432]{1,0:T(4,128)S(1)}, f32[4,2432]{1,0:T(4,128)}, u32[]{:S(2)}) copy-start(f32[4,2432]{1,0:T(4,128)} %get-tuple-element.16) | copy-start | bytes 116740
  254.4 7.0 %copy-start.6 = (f32[4,2432]{1,0:T(4,128)S(1)}, f32[4,2432]{1,0:T(4,128)}, u32[]{:S(2)}) copy-start(f32[4,2432]{1,0:T(4,128)} %get-tuple-element.13) | copy-start | bytes 116740
  254.4 20.3 %all-to-all-start.2 = ((bf16[8,16,2560]{2,1,0:T(8,128)(2,1)}), bf16[8,16,2560]{2,1,0:T(8,128)(2,1)S(1)}, u32[]{:S(2)}, u32[]{:S(2)}) async-start(bf16[8,16,2560]{2,1,0:T(8,128)(2,1)} %bitcast.119), calls=%async_computation.2 | async-start | bytes 1310720 | tf_op jit(solution)/shard_map/all_to_all | solution.py:41
  274.9 3.4 %copy-start.17 = (s32[4]{0:T(128)S(1)}, s32[4]{0:T(128)}, u32[]{:S(2)}) copy-start(s32[4]{0:T(128)} %param.17) | copy-start | bytes 52
  274.9 6.4 %copy-start.14 = (f32[4,2,64]{2,1,0:T(2,128)S(1)}, f32[4,2,64]{2,1,0:T(2,128)}, u32[]{:S(2)}) copy-start(f32[4,2,64]{2,1,0:T(2,128)} %param.13) | copy-start | bytes 6148
  275.9 5.5 %collective-permute-start = (f32[4,2,64]{2,1,0:T(2,128)S(1)}, f32[4,2,64]{2,1,0:T(2,128)S(1)}, u32[]{:S(2)}, u32[]{:S(2)}) collective-permute-start(f32[4,2,64]{2,1,0:T(2,128)S(1)} %constant_dynamic-slice_fusion), channel_id=1, source_target_pairs={{0,256},{256,0},{1,257},{257,1},{2,258},{258,2},{3,259},{259,3},{4... | collective-permute-start | bytes 6152 | tf_op jit(solution)/shard_map/ppermute | solution.py:20
Sparse Core Ops, SparseCore 0:
  11.3 79.1 all-gather.7
  99.5 70.7 all-gather.9
  172.4 75.3 all-gather.11
